TPU v7x, 256 devices: a whole 4x4x8 slice. The times are simulated.
256 devices in a mesh: member: 4 (over x), fsdp: 64 (over z, y, core).
Axes of the slice: x: 4, y: 4, z: 8, core: 2. Of those that a mesh axis runs over, the one named last changes fastest.
Arguments:
- query_rows: bfloat16 [65536, 2560], P(('member', 'fsdp')), parts along dimension 0, may hold values from -110 to 110
- key_rows: bfloat16 [65536, 2560], P(('member', 'fsdp')), parts along dimension 0, may hold values from -9 to 9
- value_rows: bfloat16 [65536, 2560], P(('member', 'fsdp')), parts along dimension 0, may hold values from -24 to 24
- weight_out: bfloat16 [10240, 2560], P(('member', 'fsdp')), parts along dimension 0, may hold values from -0.125 to 0.125
- cotangent: bfloat16 [65536, 2560], P(('member', 'fsdp')), parts along dimension 0, may hold values from -24 to 24
- pattern: int32 [64, 16, 6], P('member'), parts along dimension 0, may hold values from 0 to 15, as said below
Outputs:
- sublayer_out: bfloat16 [65536, 2560], P(('member', 'fsdp')), parts along dimension 0
- grad_queries: bfloat16 [65536, 2560], P(('member', 'fsdp')), parts along dimension 0
- grad_keys: bfloat16 [65536, 2560], P(('member', 'fsdp')), parts along dimension 0
- grad_values: bfloat16 [65536, 2560], P(('member', 'fsdp')), parts along dimension 0
There are 4 independent parts, one for each index of `member`. A program takes and returns all parts, laid end to end along the dimension named above; each array names one. Nothing has to cross between parts.
Inputs may be any that keep to these rules, and one draw needn't show every extreme that they name: `pattern`: for each sequence and query block b the 6 entries are distinct key blocks of the same sequence; they include b, b - 1 and b + 1 where these exist and block 0, and the others are random.
All inputs are finite; a program needn't handle non-finite values.
Results may differ from a plain program's by a relative error of at most 0.035.
Values may be sent and summed in bfloat16 or wider, within the bound.
No kernel may reach another device: no remote copies, remote signals or barrier semaphores. Data moves between devices by JAX's collectives and lax.ppermute only.
A program may use at most 192 MiB of HBM per device.

v0:
```python
import math

import jax
import jax.numpy as jnp
from jax import lax
from jax.sharding import PartitionSpec as P

HEADS = 20
HSIZE = 128
BLK = 64
QBLK = 16
NSEL = 6
LEN = 1024


def partner(block, axis, apart):
    count = lax.axis_size(axis)
    route = []
    for low in range(count):
        high = low | 1 << apart
        if high != low and high < count:
            route += [(low, high), (high, low)]
    return lax.ppermute(block, axis, route)


def stitch(current, incoming, low_side):
    earlier = jnp.where(low_side, current, incoming)
    later_part = jnp.where(low_side, incoming, current)
    return jnp.stack([earlier, later_part])


def per_device(query_rows, key_rows, value_rows, weight_out, cotangent, pattern):
    tok_rows = query_rows.shape[0]
    feat_width = query_rows.shape[1]
    seq_shards = LEN // tok_rows
    levels = seq_shards.bit_length() - 1
    blocks_here = tok_rows // BLK
    scaling = 1.0 / math.sqrt(HSIZE)
    device_at = lax.axis_index("fsdp")
    sequence = device_at // seq_shards
    position = device_at % seq_shards
    full_weight = lax.all_gather(weight_out, "fsdp", axis=0, tiled=True)
    seq_plan = lax.dynamic_index_in_dim(pattern, sequence, 0, keepdims=False)
    own_plan = lax.dynamic_slice_in_dim(seq_plan, position * blocks_here, blocks_here, 0)
    bit_order = list(range(levels))
    held_keys = key_rows
    held_values = value_rows
    for bit_no in bit_order:
        other_keys, other_values = partner((held_keys, held_values), "fsdp", bit_no)
        low_side = position // (1 << bit_no) % 2 == 0
        held_keys = stitch(held_keys, other_keys, low_side)
        held_values = stitch(held_values, other_values, low_side)
    arrange = sorted(range(levels), key=lambda axis_pos: -bit_order[levels - 1 - axis_pos])
    seq_keys = jnp.transpose(held_keys, arrange + [levels, levels + 1]).reshape(
        QBLK, BLK, feat_width
    )
    seq_values = jnp.transpose(held_values, arrange + [levels, levels + 1]).reshape(
        QBLK, BLK, feat_width
    )
    query_blk = query_rows.reshape(blocks_here, BLK, HEADS, HSIZE)
    key_sel = jnp.take(seq_keys, own_plan, axis=0).reshape(blocks_here, NSEL * BLK, HEADS, HSIZE)
    value_sel = jnp.take(seq_values, own_plan, axis=0).reshape(
        blocks_here, NSEL * BLK, HEADS, HSIZE
    )
    scores = (
        jnp.einsum("bqhe,bkhe->bhqk", query_blk, key_sel, preferred_element_type=jnp.float32)
        * scaling
    )
    row_peak = jnp.max(scores, axis=-1, keepdims=True)
    log_total = row_peak + jnp.log(jnp.sum(jnp.exp(scores - row_peak), axis=-1, keepdims=True))
    probs = jnp.exp(scores - log_total)
    probs_low = probs.astype(jnp.bfloat16)
    context = jnp.einsum(
        "bhqk,bkhe->bqhe", probs_low, value_sel, preferred_element_type=jnp.float32
    ).astype(jnp.bfloat16)
    flat_context = context.reshape(tok_rows, feat_width)
    out_full = jnp.dot(flat_context, full_weight, preferred_element_type=jnp.float32)
    grad_full = lax.dot_general(
        cotangent, full_weight, (((1,), (1,)), ((), ())), preferred_element_type=jnp.float32
    )
    sublayer_out = out_full.astype(jnp.bfloat16)
    grad_context = grad_full.astype(jnp.bfloat16)
    grad_blk = grad_context.reshape(blocks_here, BLK, HEADS, HSIZE)
    grad_prob = jnp.einsum(
        "bqhe,bkhe->bhqk", grad_blk, value_sel, preferred_element_type=jnp.float32
    )
    row_delta = jnp.einsum("bqhe,bqhe->bhq", grad_blk, context, preferred_element_type=jnp.float32)
    grad_score = (probs * (grad_prob - row_delta[..., None])).astype(jnp.bfloat16)
    grad_queries = (
        jnp.einsum("bhqk,bkhe->bqhe", grad_score, key_sel, preferred_element_type=jnp.float32)
        * scaling
    )
    grad_queries = grad_queries.astype(jnp.bfloat16).reshape(tok_rows, feat_width)
    key_contrib = (
        jnp.einsum("bhqk,bqhe->bkhe", grad_score, query_blk, preferred_element_type=jnp.float32)
        * scaling
    )
    value_contrib = jnp.einsum(
        "bhqk,bqhe->bkhe", probs_low, grad_blk, preferred_element_type=jnp.float32
    )
    onehot = (own_plan[:, :, None] == jnp.arange(QBLK, dtype=jnp.int32)[None, None, :]).astype(
        jnp.float32
    )

    def by_owner(contrib):
        grouped = contrib.reshape(blocks_here, NSEL, BLK * feat_width)
        spread = jnp.einsum("psk,psr->kr", onehot, grouped, precision=lax.Precision.HIGHEST)
        return spread.astype(jnp.bfloat16).reshape(seq_shards, tok_rows, feat_width)

    held_dkeys = by_owner(key_contrib)
    held_dvalues = by_owner(value_contrib)
    for bit_no in range(levels):
        bit_span = 1 << bit_no
        own_bit = position // bit_span % 2
        shaped_keys = held_dkeys.reshape(
            seq_shards // (2 * bit_span), 2, bit_span, tok_rows, feat_width
        )
        shaped_values = held_dvalues.reshape(
            seq_shards // (2 * bit_span), 2, bit_span, tok_rows, feat_width
        )
        send_keys = lax.dynamic_index_in_dim(shaped_keys, 1 - own_bit, 1, keepdims=False)
        send_values = lax.dynamic_index_in_dim(shaped_values, 1 - own_bit, 1, keepdims=False)
        arrived_keys, arrived_values = partner((send_keys, send_values), "fsdp", bit_no)
        slot_mask = (jnp.arange(2) == 1 - own_bit)[None, :, None, None, None]
        held_dkeys = jnp.where(slot_mask, arrived_keys[:, None], shaped_keys).reshape(
            seq_shards, tok_rows, feat_width
        )
        held_dvalues = jnp.where(slot_mask, arrived_values[:, None], shaped_values).reshape(
            seq_shards, tok_rows, feat_width
        )
    grad_keys = jnp.sum(held_dkeys.astype(jnp.float32), axis=0).astype(jnp.bfloat16)
    grad_values = jnp.sum(held_dvalues.astype(jnp.float32), axis=0).astype(jnp.bfloat16)
    return (sublayer_out, grad_queries, grad_keys, grad_values)


def solution(mesh):
    placed = (
        P(("member", "fsdp"), None),
        P(("member", "fsdp"), None),
        P(("member", "fsdp"), None),
        P(("member", "fsdp"), None),
        P(("member", "fsdp"), None),
        P("member", None, None),
    )
    return jax.shard_map(
        per_device,
        mesh=mesh,
        in_specs=placed,
        out_specs=(
            P(("member", "fsdp"), None),
            P(("member", "fsdp"), None),
            P(("member", "fsdp"), None),
            P(("member", "fsdp"), None),
        ),
        check_vma=False,
    )
```

profile of v0, /device:TPU:1, one launch (start us, length us, event | category | flops | bytes accessed | tf_op | source)
XLA Modules:
  0.0 544.8 jit_solution(4429675532837432246)
XLA Ops:
  7.2 0.0 copy-start
  7.2 0.0 all-gather.2.cloned.1.call-start
  7.2 0.7 all-gather.2.cloned.1.call-update
  7.9 3.3 collective-permute-start.2
  11.2 0.1 collective-permute-start
  11.3 2.8 collective-permute-done.2
  14.1 2.0 collective-permute-done
  16.1 2.4 select_bitcast_fusion.5
  18.6 0.0 copy-start.7
  18.6 1.9 pad_maximum_fusion.2
  20.5 2.0 pad_maximum_fusion.3
  22.5 1.8 collective-permute-start.1
  24.3 0.8 constant_dynamic-slice_fusion.2
  25.1 0.1 copy.15
  25.2 0.1 reshape.168
  25.3 2.6 reshape.142
  27.9 69.2 %collective-permute-done.3 = bf16[2,256,2560]{2,1,0:T(8,128)(2,1)} collective-permute-done((bf16[2,256,2560]{2,1,0:T(8,128)(2,1)}, bf16[2,256,2560]{2,1,0:T(8,128)(2,1)}, u32[]{:S(2)}, u32[]{:S(2)}) %collective-permute-start.3) | collective-permute-done | bytes 2621472 | tf_op jit(solution)/shard_map/ppermute | solution.py:23
  97.1 3.0 select_bitcast_fusion.1
  100.2 2.8 pad_maximum_fusion
  103.0 7.7 %gather_fusion.1 = bf16[24,64,2560]{2,1,0:T(8,128)(2,1)} fusion(bf16[16,64,2560]{2,1,0:T(8,128)(2,1)} %bitcast.96, s32[1024]{0:T(1024)S(1)} %pad_clamp_fusion), kind=kCustom, calls=%fused_computation.1.clone | custom fusion | bytes 15728736 | tf_op jit(solution)/shard_map/jit(_take)/gather | solution.py:61
  110.7 54.0 %collective-permute-done.1 = bf16[2,256,2560]{2,1,0:T(8,128)(2,1)} collective-permute-done((bf16[2,256,2560]{2,1,0:T(8,128)(2,1)}, bf16[2,256,2560]{2,1,0:T(8,128)(2,1)}, u32[]{:S(2)}, u32[]{:S(2)}) %collective-permute-start.1) | collective-permute-done | bytes 2621472 | tf_op jit(solution)/shard_map/ppermute | solution.py:23
  164.7 2.8 select_bitcast_fusion.3
  167.5 2.8 pad_maximum_fusion.1
  170.4 7.7 %gather_fusion = bf16[24,64,2560]{2,1,0:T(8,128)(2,1)} fusion(bf16[16,64,2560]{2,1,0:T(8,128)(2,1)} %bitcast.95, s32[1024]{0:T(1024)S(1)} %pad_clamp_fusion), kind=kCustom, calls=%fused_computation.clone | custom fusion | bytes 15728736 | tf_op jit(solution)/shard_map/jit(_take)/gather | solution.py:62
  178.0 11.2 %broadcast_select_fusion = (bf16[4,6,64,2560]{3,2,1,0:T(8,128)(2,1)}, bf16[4,6,64,2560]{3,2,1,0:T(8,128)(2,1)}) fusion(bf16[4,6,64,2560]{3,2,1,0:T(8,128)(2,1)} %bitcast.97, pred[4,6]{1,0:T(4,128)(4,1)S(1)} %compare_and_fusion, bf16[4,6,64,2560]{3,2,1,0:T(8,128)(2,1)} %bitcast.98), kind=kLoop, calls=%fused_computation.15 | loop fusion | flops 7864320 | bytes 31457304 | tf_op jit(solution)/shard_map/jit(_take)/select_n | solution.py:61
  189.2 14.0 %reshape.139 = bf16[4,384,20,128]{3,2,1,0:T(8,128)(2,1)} reshape(bf16[4,6,64,2560]{3,2,1,0:T(8,128)(2,1)} %get-tuple-element.18) | data formatting | bytes 15728640 | tf_op jit(solution)/shard_map/reshape | solution.py:62
  203.2 14.0 %reshape.141 = bf16[4,384,20,128]{3,2,1,0:T(8,128)(2,1)} reshape(bf16[4,6,64,2560]{3,2,1,0:T(8,128)(2,1)} %get-tuple-element.17) | data formatting | bytes 15728640 | tf_op jit(solution)/shard_map/reshape | solution.py:61
  217.2 10.4 %bitcast_reduce_fusion = (f32[4,20,64]{2,1,0:T(8,128)S(1)}, f32[4,20,384,64]{2,3,1,0:T(8,128)}) fusion(bf16[4,64,20,128]{3,2,1,0:T(8,128)(2,1)S(1)} %reshape.142, bf16[4,384,20,128]{3,2,1,0:T(8,128)(2,1)} %reshape.141), kind=kOutput, calls=%fused_computation.10 | convolution fusion | flops 507243520 | bytes 17059840 | tf_op jit(solution)/shard_map/bqhe,bkhe->bhqk/dot_general | solution.py:66
  227.6 4.3 fusion.3
  232.0 0.0 all-gather.2.cloned.1.call-done
  232.0 9.4 %convolution_convert_fusion = bf16[256,2560]{1,0:T(8,128)(2,1)} fusion(bf16[256,2560]{1,0:T(8,128)(2,1)S(1)} %copy-done, bf16[2560,2560]{1,0:T(8,128)(2,1)} %all-gather.2.cloned.1.call-done), kind=kOutput, calls=%fused_computation.30 | convolution fusion | flops 3356098560 | bytes 15728640 | tf_op jit(solution)/shard_map/dot_general | solution.py:78
  241.4 2.7 reshape.144
  244.1 0.2 bitcast_convert_fusion
  244.3 8.9 %convolution_bitcast_fusion.2 = f32[4,384,20,128]{1,3,2,0:T(8,128)} fusion(bf16[4,64,20,128]{3,2,1,0:T(8,128)(2,1)S(1)} %reshape.144, f32[4,20,384,64]{2,3,1,0:T(8,128)} %get-tuple-element.20, f32[4,20,64]{2,1,0:T(8,128)S(1)} %log_add_fusion), kind=kOutput, calls=%fused_computation.7 | convolution fusion | flops 509214720 | bytes 24924160 | tf_op jit(solution)/shard_map/bhqk,bqhe->bkhe/dot_general | solution.py:98
  253.2 9.3 %multiply_reduce_fusion = (f32[4,20,64]{2,1,0:T(8,128)S(1)}, bf16[4,20,128,64]{2,3,1,0:T(8,128)(2,1)S(1)}) fusion(f32[4,20,64,128]{3,1,2,0:T(8,128)S(1)} %bitcast_convert_fusion, bf16[4,384,20,128]{3,2,1,0:T(8,128)(2,1)} %reshape.139, f32[4,20,384,64]{2,3,1,0:T(8,128)} %get-tuple-element.20, f32[4,20,64]{2,1,0:T(8,128)S(1)} %log_add_fusion), kind=kOutput, calls=%fused_computation.38 | convolution fusion | flops 511831040 | bytes 19701760 | tf_op jit(solution)/shard_map/bhqk,bkhe->bqhe/dot_general | solution.py:73
  262.5 9.4 %multiply_convert_fusion = bf16[4,20,64,384]{3,2,1,0:T(8,128)(2,1)} fusion(f32[4,20,384,64]{2,3,1,0:T(8,128)} %get-tuple-element.20, f32[4,20,64]{2,1,0:T(8,128)S(1)} %get-tuple-element.21, f32[4,20,64]{2,1,0:T(8,128)S(1)} %log_add_fusion, bf16[4,384,20,128]{3,2,1,0:T(8,128)(2,1)} %reshape.139, bf16[4,64,20,128]{3,2,1,0:T(8,128)(2,1)S(1)} %reshape.144), kind=kOutput, calls=%fused_computation.14 | convolution fusion | flops 513146880 | bytes 21012480 | tf_op jit(solution)/shard_map/bqhe,bkhe->bhqk/dot_general | solution.py:84
  272.0 17.5 %copy.27 = f32[4,384,20,128]{3,2,1,0:T(8,128)} copy(f32[4,384,20,128]{1,3,2,0:T(8,128)} %convolution_bitcast_fusion.2) | data formatting | bytes 31457280 | tf_op jit(solution)/shard_map/bhqk,bqhe->bkhe/transpose | solution.py:98
  289.5 23.2 %reshape.147 = f32[4,6,163840]{2,1,0:T(8,128)} reshape(f32[4,384,20,128]{3,2,1,0:T(8,128)} %copy.27) | data formatting | bytes 31457280 | tf_op jit(solution)/shard_map/reshape | solution.py:106
  312.7 15.0 %fusion.1 = bf16[16,163840]{1,0:T(8,128)(2,1)} fusion(f32[4,6,163840]{2,1,0:T(8,128)} %reshape.147, s32[4,6]{1,0:T(4,128)S(1)} %bitcast.107), kind=kOutput, calls=%fused_computation.5 | convolution fusion | flops 757596544 | bytes 20971616 | tf_op jit(solution)/shard_map/psk,psr->kr/dot_general | solution.py:107
  327.6 5.8 %reshape_reshape.14 = bf16[2,2,1,256,2560]{4,3,1,0,2:T(8,128)(2,1)} reshape(bf16[16,163840]{1,0:T(8,128)(2,1)} %fusion.1) | data formatting | bytes 10485760 | tf_op jit(solution)/shard_map/reshape;reshape | solution.py:118
  333.4 4.4 multiply_bitcast_fusion
  337.8 13.1 %copy.25 = f32[4,384,20,128]{3,2,1,0:T(8,128)} copy(f32[4,384,20,128]{3,1,2,0:T(8,128)S(1)} %multiply_bitcast_fusion) | data formatting | bytes 31457280 | tf_op jit(solution)/shard_map/mul | solution.py:95
  350.9 23.2 %reshape.146 = f32[4,6,163840]{2,1,0:T(8,128)} reshape(f32[4,384,20,128]{3,2,1,0:T(8,128)} %copy.25) | data formatting | bytes 31457280 | tf_op jit(solution)/shard_map/reshape | solution.py:106
  374.1 15.3 %fusion = bf16[16,163840]{1,0:T(8,128)(2,1)} fusion(f32[4,6,163840]{2,1,0:T(8,128)} %reshape.146, s32[4,6]{1,0:T(4,128)S(1)} %bitcast.108), kind=kOutput, calls=%fused_computation.4 | convolution fusion | flops 757596544 | bytes 20971616 | tf_op jit(solution)/shard_map/psk,psr->kr/dot_general | solution.py:107
  389.4 5.7 %reshape_reshape.12 = bf16[2,2,1,256,2560]{4,3,1,0,2:T(8,128)(2,1)} reshape(bf16[16,163840]{1,0:T(8,128)(2,1)} %fusion) | data formatting | bytes 10485760 | tf_op jit(solution)/shard_map/reshape;reshape | solution.py:115
  395.1 3.4 dynamic-slice_bitcast_fusion.1
  398.4 1.2 collective-permute-start.4
  399.7 3.4 dynamic-slice_bitcast_fusion
  403.1 1.5 collective-permute-done.4
  404.6 1.5 constant_dynamic-slice_fusion.1
  406.0 2.3 collective-permute-done.6
  408.3 1.4 constant_dynamic-slice_fusion
  409.7 4.7 fusion.15
  414.4 1.5 collective-permute-start.5
  415.8 5.8 %reshape_reshape.15 = bf16[2,2,256,2560]{3,2,1,0:T(8,128)(2,1)} reshape(bf16[16,163840]{1,0:T(8,128)(2,1)} %fusion.1) | data formatting | bytes 10485760 | tf_op jit(solution)/shard_map/reshape;reshape | solution.py:118
  421.7 5.6 %reshape_reshape.13 = bf16[2,2,256,2560]{3,2,1,0:T(8,128)(2,1)} reshape(bf16[16,163840]{1,0:T(8,128)(2,1)} %fusion) | data formatting | bytes 10485760 | tf_op jit(solution)/shard_map/reshape;reshape | solution.py:115
  427.2 0.9 copy.19
  428.1 6.5 %fusion.23 = bf16[4,64,20,128]{3,1,2,0:T(8,128)(2,1)S(1)} fusion(bf16[4,20,64,384]{3,2,1,0:T(8,128)(2,1)} %multiply_convert_fusion, bf16[4,384,20,128]{3,2,1,0:T(8,128)(2,1)} %reshape.141), kind=kOutput, calls=%fused_computation.48 | convolution fusion | flops 504627200 | bytes 13107200 | tf_op jit(solution)/shard_map/bhqk,bkhe->bqhe/dot_general | solution.py:90
  434.6 0.9 copy.23
  435.5 1.2 copy.72
  436.8 9.5 %convolution_convert_fusion.1 = bf16[256,2560]{1,0:T(8,128)(2,1)} fusion(bf16[2560,2560]{1,0:T(8,128)(2,1)} %all-gather.2.cloned.1.call-done, bf16[32,8,20,128]{3,2,1,0:T(8,128)(2,1)S(1)} %bitcast.105), kind=kOutput, calls=%fused_computation.31 | convolution fusion | flops 3356098560 | bytes 15728640 | tf_op jit(solution)/shard_map/dot_general | solution.py:77
  446.2 26.5 %collective-permute-done.7 = bf16[1,2,256,2560]{3,2,1,0:T(8,128)(2,1)} collective-permute-done((bf16[1,2,256,2560]{3,2,1,0:T(8,128)(2,1)}, bf16[1,2,256,2560]{3,2,1,0:T(8,128)(2,1)}, u32[]{:S(2)}, u32[]{:S(2)}) %collective-permute-start.7) | collective-permute-done | bytes 2621472 | tf_op jit(solution)/shard_map/ppermute | solution.py:23
  472.7 56.2 %collective-permute-done.5 = bf16[1,2,256,2560]{3,2,1,0:T(8,128)(2,1)} collective-permute-done((bf16[1,2,256,2560]{3,2,1,0:T(8,128)(2,1)}, bf16[1,2,256,2560]{3,2,1,0:T(8,128)(2,1)}, u32[]{:S(2)}, u32[]{:S(2)}) %collective-permute-start.5) | collective-permute-done | bytes 2621472 | tf_op jit(solution)/shard_map/ppermute | solution.py:23
  529.0 8.8 %select_reduce_fusion = (bf16[256,2560]{1,0:T(8,128)(2,1)}, bf16[256,2560]{1,0:T(8,128)(2,1)}) fusion(bf16[2,2,256,2560]{3,2,1,0:T(8,128)(2,1)S(1)} %bitcast.100, pred[2]{0:T(512)(128)(4,1)S(1)} %iota_compare_fusion.3, pred[2]{0:T(512)(128)(4,1)S(1)} %iota_compare_fusion.4, bf16[2,256,2560]{2,1,0:T(8,128)(2,1)} %bitcast.28, ...), kind=kLoop, calls=%fused_computation.28 | loop fusion | flops 14417920 | bytes 23592964 | tf_op jit(solution)/shard_map/reduce_sum | solution.py:132
  (35 shorter events, 0.1 us)
Async XLA Ops:
  7.2 224.8 %copy-start = (bf16[256,2560]{1,0:T(8,128)(2,1)S(1)}, bf16[256,2560]{1,0:T(8,128)(2,1)}, u32[]{:S(2)}) copy-start(bf16[256,2560]{1,0:T(8,128)(2,1)} %param.12) | copy-start | bytes 3932164
  7.2 224.8 %all-gather.2.cloned.1.call-start = ((), (), s32[]{:S(2)}) async-start(), calls=%async_computation | async-start | bytes 13312000 | tf_op jit(solution)/shard_map/all_gather | solution.py:42
  7.9 6.2 %collective-permute-start.2 = (bf16[256,2560]{1,0:T(8,128)(2,1)}, bf16[256,2560]{1,0:T(8,128)(2,1)S(1)}, u32[]{:S(2)}, u32[]{:S(2)}) collective-permute-start(bf16[256,2560]{1,0:T(8,128)(2,1)} %param.9), channel_id=1, source_target_pairs={{0,1},{1,0},{2,3},{3,2},{4,5},{5,4},{6,7},{7,6},{8,9},{9,8},{10,11... | collective-permute-start | bytes 3932168 | tf_op jit(solution)/shard_map/ppermute | solution.py:23
  11.2 4.9 collective-permute-start
  18.5 4.0 copy-start.5
  18.5 4.0 copy-start.6
  18.6 4.0 copy-start.7
  18.6 4.0 copy-start.8
  20.5 76.6 %collective-permute-start.3 = (bf16[2,256,2560]{2,1,0:T(8,128)(2,1)}, bf16[2,256,2560]{2,1,0:T(8,128)(2,1)}, u32[]{:S(2)}, u32[]{:S(2)}) collective-permute-start(bf16[2,256,2560]{2,1,0:T(8,128)(2,1)} %pad_maximum_fusion.2), channel_id=1, source_target_pairs={{0,2},{2,0},{1,3},{3,1},{4,6},{6,4},{5,7},{7,5},{8,10},{10,8},{9,1... | collective-permute-start | bytes 7864328 | tf_op jit(solution)/shard_map/ppermute | solution.py:23
  22.5 142.2 %collective-permute-start.1 = (bf16[2,256,2560]{2,1,0:T(8,128)(2,1)}, bf16[2,256,2560]{2,1,0:T(8,128)(2,1)}, u32[]{:S(2)}, u32[]{:S(2)}) collective-permute-start(bf16[2,256,2560]{2,1,0:T(8,128)(2,1)} %pad_maximum_fusion.3), channel_id=1, source_target_pairs={{0,2},{2,0},{1,3},{3,1},{4,6},{6,4},{5,7},{7,5},{8,10},{10,8},{9,1... | collective-permute-start | bytes 7864328 | tf_op jit(solution)/shard_map/ppermute | solution.py:23
  27.9 189.3 %copy-start.3 = (bf16[4,64,20,128]{3,2,1,0:T(8,128)(2,1)}, bf16[4,64,20,128]{3,2,1,0:T(8,128)(2,1)S(1)}, u32[]{:S(2)}) copy-start(bf16[4,64,20,128]{3,2,1,0:T(8,128)(2,1)S(1)} %reshape.142) | copy-start | bytes 3932164
  327.6 5.8 %copy-start.4 = (bf16[4,64,20,128]{3,2,1,0:T(8,128)(2,1)S(1)}, bf16[4,64,20,128]{3,2,1,0:T(8,128)(2,1)}, u32[]{:S(2)}) copy-start(bf16[4,64,20,128]{3,2,1,0:T(8,128)(2,1)} %copy-done.3) | copy-start | bytes 3932164
  398.4 6.1 %collective-permute-start.4 = (bf16[2,1,256,2560]{3,2,0,1:T(8,128)(2,1)}, bf16[2,1,256,2560]{3,2,0,1:T(8,128)(2,1)}, u32[]{:S(2)}, u32[]{:S(2)}) collective-permute-start(bf16[2,1,256,2560]{3,2,0,1:T(8,128)(2,1)} %dynamic-slice_bitcast_fusion.1), channel_id=1, source_target_pairs={{0,1},{1,0},{2,3},{3,2},{4,5},{5,4},{6,7},{7,6},{8,9},{9,8},{10,11... | collective-permute-start | bytes 7864328 | tf_op jit(solution)/shard_map/ppermute | solution.py:23
  403.1 5.3 collective-permute-start.6
  403.1 6.7 %copy-start.2 = (bf16[2,2,1,256,2560]{4,3,1,0,2:T(8,128)(2,1)S(1)}, bf16[2,2,1,256,2560]{4,3,1,0,2:T(8,128)(2,1)}, u32[]{:S(2)}) copy-start(bf16[2,2,1,256,2560]{4,3,1,0,2:T(8,128)(2,1)} %reshape_reshape.12) | copy-start | bytes 15728644
  414.4 58.4 %collective-permute-start.7 = (bf16[1,2,256,2560]{3,2,1,0:T(8,128)(2,1)}, bf16[1,2,256,2560]{3,2,1,0:T(8,128)(2,1)}, u32[]{:S(2)}, u32[]{:S(2)}) collective-permute-start(bf16[1,2,256,2560]{3,2,1,0:T(8,128)(2,1)} %get-tuple-element.16), channel_id=1, source_target_pairs={{0,2},{2,0},{1,3},{3,1},{4,6},{6,4},{5,7},{7,5},{8,10},{10,8},{9,1... | collective-permute-start | bytes 7864328 | tf_op jit(solution)/shard_map/ppermute | solution.py:23
  414.4 114.5 %collective-permute-start.5 = (bf16[1,2,256,2560]{3,2,1,0:T(8,128)(2,1)}, bf16[1,2,256,2560]{3,2,1,0:T(8,128)(2,1)}, u32[]{:S(2)}, u32[]{:S(2)}) collective-permute-start(bf16[1,2,256,2560]{3,2,1,0:T(8,128)(2,1)} %get-tuple-element.15), channel_id=1, source_target_pairs={{0,2},{2,0},{1,3},{3,1},{4,6},{6,4},{5,7},{7,5},{8,10},{10,8},{9,1... | collective-permute-start | bytes 7864328 | tf_op jit(solution)/shard_map/ppermute | solution.py:23
  436.7 92.2 %slice-start = ((s8[5242880]{0:T(1024)(128)(4,1)}), s8[4194304]{0:T(1024)(128)(4,1)S(1)}, s32[]{:S(2)}) async-start(s8[5242880]{0:T(1024)(128)(4,1)} %bitcast.99), calls=%async_computation.1 | async-start | bytes 8388608
  436.7 92.2 %slice-start.2 = ((s8[5242880]{0:T(1024)(128)(4,1)}), s8[4194304]{0:T(1024)(128)(4,1)S(1)}, s32[]{:S(2)}) async-start(s8[5242880]{0:T(1024)(128)(4,1)} %bitcast.101), calls=%async_computation.3 | async-start | bytes 8388608
  436.7 92.2 %slice-start.1 = ((s8[5242880]{0:T(1024)(128)(4,1)}), s8[1048576]{0:T(1024)(128)(4,1)S(1)}, s32[]{:S(2)}) async-start(s8[5242880]{0:T(1024)(128)(4,1)} %bitcast.99), calls=%async_computation.2 | async-start | bytes 2097152
  436.7 92.2 %slice-start.3 = ((s8[5242880]{0:T(1024)(128)(4,1)}), s8[1048576]{0:T(1024)(128)(4,1)S(1)}, s32[]{:S(2)}) async-start(s8[5242880]{0:T(1024)(128)(4,1)} %bitcast.101), calls=%async_computation.4 | async-start | bytes 2097152
  529.0 8.8 %copy-start.1 = (bf16[256,2560]{1,0:T(8,128)(2,1)S(1)}, bf16[256,2560]{1,0:T(8,128)(2,1)}, u32[]{:S(2)}) copy-start(bf16[256,2560]{1,0:T(8,128)(2,1)} %param.12) | copy-start | bytes 3932164
Sparse Core Ops, SparseCore 0:
  10.7 119.9 all-gather.1
where the time goes:
time: 550 us; the launch traced here: 545 us
  waiting for transfers between devices  215 us (39%)
  local copies, waits for them, and re-layouts  162 us (29%)
  matrix products  98 us (18%)
  other arithmetic  47.2 us (9%)
  between operations  14.5 us (3%)
  starting transfers between devices  7.91 us (1%)
    ppermute x8, waiting for transfers between devices, partner(): return lax.ppermute(block, axis, route)  214 us
    reshape x2, local copies, waits for them, and re-layouts, by_owner(): grouped = contrib.reshape(blocks_here, NSEL, BLK * feat_width)  46.3 us
    dot_general x2, matrix products, by_owner(): jnp.einsum('psk,psr->kr', onehot, grouped, precision=lax.Precision.HIGHEST)  30.3 us
    another operation x7, other arithmetic, stitch(): return jnp.stack([earlier, later_part])  17.9 us
    transpose x1, local copies, waits for them, and re-layouts, per_device(): jnp.einsum('bhqk,bqhe->bkhe', probs_low, grad_blk, preferred_element_type...  17.5 us
    reshape x1, local copies, waits for them, and re-layouts, per_device(): jnp.take(seq_keys, own_plan, axis=0)  14 us
    reshape x1, local copies, waits for them, and re-layouts, per_device(): jnp.take(seq_values, own_plan, axis=0)  14 us
    mul x1, local copies, waits for them, and re-layouts, per_device(): jnp.einsum('bhqk,bqhe->bkhe', grad_score, query_blk, preferred_element_ty...  13.1 us
  transfers between devices with their start and end apart: 9, of which 8 were waited for; matrix products, arithmetic and copies ran while one was open for 23% of the time, Pallas kernels for 0%

commit v1 on v0

v1 whole, which is shorter than its diff:
```python
import math

import jax
import jax.numpy as jnp
from jax import lax
from jax.experimental import pallas as pl
from jax.experimental.pallas import tpu as pltpu
from jax.sharding import Mesh
from jax.sharding import PartitionSpec as P

HEADS = 20
HSIZE = 128
BLK = 64
QBLK = 16
NSEL = 6
LEN = 1024

SLOT_XOR = (0, 2, 1, 3)


def attn_kernel(q_ref, k0, k1, k2, k3, v0, v1, v2, v3, do_ref, mask_ref,
                ctx_ref, dq_ref, dk_ref, dv_ref):
    scaling = 1.0 / math.sqrt(HSIZE)
    q = q_ref[...]
    k = jnp.concatenate([k0[...], k1[...], k2[...], k3[...]], axis=0)
    v = jnp.concatenate([v0[...], v1[...], v2[...], v3[...]], axis=0)
    nt = (((1,), (1,)), ((), ()))
    tn = (((0,), (0,)), ((), ()))
    s = lax.dot_general(q, k, nt, preferred_element_type=jnp.float32) * scaling
    s = jnp.where(mask_ref[...] > 0, s, -jnp.inf)
    m = jnp.max(s, axis=1, keepdims=True)
    total = jnp.sum(jnp.exp(s - m), axis=1, keepdims=True)
    lse = m + jnp.log(total)
    p = jnp.exp(s - lse)
    p_low = p.astype(jnp.bfloat16)
    ctx = jnp.dot(p_low, v, preferred_element_type=jnp.float32).astype(jnp.bfloat16)
    ctx_ref[...] = ctx
    do = do_ref[...]
    dp = lax.dot_general(do, v, nt, preferred_element_type=jnp.float32)
    delta = jnp.sum(do.astype(jnp.float32) * ctx.astype(jnp.float32), axis=1, keepdims=True)
    ds = (p * (dp - delta)).astype(jnp.bfloat16)
    dq = jnp.dot(ds, k, preferred_element_type=jnp.float32) * scaling
    dq_ref[...] = dq.astype(jnp.bfloat16)
    dk = lax.dot_general(ds, q, tn, preferred_element_type=jnp.float32) * scaling
    dv = lax.dot_general(p_low, do, tn, preferred_element_type=jnp.float32)
    dk_ref[...] = dk.astype(jnp.bfloat16).reshape(dk_ref.shape)
    dv_ref[...] = dv.astype(jnp.bfloat16).reshape(dv_ref.shape)


def attention(q, ks, vs, do, mask):
    rows, width = q.shape
    keys = mask.shape[1]
    col = pl.BlockSpec((rows, HSIZE), lambda h: (0, h))
    slot_col = pl.BlockSpec((4, rows, HSIZE), lambda h: (0, 0, h))
    return pl.pallas_call(
        attn_kernel,
        grid=(width // HSIZE,),
        in_specs=[col] * 9 + [col, pl.BlockSpec((rows, keys), lambda h: (0, 0))],
        out_specs=[col, col, slot_col, slot_col],
        out_shape=[
            jax.ShapeDtypeStruct((rows, width), jnp.bfloat16),
            jax.ShapeDtypeStruct((rows, width), jnp.bfloat16),
            jax.ShapeDtypeStruct((4, rows, width), jnp.bfloat16),
            jax.ShapeDtypeStruct((4, rows, width), jnp.bfloat16),
        ],
    )(q, *ks, *vs, do, mask)


def swap(x, axis):
    count = lax.axis_size(axis)
    return lax.ppermute(x, axis, [(i, i ^ 1) for i in range(count)])


def per_device(query_rows, key_rows, value_rows, weight_out, cotangent, pattern):
    tok_rows = query_rows.shape[0]
    blocks_here = tok_rows // BLK
    chip = lax.axis_index("chip")
    core = lax.axis_index("core")
    seq_shards = LEN // tok_rows
    position = (chip % 2) * 2 + core
    sequence = chip // 2

    w_chip = lax.all_gather(weight_out, "chip", axis=0, tiled=False)
    w_full = lax.all_gather(w_chip, "core", axis=1, tiled=False)
    full_weight = w_full.reshape(-1, weight_out.shape[1])

    k_x = swap(key_rows, "chip")
    v_x = swap(value_rows, "chip")
    k_p = swap(key_rows, "core")
    v_p = swap(value_rows, "core")
    k_d = swap(k_x, "core")
    v_d = swap(v_x, "core")

    seq_plan = lax.dynamic_index_in_dim(pattern, sequence, 0, keepdims=False)
    own_plan = lax.dynamic_slice_in_dim(seq_plan, position * blocks_here, blocks_here, 0)
    rel = jnp.arange(seq_shards * blocks_here, dtype=jnp.int32)
    slot_xor = jnp.array(SLOT_XOR, dtype=jnp.int32)[rel // blocks_here]
    key_block = (position ^ slot_xor) * blocks_here + rel % blocks_here
    block_mask = jnp.any(own_plan[:, :, None] == key_block[None, None, :], axis=1)
    mask = jnp.broadcast_to(
        block_mask.astype(jnp.float32)[:, None, :, None],
        (blocks_here, BLK, seq_shards * blocks_here, BLK),
    ).reshape(tok_rows, seq_shards * tok_rows)

    grad_context = lax.dot_general(
        cotangent, full_weight, (((1,), (1,)), ((), ())), preferred_element_type=jnp.float32
    ).astype(jnp.bfloat16)

    ctx, grad_queries, dk, dv = attention(
        query_rows, (key_rows, k_x, k_p, k_d), (value_rows, v_x, v_p, v_d), grad_context, mask
    )
    sublayer_out = jnp.dot(ctx, full_weight, preferred_element_type=jnp.float32).astype(
        jnp.bfloat16
    )

    def reduce_parts(parts):
        back = swap(parts[2:4], "core")
        own = parts[0].astype(jnp.float32) + back[0].astype(jnp.float32)
        cross = (parts[1].astype(jnp.float32) + back[1].astype(jnp.float32)).astype(jnp.bfloat16)
        arrived = swap(cross, "chip")
        return (own + arrived.astype(jnp.float32)).astype(jnp.bfloat16)

    grad_keys = reduce_parts(dk)
    grad_values = reduce_parts(dv)
    return (sublayer_out, grad_queries, grad_keys, grad_values)


def solution(mesh):
    devices = mesh.devices.reshape(mesh.devices.shape[0], -1, 2)
    split = Mesh(devices, ("member", "chip", "core"))
    rows = P(("member", "chip", "core"), None)
    return jax.shard_map(
        per_device,
        mesh=split,
        in_specs=(rows, rows, rows, rows, rows, P("member", None, None)),
        out_specs=(rows, rows, rows, rows),
        check_vma=False,
    )
```

time: 550 us -> 280 us (0.51)
  local copies, waits for them, and re-layouts: 162 us -> 6.76 us
  matrix products: 98 us -> 18.7 us
  other arithmetic: 47.2 us -> 3.81 us
  Pallas kernels: 0 us -> 31.6 us
  waiting for transfers between devices: 215 us -> 195 us
    ppermute x8 -> x10, waiting for transfers between devices: 214 us -> 99.4 us  [swap(): return lax.ppermute(x, axis, [(i, i ^ 1) for i in range(count)])]
    all_gather x1 -> x2, waiting for transfers between devices: 0.02 us -> 95.3 us  [the longest x1 95.3 us: per_device(): w_chip = lax.all_gather(weight_out, 'chip', axis=0, tiled=False)]
    dot_general x9 -> x1, matrix products: 88.7 us -> 9.37 us  [per_device(): jnp.dot(ctx, full_weight, preferred_element_type=jnp.float32)]
    reshape x6 -> x1, local copies, waits for them, and re-layouts: 79.6 us -> 1.54 us  [per_device(): mask = jnp.broadcast_to(block_mask.astype(jnp.float32)[:, None, :, None],...]
    pallas_call x0 -> x1, Pallas kernels: none -> 31.6 us  [attention(): pl.pallas_call(attn_kernel, grid=(width // HSIZE,), in_specs=[col] * 9 +...]
    another operation x4 -> x0, local copies, waits for them, and re-layouts: 22.9 us -> none  [the longest x2 11.6 us: per_device(): held_dvalues.reshape(seq_shards // (2 * bit_span), 2, bit_span, tok_rows,...]
    another operation x7 -> x0, other arithmetic: 17.9 us -> none  [stitch(): return jnp.stack([earlier, later_part])]
    transpose x1 -> x0, local copies, waits for them, and re-layouts: 17.5 us -> none  [per_device(): jnp.einsum('bhqk,bqhe->bkhe', probs_low, grad_blk, preferred_element_type...]
  transfers between devices with their start and end apart: 9 -> 12, of which waited for: 8 -> 7; matrix products, arithmetic and copies ran while one was open for 23% -> 9% of each run, Pallas kernels for 0% -> 0%
where the time goes in v1:
time: 280 us
  waiting for transfers between devices  195 us (70%)
  Pallas kernels  31.6 us (11%)
  matrix products  18.7 us (7%)
  between operations  14.2 us (5%)
  starting transfers between devices  9.49 us (3%)
  local copies, waits for them, and re-layouts  6.76 us (2%)
  other arithmetic  3.81 us (1%)
    ppermute x10, waiting for transfers between devices, swap(): return lax.ppermute(x, axis, [(i, i ^ 1) for i in range(count)])  99.4 us
    all_gather x1, waiting for transfers between devices, per_device(): w_chip = lax.all_gather(weight_out, 'chip', axis=0, tiled=False)  95.3 us
    pallas_call x1, Pallas kernels, attention(): pl.pallas_call(attn_kernel, grid=(width // HSIZE,), in_specs=[col] * 9 +...  31.6 us
    ppermute x10, starting transfers between devices, swap(): return lax.ppermute(x, axis, [(i, i ^ 1) for i in range(count)])  9.41 us
    dot_general x1, matrix products, per_device(): jnp.dot(ctx, full_weight, preferred_element_type=jnp.float32)  9.37 us
    dot_general x1, matrix products, per_device(): lax.dot_general(cotangent, full_weight, (((1,), (1,)), ((), ())), preferr...  9.36 us
  transfers between devices with their start and end apart: 12, of which 7 were waited for; matrix products, arithmetic and copies ran while one was open for 9% of the time, Pallas kernels for 0%

profile of v1, /device:TPU:1, one launch (start us, length us, event | category | flops | bytes accessed | tf_op | source)
XLA Modules:
  0.0 279.9 jit_solution(13982829866422212185)
XLA Ops:
  7.2 0.0 copy-start
  7.2 0.0 all-gather.5.cloned.1.call-start
  7.2 0.7 all-gather.5.cloned.1.call-update
  7.9 0.0 all-gather.7.cloned.1.call-start
  8.0 95.3 %all-gather.5.cloned.1.call-done = bf16[1280,2560]{1,0:T(8,128)(2,1)} async-done(((bf16[40,2560]{1,0:T(8,128)(2,1)}), bf16[1280,2560]{1,0:T(8,128)(2,1)}) %all-gather.5.cloned.1.call-update) | async-done | bytes 6553616 | tf_op jit(solution)/shard_map/all_gather | solution.py:83
  103.3 0.0 copy-start.2
  103.3 0.0 all-gather.7.cloned.1.call-update
  103.3 0.1 collective-permute-start
  103.4 1.4 collective-permute-start.3
  104.8 1.7 collective-permute-start.1
  106.5 0.0 collective-permute-start.4
  106.6 0.8 constant_dynamic-slice_fusion
  107.4 0.1 copy.13
  107.5 0.1 copy.14
  107.6 0.0 copy-done.2
  107.6 0.7 gather_fusion
  108.2 24.6 %collective-permute-done.k1 = bf16[256,2560]{1,0:T(8,128)(2,1)} collective-permute-done((bf16[256,2560]{1,0:T(8,128)(2,1)}, bf16[256,2560]{1,0:T(8,128)(2,1)}, u32[]{:S(2)}, u32[]{:S(2)}) %collective-permute-start) | collective-permute-done | bytes 1310752 | tf_op jit(solution)/shard_map/ppermute | solution.py:71
  132.9 3.6 %collective-permute-start.2 = (bf16[256,2560]{1,0:T(8,128)(2,1)}, bf16[256,2560]{1,0:T(8,128)(2,1)}, u32[]{:S(2)}, u32[]{:S(2)}) collective-permute-start(bf16[256,2560]{1,0:T(8,128)(2,1)} %collective-permute-done.k1), channel_id=1, source_target_pairs={{0,1},{1,0},{2,3},{3,2},{4,5},{5,4},{6,7},{7,6},{8,9},{9,8},{10,11... | collective-permute-start | bytes 3932168 | tf_op jit(solution)/shard_map/ppermute | solution.py:71
  136.5 24.5 %collective-permute-done.3.v1 = bf16[256,2560]{1,0:T(8,128)(2,1)} collective-permute-done((bf16[256,2560]{1,0:T(8,128)(2,1)}, bf16[256,2560]{1,0:T(8,128)(2,1)}, u32[]{:S(2)}, u32[]{:S(2)}) %collective-permute-start.3) | collective-permute-done | bytes 1310752 | tf_op jit(solution)/shard_map/ppermute | solution.py:71
  161.0 2.0 collective-permute-start.5
  163.0 0.1 compare_reduce_fusion
  163.1 0.2 broadcast_in_dim.2
  163.3 1.5 reshape.92.mask_ref
  164.8 0.0 all-gather.7.cloned.1.call-done
  164.8 0.0 copy-done
  164.8 9.4 %convolution_convert_fusion.1.do_ref = bf16[256,2560]{1,0:T(8,128)(2,1)} fusion(bf16[256,2560]{1,0:T(8,128)(2,1)S(1)} %copy-done, bf16[2560,2560]{1,0:T(8,128)(2,1)} %bitcast.25), kind=kOutput, calls=%fused_computation.2 | convolution fusion | flops 3356098560 | bytes 15728640 | tf_op jit(solution)/shard_map/dot_general | solution.py:105
  174.2 0.0 collective-permute-done.1.k2
  174.2 0.0 collective-permute-done.4.v2
  174.2 0.0 collective-permute-done.2.k3
  174.2 0.0 collective-permute-done.5.v3
  174.2 31.6 %shard_map.102 = (bf16[256,2560]{1,0:T(8,128)(2,1)}, bf16[256,2560]{1,0:T(8,128)(2,1)}, bf16[4,256,2560]{2,1,0:T(8,128)(2,1)}, bf16[4,256,2560]{2,1,0:T(8,128)(2,1)}) custom-call(bf16[256,2560]{1,0:T(8,128)(2,1)} %q_ref.1, bf16[256,2560]{1,0:T(8,128)(2,1)} %k0.1, bf16[256,2560]{1,0:T(8,128)(2,1)} %collective-permute-done.k1, ...), custom_call_target="tpu_custom_call" | custom-call | tf_op jit(solution)/shard_map/pallas_call | solution.py:55
  205.8 0.0 copy-start.3
  205.8 2.1 slice.36
  207.8 0.1 collective-permute-start.8
  207.9 1.1 copy-done.3
  209.0 0.0 copy-start.4
  209.0 0.2 slice.31
  209.2 0.1 collective-permute-start.6
  209.3 3.5 %collective-permute-done.8 = bf16[2,256,2560]{2,1,0:T(8,128)(2,1)S(1)} collective-permute-done((bf16[2,256,2560]{2,1,0:T(8,128)(2,1)S(1)}, bf16[2,256,2560]{2,1,0:T(8,128)(2,1)S(1)}, u32[]{:S(2)}, u32[]{:S(2)}) %collective-permute-start.8) | collective-permute-done | bytes 2621472 | tf_op jit(solution)/shard_map/ppermute | solution.py:71
  212.8 0.0 copy-done.4
  212.8 0.3 fusion.3
  213.2 0.0 copy-start.5
  213.2 0.1 collective-permute-start.9
  213.3 3.3 %collective-permute-done.6 = bf16[2,256,2560]{2,1,0:T(8,128)(2,1)S(1)} collective-permute-done((bf16[2,256,2560]{2,1,0:T(8,128)(2,1)S(1)}, bf16[2,256,2560]{2,1,0:T(8,128)(2,1)S(1)}, u32[]{:S(2)}, u32[]{:S(2)}) %collective-permute-start.6) | collective-permute-done | bytes 2621472 | tf_op jit(solution)/shard_map/ppermute | solution.py:71
  216.6 0.3 fusion.2
  216.9 0.3 collective-permute-start.7
  217.2 0.0 copy-done.5
  217.2 9.4 %convolution_convert_fusion = bf16[256,2560]{1,0:T(8,128)(2,1)} fusion(bf16[256,2560]{1,0:T(8,128)(2,1)S(1)} %copy-done.5, bf16[2560,2560]{1,0:T(8,128)(2,1)} %bitcast.26), kind=kOutput, calls=%fused_computation.1 | convolution fusion | flops 3356098560 | bytes 15728640 | tf_op jit(solution)/shard_map/dot_general | solution.py:112
  226.6 16.9 %collective-permute-done.9 = bf16[256,2560]{1,0:T(8,128)(2,1)S(1)} collective-permute-done((bf16[256,2560]{1,0:T(8,128)(2,1)S(1)}, bf16[256,2560]{1,0:T(8,128)(2,1)S(1)}, u32[]{:S(2)}, u32[]{:S(2)}) %collective-permute-start.9) | collective-permute-done | bytes 1310752 | tf_op jit(solution)/shard_map/ppermute | solution.py:71
  243.5 1.5 fusion
  245.0 26.6 %collective-permute-done.7 = bf16[256,2560]{1,0:T(8,128)(2,1)S(1)} collective-permute-done((bf16[256,2560]{1,0:T(8,128)(2,1)S(1)}, bf16[256,2560]{1,0:T(8,128)(2,1)S(1)}, u32[]{:S(2)}, u32[]{:S(2)}) %collective-permute-start.7) | collective-permute-done | bytes 1310752 | tf_op jit(solution)/shard_map/ppermute | solution.py:71
  271.5 0.0 copy-start.1
  271.5 1.5 fusion.1
  273.1 0.0 copy-done.1
  (4 shorter events, 0.0 us)
Async XLA Ops:
  7.2 157.7 %copy-start = (bf16[256,2560]{1,0:T(8,128)(2,1)S(1)}, bf16[256,2560]{1,0:T(8,128)(2,1)}, u32[]{:S(2)}) copy-start(bf16[256,2560]{1,0:T(8,128)(2,1)} %param.11) | copy-start | bytes 3932164
  7.2 96.1 %all-gather.5.cloned.1.call-start = ((), (), s32[]{:S(2)}) async-start(), calls=%async_computation | async-start | bytes 6758400 | tf_op jit(solution)/shard_map/all_gather | solution.py:83
  7.9 156.9 %all-gather.7.cloned.1.call-start = ((), (), s32[]{:S(2)}) async-start(), calls=%async_computation.1 | async-start | bytes 19660800 | tf_op jit(solution)/shard_map/all_gather | solution.py:84
  103.3 4.3 %copy-start.2 = (s32[4]{0:T(128)S(1)}, s32[4]{0:T(128)}, u32[]{:S(2)}) copy-start(s32[4]{0:T(128)} %constant.90.clone) | copy-start | bytes 52
  103.3 29.6 %collective-permute-start = (bf16[256,2560]{1,0:T(8,128)(2,1)}, bf16[256,2560]{1,0:T(8,128)(2,1)}, u32[]{:S(2)}, u32[]{:S(2)}) collective-permute-start(bf16[256,2560]{1,0:T(8,128)(2,1)} %k0.1), channel_id=1, source_target_pairs={{0,2},{2,0},{4,6},{6,4},{8,10},{10,8},{12,14},{14,12},{16,18},{18,... | collective-permute-start | bytes 3932168 | tf_op jit(solution)/shard_map/ppermute | solution.py:71
  103.4 57.6 %collective-permute-start.3 = (bf16[256,2560]{1,0:T(8,128)(2,1)}, bf16[256,2560]{1,0:T(8,128)(2,1)}, u32[]{:S(2)}, u32[]{:S(2)}) collective-permute-start(bf16[256,2560]{1,0:T(8,128)(2,1)} %v0.1), channel_id=1, source_target_pairs={{0,2},{2,0},{4,6},{6,4},{8,10},{10,8},{12,14},{14,12},{16,18},{18,... | collective-permute-start | bytes 3932168 | tf_op jit(solution)/shard_map/ppermute | solution.py:71
  104.8 69.3 %collective-permute-start.1 = (bf16[256,2560]{1,0:T(8,128)(2,1)}, bf16[256,2560]{1,0:T(8,128)(2,1)}, u32[]{:S(2)}, u32[]{:S(2)}) collective-permute-start(bf16[256,2560]{1,0:T(8,128)(2,1)} %k0.1), channel_id=1, source_target_pairs={{0,1},{1,0},{2,3},{3,2},{4,5},{5,4},{6,7},{7,6},{8,9},{9,8},{10,11... | collective-permute-start | bytes 3932168 | tf_op jit(solution)/shard_map/ppermute | solution.py:71
  106.5 67.6 %collective-permute-start.4 = (bf16[256,2560]{1,0:T(8,128)(2,1)}, bf16[256,2560]{1,0:T(8,128)(2,1)}, u32[]{:S(2)}, u32[]{:S(2)}) collective-permute-start(bf16[256,2560]{1,0:T(8,128)(2,1)} %v0.1), channel_id=1, source_target_pairs={{0,1},{1,0},{2,3},{3,2},{4,5},{5,4},{6,7},{7,6},{8,9},{9,8},{10,11... | collective-permute-start | bytes 3932168 | tf_op jit(solution)/shard_map/ppermute | solution.py:71
  132.9 41.3 %collective-permute-start.2 = (bf16[256,2560]{1,0:T(8,128)(2,1)}, bf16[256,2560]{1,0:T(8,128)(2,1)}, u32[]{:S(2)}, u32[]{:S(2)}) collective-permute-start(bf16[256,2560]{1,0:T(8,128)(2,1)} %collective-permute-done.k1), channel_id=1, source_target_pairs={{0,1},{1,0},{2,3},{3,2},{4,5},{5,4},{6,7},{7,6},{8,9},{9,8},{10,11... | collective-permute-start | bytes 3932168 | tf_op jit(solution)/shard_map/ppermute | solution.py:71
  161.0 13.2 %collective-permute-start.5 = (bf16[256,2560]{1,0:T(8,128)(2,1)}, bf16[256,2560]{1,0:T(8,128)(2,1)}, u32[]{:S(2)}, u32[]{:S(2)}) collective-permute-start(bf16[256,2560]{1,0:T(8,128)(2,1)} %collective-permute-done.3.v1), channel_id=1, source_target_pairs={{0,1},{1,0},{2,3},{3,2},{4,5},{5,4},{6,7},{7,6},{8,9},{9,8},{10,11... | collective-permute-start | bytes 3932168 | tf_op jit(solution)/shard_map/ppermute | solution.py:71
  205.8 3.3 %copy-start.3 = (bf16[4,256,2560]{2,1,0:T(8,128)(2,1)S(1)}, bf16[4,256,2560]{2,1,0:T(8,128)(2,1)}, u32[]{:S(2)}) copy-start(bf16[4,256,2560]{2,1,0:T(8,128)(2,1)} %get-tuple-element.10) | copy-start | bytes 15728644
  207.8 5.0 %collective-permute-start.8 = (bf16[2,256,2560]{2,1,0:T(8,128)(2,1)S(1)}, bf16[2,256,2560]{2,1,0:T(8,128)(2,1)S(1)}, u32[]{:S(2)}, u32[]{:S(2)}) collective-permute-start(bf16[2,256,2560]{2,1,0:T(8,128)(2,1)S(1)} %slice.36), channel_id=1, source_target_pairs={{0,1},{1,0},{2,3},{3,2},{4,5},{5,4},{6,7},{7,6},{8,9},{9,8},{10,11... | collective-permute-start | bytes 7864328 | tf_op jit(solution)/shard_map/ppermute | solution.py:71
  209.0 3.8 %copy-start.4 = (bf16[4,256,2560]{2,1,0:T(8,128)(2,1)S(1)}, bf16[4,256,2560]{2,1,0:T(8,128)(2,1)}, u32[]{:S(2)}) copy-start(bf16[4,256,2560]{2,1,0:T(8,128)(2,1)} %get-tuple-element.11) | copy-start | bytes 15728644
  209.2 7.4 %collective-permute-start.6 = (bf16[2,256,2560]{2,1,0:T(8,128)(2,1)S(1)}, bf16[2,256,2560]{2,1,0:T(8,128)(2,1)S(1)}, u32[]{:S(2)}, u32[]{:S(2)}) collective-permute-start(bf16[2,256,2560]{2,1,0:T(8,128)(2,1)S(1)} %slice.31), channel_id=1, source_target_pairs={{0,1},{1,0},{2,3},{3,2},{4,5},{5,4},{6,7},{7,6},{8,9},{9,8},{10,11... | collective-permute-start | bytes 7864328 | tf_op jit(solution)/shard_map/ppermute | solution.py:71
  213.2 4.0 %copy-start.5 = (bf16[256,2560]{1,0:T(8,128)(2,1)S(1)}, bf16[256,2560]{1,0:T(8,128)(2,1)}, u32[]{:S(2)}) copy-start(bf16[256,2560]{1,0:T(8,128)(2,1)} %get-tuple-element.8) | copy-start | bytes 3932164
  213.2 30.3 %collective-permute-start.9 = (bf16[256,2560]{1,0:T(8,128)(2,1)S(1)}, bf16[256,2560]{1,0:T(8,128)(2,1)S(1)}, u32[]{:S(2)}, u32[]{:S(2)}) collective-permute-start(bf16[256,2560]{1,0:T(8,128)(2,1)S(1)} %fusion.3), channel_id=1, source_target_pairs={{0,2},{2,0},{4,6},{6,4},{8,10},{10,8},{12,14},{14,12},{16,18},{18,... | collective-permute-start | bytes 3932168 | tf_op jit(solution)/shard_map/ppermute | solution.py:71
  216.9 54.6 %collective-permute-start.7 = (bf16[256,2560]{1,0:T(8,128)(2,1)S(1)}, bf16[256,2560]{1,0:T(8,128)(2,1)S(1)}, u32[]{:S(2)}, u32[]{:S(2)}) collective-permute-start(bf16[256,2560]{1,0:T(8,128)(2,1)S(1)} %fusion.2), channel_id=1, source_target_pairs={{0,2},{2,0},{4,6},{6,4},{8,10},{10,8},{12,14},{14,12},{16,18},{18,... | collective-permute-start | bytes 3932168 | tf_op jit(solution)/shard_map/ppermute | solution.py:71
  271.5 1.5 copy-start.1
Sparse Core Ops, SparseCore 0:
  10.6 92.6 all-gather.4
  105.1 28.7 all-gather.6

commit v2 on v1

v2 whole, which is shorter than its diff:
```python
import math

import jax
import jax.numpy as jnp
from jax import lax
from jax.experimental import pallas as pl
from jax.experimental.pallas import tpu as pltpu
from jax.sharding import Mesh
from jax.sharding import PartitionSpec as P

HEADS = 20
HSIZE = 128
BLK = 64
QBLK = 16
NSEL = 6
LEN = 1024

SLOT_XOR = (0, 2, 1, 3)


def masked_scores(q, k, mask):
    scaling = 1.0 / math.sqrt(HSIZE)
    nt = (((1,), (1,)), ((), ()))
    s = lax.dot_general(q, k, nt, preferred_element_type=jnp.float32) * scaling
    return jnp.where(mask > 0, s, -jnp.inf)


def fwd_kernel(q_ref, k0, k1, k2, k3, v0, v1, v2, v3, mask_ref, ctx_ref, lse_ref):
    q = q_ref[...]
    k = jnp.concatenate([k0[...], k1[...], k2[...], k3[...]], axis=0)
    v = jnp.concatenate([v0[...], v1[...], v2[...], v3[...]], axis=0)
    s = masked_scores(q, k, mask_ref[...])
    m = jnp.max(s, axis=1, keepdims=True)
    total = jnp.sum(jnp.exp(s - m), axis=1, keepdims=True)
    lse = m + jnp.log(total)
    p_low = jnp.exp(s - lse).astype(jnp.bfloat16)
    ctx_ref[...] = jnp.dot(p_low, v, preferred_element_type=jnp.float32).astype(jnp.bfloat16)
    lse_ref[...] = lse.reshape(lse_ref.shape)


def bwd_kernel(q_ref, k0, k1, k2, k3, v0, v1, v2, v3, do_ref, ctx_ref, lse_ref, mask_ref,
               dq_ref, dk_ref, dv_ref):
    scaling = 1.0 / math.sqrt(HSIZE)
    nt = (((1,), (1,)), ((), ()))
    tn = (((0,), (0,)), ((), ()))
    q = q_ref[...]
    k = jnp.concatenate([k0[...], k1[...], k2[...], k3[...]], axis=0)
    v = jnp.concatenate([v0[...], v1[...], v2[...], v3[...]], axis=0)
    s = masked_scores(q, k, mask_ref[...])
    lse = lse_ref[...].reshape(s.shape[0], 1)
    p = jnp.exp(s - lse)
    p_low = p.astype(jnp.bfloat16)
    do = do_ref[...]
    dp = lax.dot_general(do, v, nt, preferred_element_type=jnp.float32)
    delta = jnp.sum(
        do.astype(jnp.float32) * ctx_ref[...].astype(jnp.float32), axis=1, keepdims=True
    )
    ds = (p * (dp - delta)).astype(jnp.bfloat16)
    dq = jnp.dot(ds, k, preferred_element_type=jnp.float32) * scaling
    dq_ref[...] = dq.astype(jnp.bfloat16)
    dk = lax.dot_general(ds, q, tn, preferred_element_type=jnp.float32) * scaling
    dv = lax.dot_general(p_low, do, tn, preferred_element_type=jnp.float32)
    dk_ref[...] = dk.astype(jnp.bfloat16).reshape(dk_ref.shape)
    dv_ref[...] = dv.astype(jnp.bfloat16).reshape(dv_ref.shape)


def attention_fwd(q, ks, vs, mask):
    rows, width = q.shape
    heads = width // HSIZE
    col = pl.BlockSpec((rows, HSIZE), lambda h: (0, h))
    return pl.pallas_call(
        fwd_kernel,
        grid=(heads,),
        in_specs=[col] * 9 + [pl.BlockSpec(mask.shape, lambda h: (0, 0))],
        out_specs=[col, pl.BlockSpec((1, rows, 1), lambda h: (h, 0, 0))],
        out_shape=[
            jax.ShapeDtypeStruct((rows, width), jnp.bfloat16),
            jax.ShapeDtypeStruct((heads, rows, 1), jnp.float32),
        ],
    )(q, *ks, *vs, mask)


def attention_bwd(q, ks, vs, do, ctx, lse, mask, first, count):
    rows, width = q.shape
    col = pl.BlockSpec((rows, HSIZE), lambda h: (0, h + first))
    out_col = pl.BlockSpec((rows, HSIZE), lambda h: (0, h))
    slot_col = pl.BlockSpec((4, rows, HSIZE), lambda h: (0, 0, h))
    return pl.pallas_call(
        bwd_kernel,
        grid=(count,),
        in_specs=[col] * 11
        + [
            pl.BlockSpec((1, rows, 1), lambda h: (h + first, 0, 0)),
            pl.BlockSpec(mask.shape, lambda h: (0, 0)),
        ],
        out_specs=[out_col, slot_col, slot_col],
        out_shape=[
            jax.ShapeDtypeStruct((rows, count * HSIZE), jnp.bfloat16),
            jax.ShapeDtypeStruct((4, rows, count * HSIZE), jnp.bfloat16),
            jax.ShapeDtypeStruct((4, rows, count * HSIZE), jnp.bfloat16),
        ],
    )(q, *ks, *vs, do, ctx, lse, mask)


def swap(x, axis):
    count = lax.axis_size(axis)
    return lax.ppermute(x, axis, [(i, i ^ 1) for i in range(count)])


def per_device(query_rows, key_rows, value_rows, weight_out, cotangent, pattern):
    tok_rows = query_rows.shape[0]
    blocks_here = tok_rows // BLK
    zpos = lax.axis_index("z")
    ypos = lax.axis_index("y")
    core = lax.axis_index("core")
    seq_shards = LEN // tok_rows
    position = (ypos % 2) * 2 + core
    sequence = zpos * (lax.axis_size("y") // 2) + ypos // 2

    full_weight = lax.all_gather(weight_out, ("z", "y", "core"), axis=0, tiled=True)

    k_x = swap(key_rows, "y")
    v_x = swap(value_rows, "y")
    k_p = swap(key_rows, "core")
    v_p = swap(value_rows, "core")
    k_d = swap(k_x, "core")
    v_d = swap(v_x, "core")

    seq_plan = lax.dynamic_index_in_dim(pattern, sequence, 0, keepdims=False)
    own_plan = lax.dynamic_slice_in_dim(seq_plan, position * blocks_here, blocks_here, 0)
    rel = jnp.arange(seq_shards * blocks_here, dtype=jnp.int32)
    slot_xor = jnp.array(SLOT_XOR, dtype=jnp.int32)[rel // blocks_here]
    key_block = (position ^ slot_xor) * blocks_here + rel % blocks_here
    block_mask = jnp.any(own_plan[:, :, None] == key_block[None, None, :], axis=1)
    mask = jnp.broadcast_to(
        block_mask.astype(jnp.float32)[:, None, :, None],
        (blocks_here, BLK, seq_shards * blocks_here, BLK),
    ).reshape(tok_rows, seq_shards * tok_rows)

    ks = (key_rows, k_x, k_p, k_d)
    vs = (value_rows, v_x, v_p, v_d)
    ctx, lse = attention_fwd(query_rows, ks, vs, mask)

    grad_context = lax.dot_general(
        cotangent, full_weight, (((1,), (1,)), ((), ())), preferred_element_type=jnp.float32
    ).astype(jnp.bfloat16)

    def reduce_parts(parts):
        back = swap(parts[2:4], "core")
        own = parts[0].astype(jnp.float32) + back[0].astype(jnp.float32)
        cross = (parts[1].astype(jnp.float32) + back[1].astype(jnp.float32)).astype(jnp.bfloat16)
        arrived = swap(cross, "y")
        return (own + arrived.astype(jnp.float32)).astype(jnp.bfloat16)

    heads = query_rows.shape[1] // HSIZE
    half = heads // 2
    pieces = []
    for first, count in ((0, half), (half, heads - half)):
        dq, dk, dv = attention_bwd(
            query_rows, ks, vs, grad_context, ctx, lse, mask, first, count
        )
        pieces.append((dq, reduce_parts(dk), reduce_parts(dv)))
    grad_queries = jnp.concatenate([p[0] for p in pieces], axis=1)
    grad_keys = jnp.concatenate([p[1] for p in pieces], axis=1)
    grad_values = jnp.concatenate([p[2] for p in pieces], axis=1)

    sublayer_out = jnp.dot(ctx, full_weight, preferred_element_type=jnp.float32).astype(
        jnp.bfloat16
    )
    return (sublayer_out, grad_queries, grad_keys, grad_values)


def solution(mesh):
    devices = mesh.devices.reshape(mesh.devices.shape[0], -1, 4, 2)
    split = Mesh(devices, ("member", "z", "y", "core"))
    rows = P(("member", "z", "y", "core"), None)
    return jax.shard_map(
        per_device,
        mesh=split,
        in_specs=(rows, rows, rows, rows, rows, P("member", None, None)),
        out_specs=(rows, rows, rows, rows),
        check_vma=False,
    )
```

time: 280 us -> 236 us (0.84)
  waiting for transfers between devices: 195 us -> 110 us
  Pallas kernels: 31.6 us -> 51.2 us
  starting transfers between devices: 9.49 us -> 21.6 us
  local copies, waits for them, and re-layouts: 6.76 us -> 12.8 us
    all_gather x2 -> x1, waiting for transfers between devices: 95.3 us -> 3.63 us  [per_device(): lax.all_gather(weight_out, ('z', 'y', 'core'), axis=0, tiled=True)]
    pallas_call x1 -> x3, Pallas kernels: 31.6 us -> 51.2 us  [the longest x2 29 us: attention_bwd(): pl.pallas_call(bwd_kernel, grid=(count,), in_specs=[col] * 11 + [pl.Block...]
    ppermute x10 -> x14, starting transfers between devices: 9.41 us -> 21.6 us  [swap(): return lax.ppermute(x, axis, [(i, i ^ 1) for i in range(count)])]
    ppermute x10 -> x14, waiting for transfers between devices: 99.4 us -> 106 us  [swap(): return lax.ppermute(x, axis, [(i, i ^ 1) for i in range(count)])]
    concatenate x0 -> x3, other arithmetic: none -> 3.44 us  [the longest x1 1.15 us: per_device(): grad_values = jnp.concatenate([p[2] for p in pieces], axis=1)]
  transfers between devices with their start and end apart: 12 -> 15, of which waited for: 7 -> 6; matrix products, arithmetic and copies ran while one was open for 9% -> 8% of each run, Pallas kernels for 0% -> 10%
where the time goes in v2:
time: 236 us; the launch traced here: 234 us
  waiting for transfers between devices  110 us (47%)
  Pallas kernels  51.2 us (22%)
  starting transfers between devices  21.6 us (9%)
  matrix products  18.7 us (8%)
  between operations  14.2 us (6%)
  local copies, waits for them, and re-layouts  12.8 us (5%)
  other arithmetic  5.16 us (2%)
    ppermute x14, waiting for transfers between devices, swap(): return lax.ppermute(x, axis, [(i, i ^ 1) for i in range(count)])  106 us
    pallas_call x2, Pallas kernels, attention_bwd(): pl.pallas_call(bwd_kernel, grid=(count,), in_specs=[col] * 11 + [pl.Block...  29 us
    pallas_call x1, Pallas kernels, attention_fwd(): pl.pallas_call(fwd_kernel, grid=(heads,), in_specs=[col] * 9 + [pl.BlockS...  22.2 us
    ppermute x14, starting transfers between devices, swap(): return lax.ppermute(x, axis, [(i, i ^ 1) for i in range(count)])  21.6 us
    dot_general x1, matrix products, per_device(): jnp.dot(ctx, full_weight, preferred_element_type=jnp.float32)  9.37 us
    dot_general x1, matrix products, per_device(): lax.dot_general(cotangent, full_weight, (((1,), (1,)), ((), ())), preferr...  9.35 us
  transfers between devices with their start and end apart: 15, of which 6 were waited for; matrix products, arithmetic and copies ran while one was open for 8% of the time, Pallas kernels for 10%

profile of v2, /device:TPU:1, one launch (start us, length us, event | category | flops | bytes accessed | tf_op | source)
XLA Modules:
  0.0 233.9 jit_solution(11874783646934060670)
XLA Ops:
  7.2 0.0 copy-start
  7.2 0.0 all-gather.2.cloned.1.call-start
  7.2 0.7 all-gather.2.cloned.1.call-update
  7.9 2.2 collective-permute-start
  10.1 0.1 collective-permute-start.3
  10.2 3.0 %collective-permute-start.1 = (bf16[256,2560]{1,0:T(8,128)(2,1)}, bf16[256,2560]{1,0:T(8,128)(2,1)}, u32[]{:S(2)}, u32[]{:S(2)}) collective-permute-start(bf16[256,2560]{1,0:T(8,128)(2,1)} %k0.5), channel_id=1, source_target_pairs={{0,1},{1,0},{2,3},{3,2},{4,5},{5,4},{6,7},{7,6},{8,9},{9,8},{10,11... | collective-permute-start | bytes 3932168 | tf_op jit(solution)/shard_map/ppermute | solution.py:107
  13.2 0.0 collective-permute-start.4
  13.2 27.4 %collective-permute-done.k1 = bf16[256,2560]{1,0:T(8,128)(2,1)S(1)} collective-permute-done((bf16[256,2560]{1,0:T(8,128)(2,1)}, bf16[256,2560]{1,0:T(8,128)(2,1)S(1)}, u32[]{:S(2)}, u32[]{:S(2)}) %collective-permute-start) | collective-permute-done | bytes 1310752 | tf_op jit(solution)/shard_map/ppermute | solution.py:107
  40.7 5.7 %collective-permute-start.2 = (bf16[256,2560]{1,0:T(8,128)(2,1)S(1)}, bf16[256,2560]{1,0:T(8,128)(2,1)}, u32[]{:S(2)}, u32[]{:S(2)}) collective-permute-start(bf16[256,2560]{1,0:T(8,128)(2,1)S(1)} %collective-permute-done.k1), channel_id=1, source_target_pairs={{0,1},{1,0},{2,3},{3,2},{4,5},{5,4},{6,7},{7,6},{8,9},{9,8},{10,11... | collective-permute-start | bytes 3932168 | tf_op jit(solution)/shard_map/ppermute | solution.py:107
  46.4 26.6 %collective-permute-done.3.v1 = bf16[256,2560]{1,0:T(8,128)(2,1)} collective-permute-done((bf16[256,2560]{1,0:T(8,128)(2,1)}, bf16[256,2560]{1,0:T(8,128)(2,1)}, u32[]{:S(2)}, u32[]{:S(2)}) %collective-permute-start.3) | collective-permute-done | bytes 1310752 | tf_op jit(solution)/shard_map/ppermute | solution.py:107
  73.0 5.5 %collective-permute-start.5 = (bf16[256,2560]{1,0:T(8,128)(2,1)}, bf16[256,2560]{1,0:T(8,128)(2,1)}, u32[]{:S(2)}, u32[]{:S(2)}) collective-permute-start(bf16[256,2560]{1,0:T(8,128)(2,1)} %collective-permute-done.3.v1), channel_id=1, source_target_pairs={{0,1},{1,0},{2,3},{3,2},{4,5},{5,4},{6,7},{7,6},{8,9},{9,8},{10,11... | collective-permute-start | bytes 3932168 | tf_op jit(solution)/shard_map/ppermute | solution.py:107
  78.5 0.8 constant_dynamic-slice_fusion
  79.3 0.1 copy.13
  79.4 0.1 copy.14
  79.5 1.3 gather_fusion
  80.8 0.1 compare_reduce_fusion
  80.9 1.5 broadcast_in_dim.2
  82.4 0.0 copy-done.2
  82.4 2.8 %reshape.102.mask_ref = f32[256,1024]{1,0:T(8,128)} reshape(f32[4,64,16,64]{3,2,1,0:T(8,128)} %broadcast_in_dim.2) | data formatting | bytes 2097152 | tf_op jit(solution)/shard_map/reshape | solution.py:138
  85.2 0.0 collective-permute-done.1.k2
  85.2 0.0 collective-permute-done.4.v2
  85.2 0.0 collective-permute-done.2.k3
  85.2 0.0 collective-permute-done.5.v3
  85.2 22.2 %shard_map.102 = (bf16[256,2560]{1,0:T(8,128)(2,1)}, f32[20,256,1]{2,1,0:T(8,128)}) custom-call(bf16[256,2560]{1,0:T(8,128)(2,1)} %q_ref.5, bf16[256,2560]{1,0:T(8,128)(2,1)} %k0.5, bf16[256,2560]{1,0:T(8,128)(2,1)} %copy-done.2, bf16[256,2560]{1,0:T(8,128)(2,1)} %collective-permute-done.1.k2, bf16[256,2560]{1,0:T(8,128)(2,1)} %collective-permute-done.2.k3, ...), custom_call_target="tpu_custom_call" | custom-call | tf_op jit(solution)/shard_map/pallas_call | solution.py:71
  107.5 3.6 %all-gather.2.cloned.1.call-done = bf16[2560,2560]{1,0:T(8,128)(2,1)} async-done(((bf16[40,2560]{1,0:T(8,128)(2,1)}), bf16[2560,2560]{1,0:T(8,128)(2,1)}) %all-gather.2.cloned.1.call-update) | async-done | bytes 13107216 | tf_op jit(solution)/shard_map/all_gather | solution.py:120
  111.1 9.4 %convolution_convert_fusion.do_ref = bf16[256,2560]{1,0:T(8,128)(2,1)} fusion(bf16[256,2560]{1,0:T(8,128)(2,1)S(1)} %copy-done, bf16[2560,2560]{1,0:T(8,128)(2,1)} %all-gather.2.cloned.1.call-done), kind=kOutput, calls=%fused_computation.1 | convolution fusion | flops 3356098560 | bytes 15728640 | tf_op jit(solution)/shard_map/dot_general | solution.py:144
  120.5 14.4 %shard_map.104 = (bf16[256,1280]{1,0:T(8,128)(2,1)}, bf16[4,256,1280]{2,1,0:T(8,128)(2,1)}, bf16[4,256,1280]{2,1,0:T(8,128)(2,1)}) custom-call(bf16[256,2560]{1,0:T(8,128)(2,1)} %q_ref.5, bf16[256,2560]{1,0:T(8,128)(2,1)} %k0.5, bf16[256,2560]{1,0:T(8,128)(2,1)} %copy-done.2, bf16[256,2560]{1,0:T(8,128)(2,1)} %collective-permute-done.1.k2, ...), custom_call_target="tpu_custom_call" | custom-call | tf_op jit(solution)/shard_map/pallas_call | solution.py:88
  134.9 1.6 slice.66
  136.5 0.6 copy-done.6
  137.0 1.1 slice.76
  138.2 14.5 %shard_map.103 = (bf16[256,1280]{1,0:T(8,128)(2,1)}, bf16[4,256,1280]{2,1,0:T(8,128)(2,1)}, bf16[4,256,1280]{2,1,0:T(8,128)(2,1)}) custom-call(bf16[256,2560]{1,0:T(8,128)(2,1)} %q_ref.5, bf16[256,2560]{1,0:T(8,128)(2,1)} %k0.5, bf16[256,2560]{1,0:T(8,128)(2,1)} %copy-done.2, bf16[256,2560]{1,0:T(8,128)(2,1)} %collective-permute-done.1.k2, ...), custom_call_target="tpu_custom_call" | custom-call | tf_op jit(solution)/shard_map/pallas_call | solution.py:88
  152.7 1.6 slice.61
  154.3 0.6 copy-done.8
  154.8 0.1 slice.71
  155.0 0.4 collective-permute-start.10
  155.3 0.2 collective-permute-start.6
  155.6 0.6 copy-done.9
  156.2 0.3 collective-permute-start.12
  156.4 0.2 collective-permute-start.8
  156.7 9.4 %convolution_convert_fusion.1 = bf16[256,2560]{1,0:T(8,128)(2,1)} fusion(bf16[256,2560]{1,0:T(8,128)(2,1)S(1)} %copy-done.3, bf16[2560,2560]{1,0:T(8,128)(2,1)} %all-gather.2.cloned.1.call-done), kind=kOutput, calls=%fused_computation.2 | convolution fusion | flops 3356098560 | bytes 15728640 | tf_op jit(solution)/shard_map/dot_general | solution.py:167
  166.1 1.1 pad_maximum_fusion
  167.2 0.0 collective-permute-done.10
  167.2 0.2 fusion.6
  167.4 1.4 collective-permute-start.11
  168.8 0.0 collective-permute-done.6
  168.8 0.2 fusion.4
  169.0 0.9 collective-permute-start.7
  169.9 0.0 collective-permute-done.12
  169.9 0.2 fusion.7
  170.0 0.8 collective-permute-start.13
  170.8 0.0 collective-permute-done.8
  170.8 0.2 fusion.5
  171.0 0.9 collective-permute-start.9
  171.8 11.6 %collective-permute-done.11 = bf16[256,1280]{1,0:T(8,128)(2,1)S(1)} collective-permute-done((bf16[256,1280]{1,0:T(8,128)(2,1)S(1)}, bf16[256,1280]{1,0:T(8,128)(2,1)S(1)}, u32[]{:S(2)}, u32[]{:S(2)}) %collective-permute-start.11) | collective-permute-done | bytes 655392 | tf_op jit(solution)/shard_map/ppermute | solution.py:107
  183.5 0.2 fusion.1
  183.7 27.8 %collective-permute-done.13 = bf16[256,1280]{1,0:T(8,128)(2,1)S(1)} collective-permute-done((bf16[256,1280]{1,0:T(8,128)(2,1)S(1)}, bf16[256,1280]{1,0:T(8,128)(2,1)S(1)}, u32[]{:S(2)}, u32[]{:S(2)}) %collective-permute-start.13) | collective-permute-done | bytes 655392 | tf_op jit(solution)/shard_map/ppermute | solution.py:107
  211.6 0.2 fusion
  211.8 1.1 pad_maximum_fusion.2
  212.9 0.0 collective-permute-done.7
  212.9 0.3 fusion.3
  213.2 12.4 %collective-permute-done.9 = bf16[256,1280]{1,0:T(8,128)(2,1)S(1)} collective-permute-done((bf16[256,1280]{1,0:T(8,128)(2,1)S(1)}, bf16[256,1280]{1,0:T(8,128)(2,1)S(1)}, u32[]{:S(2)}, u32[]{:S(2)}) %collective-permute-start.9) | collective-permute-done | bytes 655392 | tf_op jit(solution)/shard_map/ppermute | solution.py:107
  225.6 0.2 fusion.2
  225.8 1.1 pad_maximum_fusion.1
  227.0 0.0 copy-done.1
  (22 shorter events, 0.1 us)
Async XLA Ops:
  7.2 103.9 %copy-start = (bf16[256,2560]{1,0:T(8,128)(2,1)S(1)}, bf16[256,2560]{1,0:T(8,128)(2,1)}, u32[]{:S(2)}) copy-start(bf16[256,2560]{1,0:T(8,128)(2,1)} %param.11) | copy-start | bytes 3932164
  7.2 103.9 %all-gather.2.cloned.1.call-start = ((), (), s32[]{:S(2)}) async-start(), calls=%async_computation | async-start | bytes 13312000 | tf_op jit(solution)/shard_map/all_gather | solution.py:120
  7.9 32.7 %collective-permute-start = (bf16[256,2560]{1,0:T(8,128)(2,1)}, bf16[256,2560]{1,0:T(8,128)(2,1)S(1)}, u32[]{:S(2)}, u32[]{:S(2)}) collective-permute-start(bf16[256,2560]{1,0:T(8,128)(2,1)} %k0.5), channel_id=1, source_target_pairs={{0,2},{2,0},{4,6},{6,4},{1,3},{3,1},{5,7},{7,5},{8,10},{10,8},{12,... | collective-permute-start | bytes 3932168 | tf_op jit(solution)/shard_map/ppermute | solution.py:107
  10.1 62.9 %collective-permute-start.3 = (bf16[256,2560]{1,0:T(8,128)(2,1)}, bf16[256,2560]{1,0:T(8,128)(2,1)}, u32[]{:S(2)}, u32[]{:S(2)}) collective-permute-start(bf16[256,2560]{1,0:T(8,128)(2,1)} %v0.5), channel_id=1, source_target_pairs={{0,2},{2,0},{4,6},{6,4},{1,3},{3,1},{5,7},{7,5},{8,10},{10,8},{12,... | collective-permute-start | bytes 3932168 | tf_op jit(solution)/shard_map/ppermute | solution.py:107
  10.2 75.0 %collective-permute-start.1 = (bf16[256,2560]{1,0:T(8,128)(2,1)}, bf16[256,2560]{1,0:T(8,128)(2,1)}, u32[]{:S(2)}, u32[]{:S(2)}) collective-permute-start(bf16[256,2560]{1,0:T(8,128)(2,1)} %k0.5), channel_id=1, source_target_pairs={{0,1},{1,0},{2,3},{3,2},{4,5},{5,4},{6,7},{7,6},{8,9},{9,8},{10,11... | collective-permute-start | bytes 3932168 | tf_op jit(solution)/shard_map/ppermute | solution.py:107
  13.2 72.0 %collective-permute-start.4 = (bf16[256,2560]{1,0:T(8,128)(2,1)}, bf16[256,2560]{1,0:T(8,128)(2,1)}, u32[]{:S(2)}, u32[]{:S(2)}) collective-permute-start(bf16[256,2560]{1,0:T(8,128)(2,1)} %v0.5), channel_id=1, source_target_pairs={{0,1},{1,0},{2,3},{3,2},{4,5},{5,4},{6,7},{7,6},{8,9},{9,8},{10,11... | collective-permute-start | bytes 3932168 | tf_op jit(solution)/shard_map/ppermute | solution.py:107
  40.7 41.8 %copy-start.2 = (bf16[256,2560]{1,0:T(8,128)(2,1)}, bf16[256,2560]{1,0:T(8,128)(2,1)S(1)}, u32[]{:S(2)}) copy-start(bf16[256,2560]{1,0:T(8,128)(2,1)S(1)} %collective-permute-done.k1) | copy-start | bytes 3932164
  40.7 44.6 %collective-permute-start.2 = (bf16[256,2560]{1,0:T(8,128)(2,1)S(1)}, bf16[256,2560]{1,0:T(8,128)(2,1)}, u32[]{:S(2)}, u32[]{:S(2)}) collective-permute-start(bf16[256,2560]{1,0:T(8,128)(2,1)S(1)} %collective-permute-done.k1), channel_id=1, source_target_pairs={{0,1},{1,0},{2,3},{3,2},{4,5},{5,4},{6,7},{7,6},{8,9},{9,8},{10,11... | collective-permute-start | bytes 3932168 | tf_op jit(solution)/shard_map/ppermute | solution.py:107
  73.0 12.3 %collective-permute-start.5 = (bf16[256,2560]{1,0:T(8,128)(2,1)}, bf16[256,2560]{1,0:T(8,128)(2,1)}, u32[]{:S(2)}, u32[]{:S(2)}) collective-permute-start(bf16[256,2560]{1,0:T(8,128)(2,1)} %collective-permute-done.3.v1), channel_id=1, source_target_pairs={{0,1},{1,0},{2,3},{3,2},{4,5},{5,4},{6,7},{7,6},{8,9},{9,8},{10,11... | collective-permute-start | bytes 3932168 | tf_op jit(solution)/shard_map/ppermute | solution.py:107
  134.9 2.1 copy-start.6
  152.7 2.1 copy-start.8
  154.8 1.3 copy-start.9
  154.8 1.8 copy-start.3
  154.9 11.1 %copy-start.10 = (bf16[256,1280]{1,0:T(8,128)(2,1)S(1)}, bf16[256,1280]{1,0:T(8,128)(2,1)}, u32[]{:S(2)}) copy-start(bf16[256,1280]{1,0:T(8,128)(2,1)} %get-tuple-element.15) | copy-start | bytes 1966084
  154.9 11.1 %copy-start.11 = (bf16[256,1280]{1,0:T(8,128)(2,1)S(1)}, bf16[256,1280]{1,0:T(8,128)(2,1)}, u32[]{:S(2)}) copy-start(bf16[256,1280]{1,0:T(8,128)(2,1)} %get-tuple-element.14) | copy-start | bytes 1966084
  155.0 12.2 %collective-permute-start.10 = (bf16[2,256,1280]{2,1,0:T(8,128)(2,1)S(1)}, bf16[2,256,1280]{2,1,0:T(8,128)(2,1)S(1)}, u32[]{:S(2)}, u32[]{:S(2)}) collective-permute-start(bf16[2,256,1280]{2,1,0:T(8,128)(2,1)S(1)} %slice.71), channel_id=1, source_target_pairs={{0,1},{1,0},{2,3},{3,2},{4,5},{5,4},{6,7},{7,6},{8,9},{9,8},{10,11... | collective-permute-start | bytes 3932168 | tf_op jit(solution)/shard_map/ppermute | solution.py:107
  155.3 13.5 %collective-permute-start.6 = (bf16[2,256,1280]{2,1,0:T(8,128)(2,1)S(1)}, bf16[2,256,1280]{2,1,0:T(8,128)(2,1)S(1)}, u32[]{:S(2)}, u32[]{:S(2)}) collective-permute-start(bf16[2,256,1280]{2,1,0:T(8,128)(2,1)S(1)} %slice.61), channel_id=1, source_target_pairs={{0,1},{1,0},{2,3},{3,2},{4,5},{5,4},{6,7},{7,6},{8,9},{9,8},{10,11... | collective-permute-start | bytes 3932168 | tf_op jit(solution)/shard_map/ppermute | solution.py:107
  156.2 13.7 %collective-permute-start.12 = (bf16[2,256,1280]{2,1,0:T(8,128)(2,1)S(1)}, bf16[2,256,1280]{2,1,0:T(8,128)(2,1)S(1)}, u32[]{:S(2)}, u32[]{:S(2)}) collective-permute-start(bf16[2,256,1280]{2,1,0:T(8,128)(2,1)S(1)} %copy-done.9), channel_id=1, source_target_pairs={{0,1},{1,0},{2,3},{3,2},{4,5},{5,4},{6,7},{7,6},{8,9},{9,8},{10,11... | collective-permute-start | bytes 3932168 | tf_op jit(solution)/shard_map/ppermute | solution.py:107
  156.4 14.4 %collective-permute-start.8 = (bf16[2,256,1280]{2,1,0:T(8,128)(2,1)S(1)}, bf16[2,256,1280]{2,1,0:T(8,128)(2,1)S(1)}, u32[]{:S(2)}, u32[]{:S(2)}) collective-permute-start(bf16[2,256,1280]{2,1,0:T(8,128)(2,1)S(1)} %slice.66), channel_id=1, source_target_pairs={{0,1},{1,0},{2,3},{3,2},{4,5},{5,4},{6,7},{7,6},{8,9},{9,8},{10,11... | collective-permute-start | bytes 3932168 | tf_op jit(solution)/shard_map/ppermute | solution.py:107
  166.1 2.7 %copy-start.5 = (bf16[4,256,1280]{2,1,0:T(8,128)(2,1)S(1)}, bf16[4,256,1280]{2,1,0:T(8,128)(2,1)}, u32[]{:S(2)}) copy-start(bf16[4,256,1280]{2,1,0:T(8,128)(2,1)} %get-tuple-element.16) | copy-start | bytes 7864324
  167.2 2.7 %copy-start.7 = (bf16[4,256,1280]{2,1,0:T(8,128)(2,1)S(1)}, bf16[4,256,1280]{2,1,0:T(8,128)(2,1)}, u32[]{:S(2)}) copy-start(bf16[4,256,1280]{2,1,0:T(8,128)(2,1)} %get-tuple-element.19) | copy-start | bytes 7864324
  167.4 16.1 %collective-permute-start.11 = (bf16[256,1280]{1,0:T(8,128)(2,1)S(1)}, bf16[256,1280]{1,0:T(8,128)(2,1)S(1)}, u32[]{:S(2)}, u32[]{:S(2)}) collective-permute-start(bf16[256,1280]{1,0:T(8,128)(2,1)S(1)} %fusion.6), channel_id=1, source_target_pairs={{0,2},{2,0},{4,6},{6,4},{1,3},{3,1},{5,7},{7,5},{8,10},{10,8},{12,... | collective-permute-start | bytes 1966088 | tf_op jit(solution)/shard_map/ppermute | solution.py:107
  168.8 2.0 copy-start.4
  169.0 44.0 %collective-permute-start.7 = (bf16[256,1280]{1,0:T(8,128)(2,1)S(1)}, bf16[256,1280]{1,0:T(8,128)(2,1)S(1)}, u32[]{:S(2)}, u32[]{:S(2)}) collective-permute-start(bf16[256,1280]{1,0:T(8,128)(2,1)S(1)} %fusion.4), channel_id=1, source_target_pairs={{0,2},{2,0},{4,6},{6,4},{1,3},{3,1},{5,7},{7,5},{8,10},{10,8},{12,... | collective-permute-start | bytes 1966088 | tf_op jit(solution)/shard_map/ppermute | solution.py:107
  170.0 41.5 %collective-permute-start.13 = (bf16[256,1280]{1,0:T(8,128)(2,1)S(1)}, bf16[256,1280]{1,0:T(8,128)(2,1)S(1)}, u32[]{:S(2)}, u32[]{:S(2)}) collective-permute-start(bf16[256,1280]{1,0:T(8,128)(2,1)S(1)} %fusion.7), channel_id=1, source_target_pairs={{0,2},{2,0},{4,6},{6,4},{1,3},{3,1},{5,7},{7,5},{8,10},{10,8},{12,... | collective-permute-start | bytes 1966088 | tf_op jit(solution)/shard_map/ppermute | solution.py:107
  171.0 54.6 %collective-permute-start.9 = (bf16[256,1280]{1,0:T(8,128)(2,1)S(1)}, bf16[256,1280]{1,0:T(8,128)(2,1)S(1)}, u32[]{:S(2)}, u32[]{:S(2)}) collective-permute-start(bf16[256,1280]{1,0:T(8,128)(2,1)S(1)} %fusion.5), channel_id=1, source_target_pairs={{0,2},{2,0},{4,6},{6,4},{1,3},{3,1},{5,7},{7,5},{8,10},{10,8},{12,... | collective-permute-start | bytes 1966088 | tf_op jit(solution)/shard_map/ppermute | solution.py:107
  225.6 1.4 copy-start.1
Sparse Core Ops, SparseCore 0:
  10.7 100.3 all-gather.1

commit v3 on v2

--- a/solution.py
+++ b/solution.py
@@ -1,3 +1,4 @@
+import functools
 import math
 
 import jax
@@ -31,9 +32,10 @@
     v = jnp.concatenate([v0[...], v1[...], v2[...], v3[...]], axis=0)
     s = masked_scores(q, k, mask_ref[...])
     m = jnp.max(s, axis=1, keepdims=True)
-    total = jnp.sum(jnp.exp(s - m), axis=1, keepdims=True)
+    e = jnp.exp(s - m)
+    total = jnp.sum(e, axis=1, keepdims=True)
     lse = m + jnp.log(total)
-    p_low = jnp.exp(s - lse).astype(jnp.bfloat16)
+    p_low = (e * (1.0 / total)).astype(jnp.bfloat16)
     ctx_ref[...] = jnp.dot(p_low, v, preferred_element_type=jnp.float32).astype(jnp.bfloat16)
     lse_ref[...] = lse.reshape(lse_ref.shape)
 
@@ -71,6 +73,10 @@
     return pl.pallas_call(
         fwd_kernel,
         grid=(heads,),
+        cost_estimate=pl.CostEstimate(
+            flops=heads * 2 * 10**9, transcendentals=heads * rows * 1024,
+            bytes_accessed=12 * rows * width * 2,
+        ),
         in_specs=[col] * 9 + [pl.BlockSpec(mask.shape, lambda h: (0, 0))],
         out_specs=[col, pl.BlockSpec((1, rows, 1), lambda h: (h, 0, 0))],
         out_shape=[
@@ -88,6 +94,10 @@
     return pl.pallas_call(
         bwd_kernel,
         grid=(count,),
+        cost_estimate=pl.CostEstimate(
+            flops=count * 14 * 10**8, transcendentals=count * rows * 1024,
+            bytes_accessed=12 * rows * width,
+        ),
         in_specs=[col] * 11
         + [
             pl.BlockSpec((1, rows, 1), lambda h: (h + first, 0, 0)),
@@ -128,14 +138,12 @@
 
     seq_plan = lax.dynamic_index_in_dim(pattern, sequence, 0, keepdims=False)
     own_plan = lax.dynamic_slice_in_dim(seq_plan, position * blocks_here, blocks_here, 0)
-    rel = jnp.arange(seq_shards * blocks_here, dtype=jnp.int32)
+    rel = jnp.arange(seq_shards * tok_rows, dtype=jnp.int32) // BLK
     slot_xor = jnp.array(SLOT_XOR, dtype=jnp.int32)[rel // blocks_here]
     key_block = (position ^ slot_xor) * blocks_here + rel % blocks_here
-    block_mask = jnp.any(own_plan[:, :, None] == key_block[None, None, :], axis=1)
-    mask = jnp.broadcast_to(
-        block_mask.astype(jnp.float32)[:, None, :, None],
-        (blocks_here, BLK, seq_shards * blocks_here, BLK),
-    ).reshape(tok_rows, seq_shards * tok_rows)
+    plan_rows = own_plan[jnp.arange(tok_rows, dtype=jnp.int32) // BLK]
+    hits = [plan_rows[:, j][:, None] == key_block[None, :] for j in range(NSEL)]
+    mask = functools.reduce(jnp.logical_or, hits).astype(jnp.float32)
 
     ks = (key_rows, k_x, k_p, k_d)
     vs = (value_rows, v_x, v_p, v_d)

time: 236 us -> 237 us (level)
  local copies, waits for them, and re-layouts: 12.8 us -> 8.9 us
  waiting for transfers between devices: 110 us -> 113 us
    all_gather x1, waiting for transfers between devices: 3.63 us -> 6.48 us  [per_device(): lax.all_gather(weight_out, ('z', 'y', 'core'), axis=0, tiled=True)]
    reshape x1 -> x0, local copies, waits for them, and re-layouts: 2.78 us -> none  [per_device(): mask = jnp.broadcast_to(block_mask.astype(jnp.float32)[:, None, :, None],...]
  transfers between devices with their start and end apart: 15 -> 15, of which waited for: 6 -> 6; matrix products, arithmetic and copies ran while one was open for 8% -> 7% of each run, Pallas kernels for 10% -> 9%
where the time goes in v3:
time: 237 us; the launch traced here: 235 us
  waiting for transfers between devices  113 us (48%)
  Pallas kernels  51.2 us (22%)
  starting transfers between devices  21.6 us (9%)
  matrix products  19.1 us (8%)
  between operations  14.2 us (6%)
  local copies, waits for them, and re-layouts  8.9 us (4%)
  other arithmetic  6.86 us (3%)
    ppermute x14, waiting for transfers between devices, swap(): return lax.ppermute(x, axis, [(i, i ^ 1) for i in range(count)])  106 us
    pallas_call x2, Pallas kernels, attention_bwd(): pl.pallas_call(bwd_kernel, grid=(count,), cost_estimate=pl.CostEstimate(f...  29 us
    pallas_call x1, Pallas kernels, attention_fwd(): pl.pallas_call(fwd_kernel, grid=(heads,), cost_estimate=pl.CostEstimate(f...  22.2 us
    ppermute x14, starting transfers between devices, swap(): return lax.ppermute(x, axis, [(i, i ^ 1) for i in range(count)])  21.6 us
    dot_general x1, matrix products, per_device(): jnp.dot(ctx, full_weight, preferred_element_type=jnp.float32)  9.74 us
    dot_general x1, matrix products, per_device(): lax.dot_general(cotangent, full_weight, (((1,), (1,)), ((), ())), preferr...  9.35 us
    all_gather x1, waiting for transfers between devices, per_device(): lax.all_gather(weight_out, ('z', 'y', 'core'), axis=0, tiled=True)  6.48 us
    slice x4, local copies, waits for them, and re-layouts, reduce_parts(): back = swap(parts[2:4], 'core')  5.39 us
  transfers between devices with their start and end apart: 15, of which 6 were waited for; matrix products, arithmetic and copies ran while one was open for 7% of the time, Pallas kernels for 9%

profile of v3, /device:TPU:1, one launch (start us, length us, event | category | flops | bytes accessed | tf_op | source)
XLA Modules:
  0.0 235.0 jit_solution(6469093034349479142)
XLA Ops:
  7.2 0.0 copy-start
  7.2 0.0 all-gather.2.cloned.1.call-start
  7.2 0.7 all-gather.2.cloned.1.call-update
  7.9 2.2 collective-permute-start
  10.1 0.1 collective-permute-start.3
  10.2 3.0 %collective-permute-start.1 = (bf16[256,2560]{1,0:T(8,128)(2,1)}, bf16[256,2560]{1,0:T(8,128)(2,1)}, u32[]{:S(2)}, u32[]{:S(2)}) collective-permute-start(bf16[256,2560]{1,0:T(8,128)(2,1)} %k0.5), channel_id=1, source_target_pairs={{0,1},{1,0},{2,3},{3,2},{4,5},{5,4},{6,7},{7,6},{8,9},{9,8},{10,11... | collective-permute-start | bytes 3932168 | tf_op jit(solution)/shard_map/ppermute | solution.py:117
  13.2 0.0 collective-permute-start.4
  13.2 27.4 %collective-permute-done.k1 = bf16[256,2560]{1,0:T(8,128)(2,1)S(1)} collective-permute-done((bf16[256,2560]{1,0:T(8,128)(2,1)}, bf16[256,2560]{1,0:T(8,128)(2,1)S(1)}, u32[]{:S(2)}, u32[]{:S(2)}) %collective-permute-start) | collective-permute-done | bytes 1310752 | tf_op jit(solution)/shard_map/ppermute | solution.py:117
  40.7 5.7 %collective-permute-start.2 = (bf16[256,2560]{1,0:T(8,128)(2,1)S(1)}, bf16[256,2560]{1,0:T(8,128)(2,1)}, u32[]{:S(2)}, u32[]{:S(2)}) collective-permute-start(bf16[256,2560]{1,0:T(8,128)(2,1)S(1)} %collective-permute-done.k1), channel_id=1, source_target_pairs={{0,1},{1,0},{2,3},{3,2},{4,5},{5,4},{6,7},{7,6},{8,9},{9,8},{10,11... | collective-permute-start | bytes 3932168 | tf_op jit(solution)/shard_map/ppermute | solution.py:117
  46.4 26.6 %collective-permute-done.3.v1 = bf16[256,2560]{1,0:T(8,128)(2,1)} collective-permute-done((bf16[256,2560]{1,0:T(8,128)(2,1)}, bf16[256,2560]{1,0:T(8,128)(2,1)}, u32[]{:S(2)}, u32[]{:S(2)}) %collective-permute-start.3) | collective-permute-done | bytes 1310752 | tf_op jit(solution)/shard_map/ppermute | solution.py:117
  73.0 5.5 %collective-permute-start.5 = (bf16[256,2560]{1,0:T(8,128)(2,1)}, bf16[256,2560]{1,0:T(8,128)(2,1)}, u32[]{:S(2)}, u32[]{:S(2)}) collective-permute-start(bf16[256,2560]{1,0:T(8,128)(2,1)} %collective-permute-done.3.v1), channel_id=1, source_target_pairs={{0,1},{1,0},{2,3},{3,2},{4,5},{5,4},{6,7},{7,6},{8,9},{9,8},{10,11... | collective-permute-start | bytes 3932168 | tf_op jit(solution)/shard_map/ppermute | solution.py:117
  78.5 0.8 constant_dynamic-slice_fusion
  79.3 0.1 copy.12
  79.4 0.7 gather_fusion
  80.2 0.5 slice_reduce_fusion.5
  80.7 1.8 or_convert_fusion.mask_ref
  82.4 0.0 collective-permute-done.1.k2
  82.4 0.0 collective-permute-done.4.v2
  82.4 0.0 collective-permute-done.2.k3
  82.5 0.0 collective-permute-done.5.v3
  82.5 22.2 %shard_map.102 = (bf16[256,2560]{1,0:T(8,128)(2,1)}, f32[20,256,1]{2,1,0:T(8,128)}) custom-call(bf16[256,2560]{1,0:T(8,128)(2,1)} %q_ref.5, bf16[256,2560]{1,0:T(8,128)(2,1)} %k0.5, bf16[256,2560]{1,0:T(8,128)(2,1)} %copy-done.10, bf16[256,2560]{1,0:T(8,128)(2,1)} %collective-permute-done.1.k2, bf16[256,2560]{1,0:T(8,128)(2,1)} %collective-permute-done.2.k3, ...), custom_call_target="tpu_custom_call" | custom-call | flops 40000000000 | bytes 15728640 | tf_op jit(solution)/shard_map/pallas_call | solution.py:73
  104.6 6.5 %all-gather.2.cloned.1.call-done = bf16[2560,2560]{1,0:T(8,128)(2,1)} async-done(((bf16[40,2560]{1,0:T(8,128)(2,1)}), bf16[2560,2560]{1,0:T(8,128)(2,1)}) %all-gather.2.cloned.1.call-update) | async-done | bytes 13107216 | tf_op jit(solution)/shard_map/all_gather | solution.py:130
  111.1 0.0 copy-done
  111.1 9.4 %convolution_convert_fusion.do_ref = bf16[256,2560]{1,0:T(8,128)(2,1)} fusion(bf16[256,2560]{1,0:T(8,128)(2,1)S(1)} %copy-done, bf16[2560,2560]{1,0:T(8,128)(2,1)} %all-gather.2.cloned.1.call-done), kind=kOutput, calls=%fused_computation.1 | convolution fusion | flops 3356098560 | bytes 15728640 | tf_op jit(solution)/shard_map/dot_general | solution.py:152
  120.5 14.4 %shard_map.104 = (bf16[256,1280]{1,0:T(8,128)(2,1)}, bf16[4,256,1280]{2,1,0:T(8,128)(2,1)}, bf16[4,256,1280]{2,1,0:T(8,128)(2,1)}) custom-call(bf16[256,2560]{1,0:T(8,128)(2,1)} %q_ref.5, bf16[256,2560]{1,0:T(8,128)(2,1)} %k0.5, bf16[256,2560]{1,0:T(8,128)(2,1)} %copy-done.10, bf16[256,2560]{1,0:T(8,128)(2,1)} %collective-permute-done.1.k2, ...), custom_call_target="tpu_custom_call" | custom-call | flops 14000000000 | bytes 7864320 | tf_op jit(solution)/shard_map/pallas_call | solution.py:94
  134.9 2.6 %slice.90 = bf16[2,256,1280]{2,1,0:T(8,128)(2,1)} slice(bf16[4,256,1280]{2,1,0:T(8,128)(2,1)} %get-tuple-element.17), slice={[2:4], [0:256], [0:1280]} | slice | bytes 2621440 | tf_op jit(solution)/shard_map/slice | solution.py:157
  137.5 1.1 slice.100
  138.7 14.6 %shard_map.103 = (bf16[256,1280]{1,0:T(8,128)(2,1)}, bf16[4,256,1280]{2,1,0:T(8,128)(2,1)}, bf16[4,256,1280]{2,1,0:T(8,128)(2,1)}) custom-call(bf16[256,2560]{1,0:T(8,128)(2,1)} %q_ref.5, bf16[256,2560]{1,0:T(8,128)(2,1)} %k0.5, bf16[256,2560]{1,0:T(8,128)(2,1)} %copy-done.10, bf16[256,2560]{1,0:T(8,128)(2,1)} %collective-permute-done.1.k2, ...), custom_call_target="tpu_custom_call" | custom-call | flops 14000000000 | bytes 7864320 | tf_op jit(solution)/shard_map/pallas_call | solution.py:94
  153.3 1.6 slice.85
  154.8 0.6 copy-done.5
  155.4 0.1 slice.95
  155.5 0.3 collective-permute-start.10
  155.9 0.2 collective-permute-start.6
  156.1 0.6 copy-done.7
  156.7 0.3 collective-permute-start.12
  157.0 0.1 copy-done.6
  157.1 0.3 collective-permute-start.8
  157.4 9.7 %convolution_convert_fusion.1 = bf16[256,2560]{1,0:T(8,128)(2,1)} fusion(bf16[256,2560]{1,0:T(8,128)(2,1)} %get-tuple-element.12.ctx_ref, bf16[2560,2560]{1,0:T(8,128)(2,1)} %all-gather.2.cloned.1.call-done), kind=kOutput, calls=%fused_computation.2 | convolution fusion | flops 3356098560 | bytes 15728640 | tf_op jit(solution)/shard_map/dot_general | solution.py:175
  167.1 0.0 copy-done.8
  167.1 1.1 pad_maximum_fusion
  168.3 0.0 collective-permute-done.10
  168.3 0.2 fusion.6
  168.4 1.4 collective-permute-start.11
  169.8 0.0 collective-permute-done.6
  169.8 0.2 fusion.4
  170.0 0.9 collective-permute-start.7
  170.9 0.0 collective-permute-done.12
  170.9 0.2 fusion.7
  171.1 0.7 collective-permute-start.13
  171.8 0.0 collective-permute-done.8
  171.8 0.0 copy-done.2
  171.8 0.2 fusion.5
  172.0 0.9 collective-permute-start.9
  172.9 11.7 %collective-permute-done.11 = bf16[256,1280]{1,0:T(8,128)(2,1)S(1)} collective-permute-done((bf16[256,1280]{1,0:T(8,128)(2,1)S(1)}, bf16[256,1280]{1,0:T(8,128)(2,1)S(1)}, u32[]{:S(2)}, u32[]{:S(2)}) %collective-permute-start.11) | collective-permute-done | bytes 655392 | tf_op jit(solution)/shard_map/ppermute | solution.py:117
  184.6 0.2 fusion.1
  184.8 27.8 %collective-permute-done.13 = bf16[256,1280]{1,0:T(8,128)(2,1)S(1)} collective-permute-done((bf16[256,1280]{1,0:T(8,128)(2,1)S(1)}, bf16[256,1280]{1,0:T(8,128)(2,1)S(1)}, u32[]{:S(2)}, u32[]{:S(2)}) %collective-permute-start.13) | collective-permute-done | bytes 655392 | tf_op jit(solution)/shard_map/ppermute | solution.py:117
  212.7 0.3 fusion
  212.9 1.1 pad_maximum_fusion.2
  214.1 0.0 collective-permute-done.7
  214.1 0.2 fusion.3
  214.3 12.4 %collective-permute-done.9 = bf16[256,1280]{1,0:T(8,128)(2,1)S(1)} collective-permute-done((bf16[256,1280]{1,0:T(8,128)(2,1)S(1)}, bf16[256,1280]{1,0:T(8,128)(2,1)S(1)}, u32[]{:S(2)}, u32[]{:S(2)}) %collective-permute-start.9) | collective-permute-done | bytes 655392 | tf_op jit(solution)/shard_map/ppermute | solution.py:117
  226.7 0.2 fusion.2
  226.9 1.1 pad_maximum_fusion.1
  228.1 0.0 copy-done.1
  (18 shorter events, 0.1 us)
Async XLA Ops:
  7.2 104.0 %copy-start = (bf16[256,2560]{1,0:T(8,128)(2,1)S(1)}, bf16[256,2560]{1,0:T(8,128)(2,1)}, u32[]{:S(2)}) copy-start(bf16[256,2560]{1,0:T(8,128)(2,1)} %param.11) | copy-start | bytes 3932164
  7.2 103.9 %all-gather.2.cloned.1.call-start = ((), (), s32[]{:S(2)}) async-start(), calls=%async_computation | async-start | bytes 13312000 | tf_op jit(solution)/shard_map/all_gather | solution.py:130
  7.9 32.7 %collective-permute-start = (bf16[256,2560]{1,0:T(8,128)(2,1)}, bf16[256,2560]{1,0:T(8,128)(2,1)S(1)}, u32[]{:S(2)}, u32[]{:S(2)}) collective-permute-start(bf16[256,2560]{1,0:T(8,128)(2,1)} %k0.5), channel_id=1, source_target_pairs={{0,2},{2,0},{4,6},{6,4},{1,3},{3,1},{5,7},{7,5},{8,10},{10,8},{12,... | collective-permute-start | bytes 3932168 | tf_op jit(solution)/shard_map/ppermute | solution.py:117
  10.1 62.9 %collective-permute-start.3 = (bf16[256,2560]{1,0:T(8,128)(2,1)}, bf16[256,2560]{1,0:T(8,128)(2,1)}, u32[]{:S(2)}, u32[]{:S(2)}) collective-permute-start(bf16[256,2560]{1,0:T(8,128)(2,1)} %v0.5), channel_id=1, source_target_pairs={{0,2},{2,0},{4,6},{6,4},{1,3},{3,1},{5,7},{7,5},{8,10},{10,8},{12,... | collective-permute-start | bytes 3932168 | tf_op jit(solution)/shard_map/ppermute | solution.py:117
  10.2 72.2 %collective-permute-start.1 = (bf16[256,2560]{1,0:T(8,128)(2,1)}, bf16[256,2560]{1,0:T(8,128)(2,1)}, u32[]{:S(2)}, u32[]{:S(2)}) collective-permute-start(bf16[256,2560]{1,0:T(8,128)(2,1)} %k0.5), channel_id=1, source_target_pairs={{0,1},{1,0},{2,3},{3,2},{4,5},{5,4},{6,7},{7,6},{8,9},{9,8},{10,11... | collective-permute-start | bytes 3932168 | tf_op jit(solution)/shard_map/ppermute | solution.py:117
  13.2 69.2 %collective-permute-start.4 = (bf16[256,2560]{1,0:T(8,128)(2,1)}, bf16[256,2560]{1,0:T(8,128)(2,1)}, u32[]{:S(2)}, u32[]{:S(2)}) collective-permute-start(bf16[256,2560]{1,0:T(8,128)(2,1)} %v0.5), channel_id=1, source_target_pairs={{0,1},{1,0},{2,3},{3,2},{4,5},{5,4},{6,7},{7,6},{8,9},{9,8},{10,11... | collective-permute-start | bytes 3932168 | tf_op jit(solution)/shard_map/ppermute | solution.py:117
  40.7 41.8 %copy-start.10 = (bf16[256,2560]{1,0:T(8,128)(2,1)}, bf16[256,2560]{1,0:T(8,128)(2,1)S(1)}, u32[]{:S(2)}) copy-start(bf16[256,2560]{1,0:T(8,128)(2,1)S(1)} %collective-permute-done.k1) | copy-start | bytes 3932164
  40.7 41.8 %collective-permute-start.2 = (bf16[256,2560]{1,0:T(8,128)(2,1)S(1)}, bf16[256,2560]{1,0:T(8,128)(2,1)}, u32[]{:S(2)}, u32[]{:S(2)}) collective-permute-start(bf16[256,2560]{1,0:T(8,128)(2,1)S(1)} %collective-permute-done.k1), channel_id=1, source_target_pairs={{0,1},{1,0},{2,3},{3,2},{4,5},{5,4},{6,7},{7,6},{8,9},{9,8},{10,11... | collective-permute-start | bytes 3932168 | tf_op jit(solution)/shard_map/ppermute | solution.py:117
  73.0 9.5 %collective-permute-start.5 = (bf16[256,2560]{1,0:T(8,128)(2,1)}, bf16[256,2560]{1,0:T(8,128)(2,1)}, u32[]{:S(2)}, u32[]{:S(2)}) collective-permute-start(bf16[256,2560]{1,0:T(8,128)(2,1)} %collective-permute-done.3.v1), channel_id=1, source_target_pairs={{0,1},{1,0},{2,3},{3,2},{4,5},{5,4},{6,7},{7,6},{8,9},{9,8},{10,11... | collective-permute-start | bytes 3932168 | tf_op jit(solution)/shard_map/ppermute | solution.py:117
  134.9 2.6 %copy-start.4 = (bf16[4,256,1280]{2,1,0:T(8,128)(2,1)S(1)}, bf16[4,256,1280]{2,1,0:T(8,128)(2,1)}, u32[]{:S(2)}) copy-start(bf16[4,256,1280]{2,1,0:T(8,128)(2,1)} %get-tuple-element.19) | copy-start | bytes 7864324
  153.3 2.1 copy-start.5
  155.4 1.3 copy-start.7
  155.4 1.7 copy-start.6
  155.5 11.6 %copy-start.8 = (bf16[256,1280]{1,0:T(8,128)(2,1)S(1)}, bf16[256,1280]{1,0:T(8,128)(2,1)}, u32[]{:S(2)}) copy-start(bf16[256,1280]{1,0:T(8,128)(2,1)} %get-tuple-element.15) | copy-start | bytes 1966084
  155.5 11.6 %copy-start.9 = (bf16[256,1280]{1,0:T(8,128)(2,1)S(1)}, bf16[256,1280]{1,0:T(8,128)(2,1)}, u32[]{:S(2)}) copy-start(bf16[256,1280]{1,0:T(8,128)(2,1)} %get-tuple-element.14) | copy-start | bytes 1966084
  155.5 12.8 %collective-permute-start.10 = (bf16[2,256,1280]{2,1,0:T(8,128)(2,1)S(1)}, bf16[2,256,1280]{2,1,0:T(8,128)(2,1)S(1)}, u32[]{:S(2)}, u32[]{:S(2)}) collective-permute-start(bf16[2,256,1280]{2,1,0:T(8,128)(2,1)S(1)} %slice.95), channel_id=1, source_target_pairs={{0,1},{1,0},{2,3},{3,2},{4,5},{5,4},{6,7},{7,6},{8,9},{9,8},{10,11... | collective-permute-start | bytes 3932168 | tf_op jit(solution)/shard_map/ppermute | solution.py:117
  155.9 14.0 %collective-permute-start.6 = (bf16[2,256,1280]{2,1,0:T(8,128)(2,1)S(1)}, bf16[2,256,1280]{2,1,0:T(8,128)(2,1)S(1)}, u32[]{:S(2)}, u32[]{:S(2)}) collective-permute-start(bf16[2,256,1280]{2,1,0:T(8,128)(2,1)S(1)} %slice.85), channel_id=1, source_target_pairs={{0,1},{1,0},{2,3},{3,2},{4,5},{5,4},{6,7},{7,6},{8,9},{9,8},{10,11... | collective-permute-start | bytes 3932168 | tf_op jit(solution)/shard_map/ppermute | solution.py:117
  156.7 14.2 %collective-permute-start.12 = (bf16[2,256,1280]{2,1,0:T(8,128)(2,1)S(1)}, bf16[2,256,1280]{2,1,0:T(8,128)(2,1)S(1)}, u32[]{:S(2)}, u32[]{:S(2)}) collective-permute-start(bf16[2,256,1280]{2,1,0:T(8,128)(2,1)S(1)} %copy-done.7), channel_id=1, source_target_pairs={{0,1},{1,0},{2,3},{3,2},{4,5},{5,4},{6,7},{7,6},{8,9},{9,8},{10,11... | collective-permute-start | bytes 3932168 | tf_op jit(solution)/shard_map/ppermute | solution.py:117
  157.1 14.7 %collective-permute-start.8 = (bf16[2,256,1280]{2,1,0:T(8,128)(2,1)S(1)}, bf16[2,256,1280]{2,1,0:T(8,128)(2,1)S(1)}, u32[]{:S(2)}, u32[]{:S(2)}) collective-permute-start(bf16[2,256,1280]{2,1,0:T(8,128)(2,1)S(1)} %copy-done.6), channel_id=1, source_target_pairs={{0,1},{1,0},{2,3},{3,2},{4,5},{5,4},{6,7},{7,6},{8,9},{9,8},{10,11... | collective-permute-start | bytes 3932168 | tf_op jit(solution)/shard_map/ppermute | solution.py:117
  167.1 2.7 %copy-start.3 = (bf16[4,256,1280]{2,1,0:T(8,128)(2,1)S(1)}, bf16[4,256,1280]{2,1,0:T(8,128)(2,1)}, u32[]{:S(2)}) copy-start(bf16[4,256,1280]{2,1,0:T(8,128)(2,1)} %get-tuple-element.16) | copy-start | bytes 7864324
  168.4 16.1 %collective-permute-start.11 = (bf16[256,1280]{1,0:T(8,128)(2,1)S(1)}, bf16[256,1280]{1,0:T(8,128)(2,1)S(1)}, u32[]{:S(2)}, u32[]{:S(2)}) collective-permute-start(bf16[256,1280]{1,0:T(8,128)(2,1)S(1)} %fusion.6), channel_id=1, source_target_pairs={{0,2},{2,0},{4,6},{6,4},{1,3},{3,1},{5,7},{7,5},{8,10},{10,8},{12,... | collective-permute-start | bytes 1966088 | tf_op jit(solution)/shard_map/ppermute | solution.py:117
  169.8 2.0 copy-start.2
  170.0 44.1 %collective-permute-start.7 = (bf16[256,1280]{1,0:T(8,128)(2,1)S(1)}, bf16[256,1280]{1,0:T(8,128)(2,1)S(1)}, u32[]{:S(2)}, u32[]{:S(2)}) collective-permute-start(bf16[256,1280]{1,0:T(8,128)(2,1)S(1)} %fusion.4), channel_id=1, source_target_pairs={{0,2},{2,0},{4,6},{6,4},{1,3},{3,1},{5,7},{7,5},{8,10},{10,8},{12,... | collective-permute-start | bytes 1966088 | tf_op jit(solution)/shard_map/ppermute | solution.py:117
  171.1 41.6 %collective-permute-start.13 = (bf16[256,1280]{1,0:T(8,128)(2,1)S(1)}, bf16[256,1280]{1,0:T(8,128)(2,1)S(1)}, u32[]{:S(2)}, u32[]{:S(2)}) collective-permute-start(bf16[256,1280]{1,0:T(8,128)(2,1)S(1)} %fusion.7), channel_id=1, source_target_pairs={{0,2},{2,0},{4,6},{6,4},{1,3},{3,1},{5,7},{7,5},{8,10},{10,8},{12,... | collective-permute-start | bytes 1966088 | tf_op jit(solution)/shard_map/ppermute | solution.py:117
  172.0 54.7 %collective-permute-start.9 = (bf16[256,1280]{1,0:T(8,128)(2,1)S(1)}, bf16[256,1280]{1,0:T(8,128)(2,1)S(1)}, u32[]{:S(2)}, u32[]{:S(2)}) collective-permute-start(bf16[256,1280]{1,0:T(8,128)(2,1)S(1)} %fusion.5), channel_id=1, source_target_pairs={{0,2},{2,0},{4,6},{6,4},{1,3},{3,1},{5,7},{7,5},{8,10},{10,8},{12,... | collective-permute-start | bytes 1966088 | tf_op jit(solution)/shard_map/ppermute | solution.py:117
  226.7 1.4 copy-start.1
Sparse Core Ops, SparseCore 0:
  10.7 100.3 all-gather.1

commit v4 on v3

--- a/solution.py
+++ b/solution.py
@@ -27,17 +27,21 @@
 
 
 def fwd_kernel(q_ref, k0, k1, k2, k3, v0, v1, v2, v3, mask_ref, ctx_ref, lse_ref):
-    q = q_ref[...]
-    k = jnp.concatenate([k0[...], k1[...], k2[...], k3[...]], axis=0)
-    v = jnp.concatenate([v0[...], v1[...], v2[...], v3[...]], axis=0)
-    s = masked_scores(q, k, mask_ref[...])
-    m = jnp.max(s, axis=1, keepdims=True)
-    e = jnp.exp(s - m)
-    total = jnp.sum(e, axis=1, keepdims=True)
-    lse = m + jnp.log(total)
-    p_low = (e * (1.0 / total)).astype(jnp.bfloat16)
-    ctx_ref[...] = jnp.dot(p_low, v, preferred_element_type=jnp.float32).astype(jnp.bfloat16)
-    lse_ref[...] = lse.reshape(lse_ref.shape)
+    mask = mask_ref[...]
+    for h in range(lse_ref.shape[0]):
+        cols = slice(h * HSIZE, (h + 1) * HSIZE)
+        q = q_ref[:, cols]
+        k = jnp.concatenate([k0[:, cols], k1[:, cols], k2[:, cols], k3[:, cols]], axis=0)
+        v = jnp.concatenate([v0[:, cols], v1[:, cols], v2[:, cols], v3[:, cols]], axis=0)
+        s = masked_scores(q, k, mask)
+        m = jnp.max(s, axis=1, keepdims=True)
+        e = jnp.exp(s - m)
+        total = jnp.sum(e, axis=1, keepdims=True)
+        lse = m + jnp.log(total)
+        p_low = (e * (1.0 / total)).astype(jnp.bfloat16)
+        ctx = jnp.dot(p_low, v, preferred_element_type=jnp.float32)
+        ctx_ref[:, cols] = ctx.astype(jnp.bfloat16)
+        lse_ref[h] = lse
 
 
 def bwd_kernel(q_ref, k0, k1, k2, k3, v0, v1, v2, v3, do_ref, ctx_ref, lse_ref, mask_ref,
@@ -45,40 +49,42 @@
     scaling = 1.0 / math.sqrt(HSIZE)
     nt = (((1,), (1,)), ((), ()))
     tn = (((0,), (0,)), ((), ()))
-    q = q_ref[...]
-    k = jnp.concatenate([k0[...], k1[...], k2[...], k3[...]], axis=0)
-    v = jnp.concatenate([v0[...], v1[...], v2[...], v3[...]], axis=0)
-    s = masked_scores(q, k, mask_ref[...])
-    lse = lse_ref[...].reshape(s.shape[0], 1)
-    p = jnp.exp(s - lse)
-    p_low = p.astype(jnp.bfloat16)
-    do = do_ref[...]
-    dp = lax.dot_general(do, v, nt, preferred_element_type=jnp.float32)
-    delta = jnp.sum(
-        do.astype(jnp.float32) * ctx_ref[...].astype(jnp.float32), axis=1, keepdims=True
-    )
-    ds = (p * (dp - delta)).astype(jnp.bfloat16)
-    dq = jnp.dot(ds, k, preferred_element_type=jnp.float32) * scaling
-    dq_ref[...] = dq.astype(jnp.bfloat16)
-    dk = lax.dot_general(ds, q, tn, preferred_element_type=jnp.float32) * scaling
-    dv = lax.dot_general(p_low, do, tn, preferred_element_type=jnp.float32)
-    dk_ref[...] = dk.astype(jnp.bfloat16).reshape(dk_ref.shape)
-    dv_ref[...] = dv.astype(jnp.bfloat16).reshape(dv_ref.shape)
-
-
-def attention_fwd(q, ks, vs, mask):
+    mask = mask_ref[...]
+    for h in range(lse_ref.shape[0]):
+        cols = slice(h * HSIZE, (h + 1) * HSIZE)
+        q = q_ref[:, cols]
+        k = jnp.concatenate([k0[:, cols], k1[:, cols], k2[:, cols], k3[:, cols]], axis=0)
+        v = jnp.concatenate([v0[:, cols], v1[:, cols], v2[:, cols], v3[:, cols]], axis=0)
+        s = masked_scores(q, k, mask)
+        p = jnp.exp(s - lse_ref[h])
+        p_low = p.astype(jnp.bfloat16)
+        do = do_ref[:, cols]
+        dp = lax.dot_general(do, v, nt, preferred_element_type=jnp.float32)
+        delta = jnp.sum(
+            do.astype(jnp.float32) * ctx_ref[:, cols].astype(jnp.float32), axis=1, keepdims=True
+        )
+        ds = (p * (dp - delta)).astype(jnp.bfloat16)
+        dq = jnp.dot(ds, k, preferred_element_type=jnp.float32) * scaling
+        dq_ref[:, cols] = dq.astype(jnp.bfloat16)
+        dk = lax.dot_general(ds, q, tn, preferred_element_type=jnp.float32) * scaling
+        dv = lax.dot_general(p_low, do, tn, preferred_element_type=jnp.float32)
+        dk_ref[:, :, cols] = dk.astype(jnp.bfloat16).reshape(4, -1, HSIZE)
+        dv_ref[:, :, cols] = dv.astype(jnp.bfloat16).reshape(4, -1, HSIZE)
+
+
+def attention_fwd(q, ks, vs, mask, per_step):
     rows, width = q.shape
     heads = width // HSIZE
-    col = pl.BlockSpec((rows, HSIZE), lambda h: (0, h))
+    col = pl.BlockSpec((rows, per_step * HSIZE), lambda h: (0, h))
     return pl.pallas_call(
         fwd_kernel,
-        grid=(heads,),
+        grid=(heads // per_step,),
         cost_estimate=pl.CostEstimate(
             flops=heads * 2 * 10**9, transcendentals=heads * rows * 1024,
             bytes_accessed=12 * rows * width * 2,
         ),
         in_specs=[col] * 9 + [pl.BlockSpec(mask.shape, lambda h: (0, 0))],
-        out_specs=[col, pl.BlockSpec((1, rows, 1), lambda h: (h, 0, 0))],
+        out_specs=[col, pl.BlockSpec((per_step, rows, 1), lambda h: (h, 0, 0))],
         out_shape=[
             jax.ShapeDtypeStruct((rows, width), jnp.bfloat16),
             jax.ShapeDtypeStruct((heads, rows, 1), jnp.float32),
@@ -86,21 +92,23 @@
     )(q, *ks, *vs, mask)
 
 
-def attention_bwd(q, ks, vs, do, ctx, lse, mask, first, count):
+def attention_bwd(q, ks, vs, do, ctx, lse, mask, first, count, per_step):
     rows, width = q.shape
-    col = pl.BlockSpec((rows, HSIZE), lambda h: (0, h + first))
-    out_col = pl.BlockSpec((rows, HSIZE), lambda h: (0, h))
-    slot_col = pl.BlockSpec((4, rows, HSIZE), lambda h: (0, 0, h))
+    lead = first // per_step
+    span = per_step * HSIZE
+    col = pl.BlockSpec((rows, span), lambda h: (0, h + lead))
+    out_col = pl.BlockSpec((rows, span), lambda h: (0, h))
+    slot_col = pl.BlockSpec((4, rows, span), lambda h: (0, 0, h))
     return pl.pallas_call(
         bwd_kernel,
-        grid=(count,),
+        grid=(count // per_step,),
         cost_estimate=pl.CostEstimate(
             flops=count * 14 * 10**8, transcendentals=count * rows * 1024,
             bytes_accessed=12 * rows * width,
         ),
         in_specs=[col] * 11
         + [
-            pl.BlockSpec((1, rows, 1), lambda h: (h + first, 0, 0)),
+            pl.BlockSpec((per_step, rows, 1), lambda h: (h + lead, 0, 0)),
             pl.BlockSpec(mask.shape, lambda h: (0, 0)),
         ],
         out_specs=[out_col, slot_col, slot_col],
@@ -147,32 +155,39 @@
 
     ks = (key_rows, k_x, k_p, k_d)
     vs = (value_rows, v_x, v_p, v_d)
-    ctx, lse = attention_fwd(query_rows, ks, vs, mask)
+    ctx, lse = attention_fwd(query_rows, ks, vs, mask, 4)
 
     grad_context = lax.dot_general(
         cotangent, full_weight, (((1,), (1,)), ((), ())), preferred_element_type=jnp.float32
     ).astype(jnp.bfloat16)
 
-    def reduce_parts(parts):
+    def presum(parts):
         back = swap(parts[2:4], "core")
         own = parts[0].astype(jnp.float32) + back[0].astype(jnp.float32)
         cross = (parts[1].astype(jnp.float32) + back[1].astype(jnp.float32)).astype(jnp.bfloat16)
+        return own, cross
+
+    def finish(own, cross):
         arrived = swap(cross, "y")
         return (own + arrived.astype(jnp.float32)).astype(jnp.bfloat16)
 
     heads = query_rows.shape[1] // HSIZE
     half = heads // 2
     pieces = []
+    later = (query_rows, grad_context, ctx)
     for first, count in ((0, half), (half, heads - half)):
-        dq, dk, dv = attention_bwd(
-            query_rows, ks, vs, grad_context, ctx, lse, mask, first, count
-        )
-        pieces.append((dq, reduce_parts(dk), reduce_parts(dv)))
+        q_in, do_in, ctx_in = later
+        dq, dk, dv = attention_bwd(q_in, ks, vs, do_in, ctx_in, lse, mask, first, count, 2)
+        k_own, k_cross = presum(dk)
+        v_own, v_cross = presum(dv)
+        later, k_cross, v_cross = lax.optimization_barrier((later, k_cross, v_cross))
+        pieces.append((dq, finish(k_own, k_cross), finish(v_own, v_cross)))
     grad_queries = jnp.concatenate([p[0] for p in pieces], axis=1)
     grad_keys = jnp.concatenate([p[1] for p in pieces], axis=1)
     grad_values = jnp.concatenate([p[2] for p in pieces], axis=1)
 
-    sublayer_out = jnp.dot(ctx, full_weight, preferred_element_type=jnp.float32).astype(
+    ctx_out = later[2]
+    sublayer_out = jnp.dot(ctx_out, full_weight, preferred_element_type=jnp.float32).astype(
         jnp.bfloat16
     )
     return (sublayer_out, grad_queries, grad_keys, grad_values)

time: 237 us -> 215 us (0.907)
  waiting for transfers between devices: 113 us -> 96.9 us
  Pallas kernels: 51.2 us -> 43.1 us
  other arithmetic: 6.86 us -> 11.2 us
    ppermute x14, waiting for transfers between devices: 106 us -> 85.2 us  [swap(): return lax.ppermute(x, axis, [(i, i ^ 1) for i in range(count)])]
    pallas_call x3, Pallas kernels: 51.2 us -> 43.1 us  [the longest x2 25.4 us: attention_bwd(): pl.pallas_call(bwd_kernel, grid=(count // per_step,), cost_estimate=pl.Co...]
    all_gather x1, waiting for transfers between devices: 6.48 us -> 11 us  [per_device(): lax.all_gather(weight_out, ('z', 'y', 'core'), axis=0, tiled=True)]
    convert_element_type x8, other arithmetic: 1.61 us -> 5.96 us  [the longest x4 3.88 us: presum(): (parts[1].astype(jnp.float32) + back[1].astype(jnp.float32)).astype(jnp.b...]
  transfers between devices with their start and end apart: 15 -> 15, of which waited for: 6 -> 7; matrix products, arithmetic and copies ran while one was open for 7% -> 10% of each run, Pallas kernels for 9% -> 14%
where the time goes in v4:
time: 215 us; the launch traced here: 214 us
  waiting for transfers between devices  96.9 us (45%)
  Pallas kernels  43.1 us (20%)
  starting transfers between devices  21.4 us (10%)
  matrix products  18.7 us (9%)
  between operations  14.2 us (7%)
  other arithmetic  11.2 us (5%)
  local copies, waits for them, and re-layouts  8.08 us (4%)
    ppermute x14, waiting for transfers between devices, swap(): return lax.ppermute(x, axis, [(i, i ^ 1) for i in range(count)])  85.2 us
    pallas_call x2, Pallas kernels, attention_bwd(): pl.pallas_call(bwd_kernel, grid=(count // per_step,), cost_estimate=pl.Co...  25.4 us
    ppermute x14, starting transfers between devices, swap(): return lax.ppermute(x, axis, [(i, i ^ 1) for i in range(count)])  21.4 us
    pallas_call x1, Pallas kernels, attention_fwd(): pl.pallas_call(fwd_kernel, grid=(heads // per_step,), cost_estimate=pl.Co...  17.7 us
    all_gather x1, waiting for transfers between devices, per_device(): lax.all_gather(weight_out, ('z', 'y', 'core'), axis=0, tiled=True)  11 us
    dot_general x1, matrix products, per_device(): jnp.dot(ctx_out, full_weight, preferred_element_type=jnp.float32)  9.37 us
    dot_general x1, matrix products, per_device(): lax.dot_general(cotangent, full_weight, (((1,), (1,)), ((), ())), preferr...  9.36 us
  transfers between devices with their start and end apart: 15, of which 7 were waited for; matrix products, arithmetic and copies ran while one was open for 10% of the time, Pallas kernels for 14%

profile of v4, /device:TPU:1, one launch (start us, length us, event | category | flops | bytes accessed | tf_op | source)
XLA Modules:
  0.0 213.6 jit_solution(16961516242352592389)
XLA Ops:
  7.2 0.0 copy-start
  7.2 0.0 all-gather.2.cloned.1.call-start
  7.2 0.7 all-gather.2.cloned.1.call-update
  7.9 2.2 %collective-permute-start = (bf16[256,2560]{1,0:T(8,128)(2,1)}, bf16[256,2560]{1,0:T(8,128)(2,1)S(1)}, u32[]{:S(2)}, u32[]{:S(2)}) collective-permute-start(bf16[256,2560]{1,0:T(8,128)(2,1)} %k0.5), channel_id=1, source_target_pairs={{0,2},{2,0},{4,6},{6,4},{1,3},{3,1},{5,7},{7,5},{8,10},{10,8},{12,... | collective-permute-start | bytes 3932168 | tf_op jit(solution)/shard_map/ppermute | solution.py:125
  10.1 0.1 collective-permute-start.3
  10.2 3.0 %collective-permute-start.1 = (bf16[256,2560]{1,0:T(8,128)(2,1)}, bf16[256,2560]{1,0:T(8,128)(2,1)}, u32[]{:S(2)}, u32[]{:S(2)}) collective-permute-start(bf16[256,2560]{1,0:T(8,128)(2,1)} %k0.5), channel_id=1, source_target_pairs={{0,1},{1,0},{2,3},{3,2},{4,5},{5,4},{6,7},{7,6},{8,9},{9,8},{10,11... | collective-permute-start | bytes 3932168 | tf_op jit(solution)/shard_map/ppermute | solution.py:125
  13.2 0.0 collective-permute-start.4
  13.2 27.4 %collective-permute-done.k1 = bf16[256,2560]{1,0:T(8,128)(2,1)S(1)} collective-permute-done((bf16[256,2560]{1,0:T(8,128)(2,1)}, bf16[256,2560]{1,0:T(8,128)(2,1)S(1)}, u32[]{:S(2)}, u32[]{:S(2)}) %collective-permute-start) | collective-permute-done | bytes 1310752 | tf_op jit(solution)/shard_map/ppermute | solution.py:125
  40.7 5.7 %collective-permute-start.2 = (bf16[256,2560]{1,0:T(8,128)(2,1)S(1)}, bf16[256,2560]{1,0:T(8,128)(2,1)}, u32[]{:S(2)}, u32[]{:S(2)}) collective-permute-start(bf16[256,2560]{1,0:T(8,128)(2,1)S(1)} %collective-permute-done.k1), channel_id=1, source_target_pairs={{0,1},{1,0},{2,3},{3,2},{4,5},{5,4},{6,7},{7,6},{8,9},{9,8},{10,11... | collective-permute-start | bytes 3932168 | tf_op jit(solution)/shard_map/ppermute | solution.py:125
  46.4 26.6 %collective-permute-done.3.v1 = bf16[256,2560]{1,0:T(8,128)(2,1)} collective-permute-done((bf16[256,2560]{1,0:T(8,128)(2,1)}, bf16[256,2560]{1,0:T(8,128)(2,1)}, u32[]{:S(2)}, u32[]{:S(2)}) %collective-permute-start.3) | collective-permute-done | bytes 1310752 | tf_op jit(solution)/shard_map/ppermute | solution.py:125
  73.0 5.5 %collective-permute-start.5 = (bf16[256,2560]{1,0:T(8,128)(2,1)}, bf16[256,2560]{1,0:T(8,128)(2,1)}, u32[]{:S(2)}, u32[]{:S(2)}) collective-permute-start(bf16[256,2560]{1,0:T(8,128)(2,1)} %collective-permute-done.3.v1), channel_id=1, source_target_pairs={{0,1},{1,0},{2,3},{3,2},{4,5},{5,4},{6,7},{7,6},{8,9},{9,8},{10,11... | collective-permute-start | bytes 3932168 | tf_op jit(solution)/shard_map/ppermute | solution.py:125
  78.5 0.8 constant_dynamic-slice_fusion
  79.3 0.1 copy.12
  79.4 0.7 gather_fusion
  80.2 0.5 slice_reduce_fusion.5
  80.7 1.8 or_convert_fusion.mask_ref
  82.4 0.0 collective-permute-done.1.k2
  82.4 0.0 collective-permute-done.4.v2
  82.5 0.0 collective-permute-done.2.k3
  82.5 0.0 collective-permute-done.5.v3
  82.5 17.7 %shard_map.102 = (bf16[256,2560]{1,0:T(8,128)(2,1)}, f32[20,256,1]{2,1,0:T(8,128)}) custom-call(bf16[256,2560]{1,0:T(8,128)(2,1)} %q_ref.4, bf16[256,2560]{1,0:T(8,128)(2,1)} %k0.5, bf16[256,2560]{1,0:T(8,128)(2,1)} %copy-done.12, bf16[256,2560]{1,0:T(8,128)(2,1)} %collective-permute-done.1.k2, bf16[256,2560]{1,0:T(8,128)(2,1)} %collective-permute-done.2.k3, ...), custom_call_target="tpu_custom_call" | custom-call | flops 40000000000 | bytes 15728640 | tf_op jit(solution)/shard_map/pallas_call | solution.py:79
  100.2 11.0 %all-gather.2.cloned.1.call-done = bf16[2560,2560]{1,0:T(8,128)(2,1)} async-done(((bf16[40,2560]{1,0:T(8,128)(2,1)}), bf16[2560,2560]{1,0:T(8,128)(2,1)}) %all-gather.2.cloned.1.call-update) | async-done | bytes 13107216 | tf_op jit(solution)/shard_map/all_gather | solution.py:138
  111.1 9.4 %convolution_convert_fusion.1.do_ref = bf16[256,2560]{1,0:T(8,128)(2,1)} fusion(bf16[256,2560]{1,0:T(8,128)(2,1)S(1)} %copy-done, bf16[2560,2560]{1,0:T(8,128)(2,1)} %all-gather.2.cloned.1.call-done), kind=kOutput, calls=%fused_computation.2 | convolution fusion | flops 3356098560 | bytes 15728640 | tf_op jit(solution)/shard_map/dot_general | solution.py:160
  120.5 12.8 %shard_map.103 = (bf16[256,1280]{1,0:T(8,128)(2,1)}, bf16[4,256,1280]{2,1,0:T(8,128)(2,1)}, bf16[4,256,1280]{2,1,0:T(8,128)(2,1)}) custom-call(bf16[256,2560]{1,0:T(8,128)(2,1)} %q_ref.4, bf16[256,2560]{1,0:T(8,128)(2,1)} %k0.5, bf16[256,2560]{1,0:T(8,128)(2,1)} %copy-done.12, bf16[256,2560]{1,0:T(8,128)(2,1)} %collective-permute-done.1.k2, ...), custom_call_target="tpu_custom_call" | custom-call | flops 14000000000 | bytes 7864320 | tf_op jit(solution)/shard_map/pallas_call | solution.py:102
  133.2 1.6 slice.88
  134.8 0.3 collective-permute-start.7
  135.2 0.2 copy-done.4
  135.4 0.1 slice.85
  135.5 0.3 collective-permute-start.6
  135.8 2.1 collective-permute-done.7
  137.9 2.5 %fusion.5 = bf16[256,1280]{1,0:T(8,128)(2,1)} fusion(bf16[2,256,1280]{2,1,0:T(8,128)(2,1)S(1)} %collective-permute-done.7, bf16[4,256,1280]{2,1,0:T(8,128)(2,1)} %get-tuple-element.23), kind=kLoop, calls=%fused_computation.20 | loop fusion | flops 1310720 | bytes 1966080 | tf_op jit(solution)/shard_map/convert_element_type | solution.py:167
  140.5 0.0 collective-permute-done.6
  140.5 1.1 copy-done.5
  141.5 1.0 fusion.4
  142.6 1.3 collective-permute-start.12
  143.9 12.7 %shard_map.104 = (bf16[256,1280]{1,0:T(8,128)(2,1)}, bf16[4,256,1280]{2,1,0:T(8,128)(2,1)}, bf16[4,256,1280]{2,1,0:T(8,128)(2,1)}) custom-call(bf16[256,2560]{1,0:T(8,128)(2,1)} %q_ref.4, bf16[256,2560]{1,0:T(8,128)(2,1)} %k0.5, bf16[256,2560]{1,0:T(8,128)(2,1)} %copy-done.12, bf16[256,2560]{1,0:T(8,128)(2,1)} %collective-permute-done.1.k2, ...), custom_call_target="tpu_custom_call" | custom-call | flops 14000000000 | bytes 7864320 | tf_op jit(solution)/shard_map/pallas_call | solution.py:102
  156.6 1.6 slice.94
  158.1 0.6 collective-permute-start.9
  158.7 0.1 slice.91
  158.8 0.6 collective-permute-start.8
  159.4 0.4 copy-done.11
  159.8 0.1 collective-permute-start.10
  159.9 0.1 copy-done.9
  160.0 0.2 copy-done.10
  160.2 1.1 pad_maximum_fusion
  161.3 0.0 collective-permute-done.12
  161.3 0.6 copy-done.8
  162.0 1.3 fusion.1
  163.3 12.3 %collective-permute-done.10 = bf16[256,1280]{1,0:T(8,128)(2,1)S(1)} collective-permute-done((bf16[256,1280]{1,0:T(8,128)(2,1)S(1)}, bf16[256,1280]{1,0:T(8,128)(2,1)S(1)}, u32[]{:S(2)}, u32[]{:S(2)}) %collective-permute-start.10) | collective-permute-done | bytes 655392 | tf_op jit(solution)/shard_map/ppermute | solution.py:125
  175.6 0.3 fusion.3
  175.9 0.0 collective-permute-done.9
  175.9 0.2 fusion.7
  176.1 0.0 copy-start.13
  176.1 0.2 fusion.6
  176.3 0.2 collective-permute-start.13
  176.5 1.3 collective-permute-start.11
  177.8 9.4 %convolution_convert_fusion = bf16[256,2560]{1,0:T(8,128)(2,1)} fusion(bf16[256,2560]{1,0:T(8,128)(2,1)S(1)} %copy-done.13, bf16[2560,2560]{1,0:T(8,128)(2,1)} %all-gather.2.cloned.1.call-done), kind=kOutput, calls=%fused_computation.1 | convolution fusion | flops 3356098560 | bytes 15728640 | tf_op jit(solution)/shard_map/dot_general | solution.py:190
  187.2 4.1 %collective-permute-done.13 = bf16[256,1280]{1,0:T(8,128)(2,1)S(1)} collective-permute-done((bf16[256,1280]{1,0:T(8,128)(2,1)S(1)}, bf16[256,1280]{1,0:T(8,128)(2,1)S(1)}, u32[]{:S(2)}, u32[]{:S(2)}) %collective-permute-start.13) | collective-permute-done | bytes 655392 | tf_op jit(solution)/shard_map/ppermute | solution.py:125
  191.3 0.2 fusion
  191.5 1.1 pad_maximum_fusion.2
  192.7 12.7 %collective-permute-done.11 = bf16[256,1280]{1,0:T(8,128)(2,1)S(1)} collective-permute-done((bf16[256,1280]{1,0:T(8,128)(2,1)S(1)}, bf16[256,1280]{1,0:T(8,128)(2,1)S(1)}, u32[]{:S(2)}, u32[]{:S(2)}) %collective-permute-start.11) | collective-permute-done | bytes 655392 | tf_op jit(solution)/shard_map/ppermute | solution.py:125
  205.3 0.2 fusion.2
  205.6 1.1 pad_maximum_fusion.1
  206.7 0.0 copy-done.1
  (24 shorter events, 0.1 us)
Async XLA Ops:
  7.2 103.9 %copy-start = (bf16[256,2560]{1,0:T(8,128)(2,1)S(1)}, bf16[256,2560]{1,0:T(8,128)(2,1)}, u32[]{:S(2)}) copy-start(bf16[256,2560]{1,0:T(8,128)(2,1)} %param.11) | copy-start | bytes 3932164
  7.2 103.9 %all-gather.2.cloned.1.call-start = ((), (), s32[]{:S(2)}) async-start(), calls=%async_computation | async-start | bytes 13312000 | tf_op jit(solution)/shard_map/all_gather | solution.py:138
  7.9 32.7 %collective-permute-start = (bf16[256,2560]{1,0:T(8,128)(2,1)}, bf16[256,2560]{1,0:T(8,128)(2,1)S(1)}, u32[]{:S(2)}, u32[]{:S(2)}) collective-permute-start(bf16[256,2560]{1,0:T(8,128)(2,1)} %k0.5), channel_id=1, source_target_pairs={{0,2},{2,0},{4,6},{6,4},{1,3},{3,1},{5,7},{7,5},{8,10},{10,8},{12,... | collective-permute-start | bytes 3932168 | tf_op jit(solution)/shard_map/ppermute | solution.py:125
  10.1 62.9 %collective-permute-start.3 = (bf16[256,2560]{1,0:T(8,128)(2,1)}, bf16[256,2560]{1,0:T(8,128)(2,1)}, u32[]{:S(2)}, u32[]{:S(2)}) collective-permute-start(bf16[256,2560]{1,0:T(8,128)(2,1)} %v0.5), channel_id=1, source_target_pairs={{0,2},{2,0},{4,6},{6,4},{1,3},{3,1},{5,7},{7,5},{8,10},{10,8},{12,... | collective-permute-start | bytes 3932168 | tf_op jit(solution)/shard_map/ppermute | solution.py:125
  10.2 72.2 %collective-permute-start.1 = (bf16[256,2560]{1,0:T(8,128)(2,1)}, bf16[256,2560]{1,0:T(8,128)(2,1)}, u32[]{:S(2)}, u32[]{:S(2)}) collective-permute-start(bf16[256,2560]{1,0:T(8,128)(2,1)} %k0.5), channel_id=1, source_target_pairs={{0,1},{1,0},{2,3},{3,2},{4,5},{5,4},{6,7},{7,6},{8,9},{9,8},{10,11... | collective-permute-start | bytes 3932168 | tf_op jit(solution)/shard_map/ppermute | solution.py:125
  13.2 69.2 %collective-permute-start.4 = (bf16[256,2560]{1,0:T(8,128)(2,1)}, bf16[256,2560]{1,0:T(8,128)(2,1)}, u32[]{:S(2)}, u32[]{:S(2)}) collective-permute-start(bf16[256,2560]{1,0:T(8,128)(2,1)} %v0.5), channel_id=1, source_target_pairs={{0,1},{1,0},{2,3},{3,2},{4,5},{5,4},{6,7},{7,6},{8,9},{9,8},{10,11... | collective-permute-start | bytes 3932168 | tf_op jit(solution)/shard_map/ppermute | solution.py:125
  40.7 41.8 %copy-start.12 = (bf16[256,2560]{1,0:T(8,128)(2,1)}, bf16[256,2560]{1,0:T(8,128)(2,1)S(1)}, u32[]{:S(2)}) copy-start(bf16[256,2560]{1,0:T(8,128)(2,1)S(1)} %collective-permute-done.k1) | copy-start | bytes 3932164
  40.7 41.8 %collective-permute-start.2 = (bf16[256,2560]{1,0:T(8,128)(2,1)S(1)}, bf16[256,2560]{1,0:T(8,128)(2,1)}, u32[]{:S(2)}, u32[]{:S(2)}) collective-permute-start(bf16[256,2560]{1,0:T(8,128)(2,1)S(1)} %collective-permute-done.k1), channel_id=1, source_target_pairs={{0,1},{1,0},{2,3},{3,2},{4,5},{5,4},{6,7},{7,6},{8,9},{9,8},{10,11... | collective-permute-start | bytes 3932168 | tf_op jit(solution)/shard_map/ppermute | solution.py:125
  73.0 9.5 %collective-permute-start.5 = (bf16[256,2560]{1,0:T(8,128)(2,1)}, bf16[256,2560]{1,0:T(8,128)(2,1)}, u32[]{:S(2)}, u32[]{:S(2)}) collective-permute-start(bf16[256,2560]{1,0:T(8,128)(2,1)} %collective-permute-done.3.v1), channel_id=1, source_target_pairs={{0,1},{1,0},{2,3},{3,2},{4,5},{5,4},{6,7},{7,6},{8,9},{9,8},{10,11... | collective-permute-start | bytes 3932168 | tf_op jit(solution)/shard_map/ppermute | solution.py:125
  133.2 2.1 copy-start.4
  134.8 3.1 %collective-permute-start.7 = (bf16[2,256,1280]{2,1,0:T(8,128)(2,1)S(1)}, bf16[2,256,1280]{2,1,0:T(8,128)(2,1)S(1)}, u32[]{:S(2)}, u32[]{:S(2)}) collective-permute-start(bf16[2,256,1280]{2,1,0:T(8,128)(2,1)S(1)} %slice.88), channel_id=1, source_target_pairs={{0,1},{1,0},{2,3},{3,2},{4,5},{5,4},{6,7},{7,6},{8,9},{9,8},{10,11... | collective-permute-start | bytes 3932168 | tf_op jit(solution)/shard_map/ppermute | solution.py:125
  135.5 5.0 %collective-permute-start.6 = (bf16[2,256,1280]{2,1,0:T(8,128)(2,1)S(1)}, bf16[2,256,1280]{2,1,0:T(8,128)(2,1)S(1)}, u32[]{:S(2)}, u32[]{:S(2)}) collective-permute-start(bf16[2,256,1280]{2,1,0:T(8,128)(2,1)S(1)} %slice.85), channel_id=1, source_target_pairs={{0,1},{1,0},{2,3},{3,2},{4,5},{5,4},{6,7},{7,6},{8,9},{9,8},{10,11... | collective-permute-start | bytes 3932168 | tf_op jit(solution)/shard_map/ppermute | solution.py:125
  137.9 4.6 %copy-start.7 = (bf16[2,256,1280]{2,1,0:T(8,128)(2,1)}, bf16[2,256,1280]{2,1,0:T(8,128)(2,1)S(1)}, u32[]{:S(2)}) copy-start(bf16[2,256,1280]{2,1,0:T(8,128)(2,1)S(1)} %collective-permute-done.7) | copy-start | bytes 3932164
  140.5 1.1 copy-start.5
  142.6 18.8 %collective-permute-start.12 = (bf16[256,1280]{1,0:T(8,128)(2,1)}, bf16[256,1280]{1,0:T(8,128)(2,1)S(1)}, u32[]{:S(2)}, u32[]{:S(2)}) collective-permute-start(bf16[256,1280]{1,0:T(8,128)(2,1)} %fusion.5), channel_id=1, source_target_pairs={{0,2},{2,0},{4,6},{6,4},{1,3},{3,1},{5,7},{7,5},{8,10},{10,8},{12,... | collective-permute-start | bytes 1966088 | tf_op jit(solution)/shard_map/ppermute | solution.py:125
  156.5 2.2 %copy-start.2 = (bf16[4,256,1280]{2,1,0:T(8,128)(2,1)S(1)}, bf16[4,256,1280]{2,1,0:T(8,128)(2,1)}, u32[]{:S(2)}) copy-start(bf16[4,256,1280]{2,1,0:T(8,128)(2,1)} %get-tuple-element.27) | copy-start | bytes 7864324
  158.1 17.8 %collective-permute-start.9 = (bf16[2,256,1280]{2,1,0:T(8,128)(2,1)S(1)}, bf16[2,256,1280]{2,1,0:T(8,128)(2,1)S(1)}, u32[]{:S(2)}, u32[]{:S(2)}) collective-permute-start(bf16[2,256,1280]{2,1,0:T(8,128)(2,1)S(1)} %slice.94), channel_id=1, source_target_pairs={{0,1},{1,0},{2,3},{3,2},{4,5},{5,4},{6,7},{7,6},{8,9},{9,8},{10,11... | collective-permute-start | bytes 3932168 | tf_op jit(solution)/shard_map/ppermute | solution.py:125
  158.7 1.1 copy-start.11
  158.7 1.3 copy-start.9
  158.7 1.5 copy-start.10
  158.8 17.3 %collective-permute-start.8 = (bf16[2,256,1280]{2,1,0:T(8,128)(2,1)S(1)}, bf16[2,256,1280]{2,1,0:T(8,128)(2,1)S(1)}, u32[]{:S(2)}, u32[]{:S(2)}) collective-permute-start(bf16[2,256,1280]{2,1,0:T(8,128)(2,1)S(1)} %slice.91), channel_id=1, source_target_pairs={{0,1},{1,0},{2,3},{3,2},{4,5},{5,4},{6,7},{7,6},{8,9},{9,8},{10,11... | collective-permute-start | bytes 3932168 | tf_op jit(solution)/shard_map/ppermute | solution.py:125
  159.8 15.8 %collective-permute-start.10 = (bf16[256,1280]{1,0:T(8,128)(2,1)S(1)}, bf16[256,1280]{1,0:T(8,128)(2,1)S(1)}, u32[]{:S(2)}, u32[]{:S(2)}) collective-permute-start(bf16[256,1280]{1,0:T(8,128)(2,1)S(1)} %copy-done.11), channel_id=1, source_target_pairs={{0,2},{2,0},{4,6},{6,4},{1,3},{3,1},{5,7},{7,5},{8,10},{10,8},{12,... | collective-permute-start | bytes 1966088 | tf_op jit(solution)/shard_map/ppermute | solution.py:125
  160.2 1.8 copy-start.8
  161.3 14.3 %copy-start.6 = (bf16[2,256,1280]{2,1,0:T(8,128)(2,1)S(1)}, bf16[2,256,1280]{2,1,0:T(8,128)(2,1)}, u32[]{:S(2)}) copy-start(bf16[2,256,1280]{2,1,0:T(8,128)(2,1)} %copy-done.5) | copy-start | bytes 3932164
  163.3 12.6 %copy-start.3 = (bf16[4,256,1280]{2,1,0:T(8,128)(2,1)S(1)}, bf16[4,256,1280]{2,1,0:T(8,128)(2,1)}, u32[]{:S(2)}) copy-start(bf16[4,256,1280]{2,1,0:T(8,128)(2,1)} %get-tuple-element.28) | copy-start | bytes 7864324
  176.1 1.7 copy-start.13
  176.3 15.0 %collective-permute-start.13 = (bf16[256,1280]{1,0:T(8,128)(2,1)S(1)}, bf16[256,1280]{1,0:T(8,128)(2,1)S(1)}, u32[]{:S(2)}, u32[]{:S(2)}) collective-permute-start(bf16[256,1280]{1,0:T(8,128)(2,1)S(1)} %fusion.7), channel_id=1, source_target_pairs={{0,2},{2,0},{4,6},{6,4},{1,3},{3,1},{5,7},{7,5},{8,10},{10,8},{12,... | collective-permute-start | bytes 1966088 | tf_op jit(solution)/shard_map/ppermute | solution.py:125
  176.5 28.9 %collective-permute-start.11 = (bf16[256,1280]{1,0:T(8,128)(2,1)S(1)}, bf16[256,1280]{1,0:T(8,128)(2,1)S(1)}, u32[]{:S(2)}, u32[]{:S(2)}) collective-permute-start(bf16[256,1280]{1,0:T(8,128)(2,1)S(1)} %fusion.6), channel_id=1, source_target_pairs={{0,2},{2,0},{4,6},{6,4},{1,3},{3,1},{5,7},{7,5},{8,10},{10,8},{12,... | collective-permute-start | bytes 1966088 | tf_op jit(solution)/shard_map/ppermute | solution.py:125
  205.3 1.4 copy-start.1
Sparse Core Ops, SparseCore 0:
  10.7 100.3 all-gather.1

commit v5 on v4

--- a/solution.py
+++ b/solution.py
@@ -45,7 +45,7 @@
 
 
 def bwd_kernel(q_ref, k0, k1, k2, k3, v0, v1, v2, v3, do_ref, ctx_ref, lse_ref, mask_ref,
-               dq_ref, dk_ref, dv_ref):
+               dq_ref, dkv_ref):
     scaling = 1.0 / math.sqrt(HSIZE)
     nt = (((1,), (1,)), ((), ()))
     tn = (((0,), (0,)), ((), ()))
@@ -68,8 +68,8 @@
         dq_ref[:, cols] = dq.astype(jnp.bfloat16)
         dk = lax.dot_general(ds, q, tn, preferred_element_type=jnp.float32) * scaling
         dv = lax.dot_general(p_low, do, tn, preferred_element_type=jnp.float32)
-        dk_ref[:, :, cols] = dk.astype(jnp.bfloat16).reshape(4, -1, HSIZE)
-        dv_ref[:, :, cols] = dv.astype(jnp.bfloat16).reshape(4, -1, HSIZE)
+        dkv_ref[:, 0, :, cols] = dk.astype(jnp.bfloat16).reshape(4, -1, HSIZE)
+        dkv_ref[:, 1, :, cols] = dv.astype(jnp.bfloat16).reshape(4, -1, HSIZE)
 
 
 def attention_fwd(q, ks, vs, mask, per_step):
@@ -98,7 +98,7 @@
     span = per_step * HSIZE
     col = pl.BlockSpec((rows, span), lambda h: (0, h + lead))
     out_col = pl.BlockSpec((rows, span), lambda h: (0, h))
-    slot_col = pl.BlockSpec((4, rows, span), lambda h: (0, 0, h))
+    slot_col = pl.BlockSpec((4, 2, rows, span), lambda h: (0, 0, 0, h))
     return pl.pallas_call(
         bwd_kernel,
         grid=(count // per_step,),
@@ -111,11 +111,10 @@
             pl.BlockSpec((per_step, rows, 1), lambda h: (h + lead, 0, 0)),
             pl.BlockSpec(mask.shape, lambda h: (0, 0)),
         ],
-        out_specs=[out_col, slot_col, slot_col],
+        out_specs=[out_col, slot_col],
         out_shape=[
             jax.ShapeDtypeStruct((rows, count * HSIZE), jnp.bfloat16),
-            jax.ShapeDtypeStruct((4, rows, count * HSIZE), jnp.bfloat16),
-            jax.ShapeDtypeStruct((4, rows, count * HSIZE), jnp.bfloat16),
+            jax.ShapeDtypeStruct((4, 2, rows, count * HSIZE), jnp.bfloat16),
         ],
     )(q, *ks, *vs, do, ctx, lse, mask)
 
@@ -173,18 +172,22 @@
 
     heads = query_rows.shape[1] // HSIZE
     half = heads // 2
-    pieces = []
     later = (query_rows, grad_context, ctx)
-    for first, count in ((0, half), (half, heads - half)):
-        q_in, do_in, ctx_in = later
-        dq, dk, dv = attention_bwd(q_in, ks, vs, do_in, ctx_in, lse, mask, first, count, 2)
-        k_own, k_cross = presum(dk)
-        v_own, v_cross = presum(dv)
-        later, k_cross, v_cross = lax.optimization_barrier((later, k_cross, v_cross))
-        pieces.append((dq, finish(k_own, k_cross), finish(v_own, v_cross)))
-    grad_queries = jnp.concatenate([p[0] for p in pieces], axis=1)
-    grad_keys = jnp.concatenate([p[1] for p in pieces], axis=1)
-    grad_values = jnp.concatenate([p[2] for p in pieces], axis=1)
+    q_in, do_in, ctx_in = later
+    dq_a, dkv_a = attention_bwd(q_in, ks, vs, do_in, ctx_in, lse, mask, 0, half, 2)
+    own_a, cross_a = presum(dkv_a)
+    later, cross_a = lax.optimization_barrier((later, cross_a))
+    arrived_a = swap(cross_a, "y")
+    q_in, do_in, ctx_in = later
+    dq_b, dkv_b = attention_bwd(q_in, ks, vs, do_in, ctx_in, lse, mask, half, heads - half, 2)
+    dkv_b, arrived_a = lax.optimization_barrier((dkv_b, arrived_a))
+    res_a = (own_a + arrived_a.astype(jnp.float32)).astype(jnp.bfloat16)
+    own_b, cross_b = presum(dkv_b)
+    later, cross_b = lax.optimization_barrier((later, cross_b))
+    res_b = finish(own_b, cross_b)
+    grad_queries = jnp.concatenate([dq_a, dq_b], axis=1)
+    grad_keys = jnp.concatenate([res_a[0], res_b[0]], axis=1)
+    grad_values = jnp.concatenate([res_a[1], res_b[1]], axis=1)
 
     ctx_out = later[2]
     sublayer_out = jnp.dot(ctx_out, full_weight, preferred_element_type=jnp.float32).astype(

time: 215 us -> 221 us (1.028)
  waiting for transfers between devices: 96.9 us -> 106 us
    ppermute x14 -> x10, waiting for transfers between devices: 85.2 us -> 94.4 us  [swap(): return lax.ppermute(x, axis, [(i, i ^ 1) for i in range(count)])]
    unnamed x28 -> x18, local copies, waits for them, and re-layouts: 2.69 us -> 0.09 us
    ppermute x14 -> x10, starting transfers between devices: 21.4 us -> 21.1 us  [swap(): return lax.ppermute(x, axis, [(i, i ^ 1) for i in range(count)])]
  transfers between devices with their start and end apart: 15 -> 11, of which waited for: 7 -> 7; matrix products, arithmetic and copies ran while one was open for 10% -> 8% of each run, Pallas kernels for 14% -> 14%
where the time goes in v5:
time: 221 us
  waiting for transfers between devices  106 us (48%)
  Pallas kernels  43.1 us (20%)
  starting transfers between devices  21.2 us (10%)
  matrix products  18.7 us (8%)
  between operations  14.2 us (6%)
  other arithmetic  11.1 us (5%)
  local copies, waits for them, and re-layouts  6.35 us (3%)
    ppermute x10, waiting for transfers between devices, swap(): return lax.ppermute(x, axis, [(i, i ^ 1) for i in range(count)])  94.4 us
    pallas_call x2, Pallas kernels, attention_bwd(): pl.pallas_call(bwd_kernel, grid=(count // per_step,), cost_estimate=pl.Co...  25.4 us
    ppermute x10, starting transfers between devices, swap(): return lax.ppermute(x, axis, [(i, i ^ 1) for i in range(count)])  21.1 us
    pallas_call x1, Pallas kernels, attention_fwd(): pl.pallas_call(fwd_kernel, grid=(heads // per_step,), cost_estimate=pl.Co...  17.7 us
    all_gather x1, waiting for transfers between devices, per_device(): lax.all_gather(weight_out, ('z', 'y', 'core'), axis=0, tiled=True)  11 us
    dot_general x1, matrix products, per_device(): jnp.dot(ctx_out, full_weight, preferred_element_type=jnp.float32)  9.37 us
    dot_general x1, matrix products, per_device(): lax.dot_general(cotangent, full_weight, (((1,), (1,)), ((), ())), preferr...  9.36 us
  transfers between devices with their start and end apart: 11, of which 7 were waited for; matrix products, arithmetic and copies ran while one was open for 8% of the time, Pallas kernels for 14%

profile of v5, /device:TPU:1, one launch (start us, length us, event | category | flops | bytes accessed | tf_op | source)
XLA Modules:
  0.0 220.6 jit_solution(7249900908036359680)
XLA Ops:
  7.2 0.0 copy-start
  7.2 0.0 all-gather.2.cloned.1.call-start
  7.2 0.7 all-gather.2.cloned.1.call-update
  7.9 2.2 collective-permute-start
  10.1 0.1 collective-permute-start.3
  10.2 3.0 %collective-permute-start.1 = (bf16[256,2560]{1,0:T(8,128)(2,1)}, bf16[256,2560]{1,0:T(8,128)(2,1)}, u32[]{:S(2)}, u32[]{:S(2)}) collective-permute-start(bf16[256,2560]{1,0:T(8,128)(2,1)} %k0.5), channel_id=1, source_target_pairs={{0,1},{1,0},{2,3},{3,2},{4,5},{5,4},{6,7},{7,6},{8,9},{9,8},{10,11... | collective-permute-start | bytes 3932168 | tf_op jit(solution)/shard_map/ppermute | solution.py:124
  13.2 0.0 collective-permute-start.4
  13.2 27.4 %collective-permute-done.k1 = bf16[256,2560]{1,0:T(8,128)(2,1)S(1)} collective-permute-done((bf16[256,2560]{1,0:T(8,128)(2,1)}, bf16[256,2560]{1,0:T(8,128)(2,1)S(1)}, u32[]{:S(2)}, u32[]{:S(2)}) %collective-permute-start) | collective-permute-done | bytes 1310752 | tf_op jit(solution)/shard_map/ppermute | solution.py:124
  40.7 0.0 copy-start.5
  40.7 5.7 %collective-permute-start.2 = (bf16[256,2560]{1,0:T(8,128)(2,1)S(1)}, bf16[256,2560]{1,0:T(8,128)(2,1)}, u32[]{:S(2)}, u32[]{:S(2)}) collective-permute-start(bf16[256,2560]{1,0:T(8,128)(2,1)S(1)} %collective-permute-done.k1), channel_id=1, source_target_pairs={{0,1},{1,0},{2,3},{3,2},{4,5},{5,4},{6,7},{7,6},{8,9},{9,8},{10,11... | collective-permute-start | bytes 3932168 | tf_op jit(solution)/shard_map/ppermute | solution.py:124
  46.4 26.6 %collective-permute-done.3.v1 = bf16[256,2560]{1,0:T(8,128)(2,1)} collective-permute-done((bf16[256,2560]{1,0:T(8,128)(2,1)}, bf16[256,2560]{1,0:T(8,128)(2,1)}, u32[]{:S(2)}, u32[]{:S(2)}) %collective-permute-start.3) | collective-permute-done | bytes 1310752 | tf_op jit(solution)/shard_map/ppermute | solution.py:124
  73.0 5.5 %collective-permute-start.5 = (bf16[256,2560]{1,0:T(8,128)(2,1)}, bf16[256,2560]{1,0:T(8,128)(2,1)}, u32[]{:S(2)}, u32[]{:S(2)}) collective-permute-start(bf16[256,2560]{1,0:T(8,128)(2,1)} %collective-permute-done.3.v1), channel_id=1, source_target_pairs={{0,1},{1,0},{2,3},{3,2},{4,5},{5,4},{6,7},{7,6},{8,9},{9,8},{10,11... | collective-permute-start | bytes 3932168 | tf_op jit(solution)/shard_map/ppermute | solution.py:124
  78.5 0.8 constant_dynamic-slice_fusion
  79.3 0.1 copy.12
  79.4 0.7 gather_fusion
  80.2 0.5 slice_reduce_fusion.5
  80.7 1.8 or_convert_fusion.mask_ref
  82.4 0.0 copy-done.5
  82.4 0.0 collective-permute-done.1.k2
  82.4 0.0 collective-permute-done.4.v2
  82.4 0.0 collective-permute-done.2.k3
  82.4 0.0 collective-permute-done.5.v3
  82.5 17.7 %shard_map.102 = (bf16[256,2560]{1,0:T(8,128)(2,1)}, f32[20,256,1]{2,1,0:T(8,128)}) custom-call(bf16[256,2560]{1,0:T(8,128)(2,1)} %q_ref.4, bf16[256,2560]{1,0:T(8,128)(2,1)} %k0.5, bf16[256,2560]{1,0:T(8,128)(2,1)} %copy-done.5, bf16[256,2560]{1,0:T(8,128)(2,1)} %collective-permute-done.1.k2, bf16[256,2560]{1,0:T(8,128)(2,1)} %collective-permute-done.2.k3, ...), custom_call_target="tpu_custom_call" | custom-call | flops 40000000000 | bytes 15728640 | tf_op jit(solution)/shard_map/pallas_call | solution.py:79
  100.1 11.0 %all-gather.2.cloned.1.call-done = bf16[2560,2560]{1,0:T(8,128)(2,1)} async-done(((bf16[40,2560]{1,0:T(8,128)(2,1)}), bf16[2560,2560]{1,0:T(8,128)(2,1)}) %all-gather.2.cloned.1.call-update) | async-done | bytes 13107216 | tf_op jit(solution)/shard_map/all_gather | solution.py:137
  111.1 0.0 copy-done
  111.1 9.4 %convolution_convert_fusion.1.do_ref = bf16[256,2560]{1,0:T(8,128)(2,1)} fusion(bf16[256,2560]{1,0:T(8,128)(2,1)S(1)} %copy-done, bf16[2560,2560]{1,0:T(8,128)(2,1)} %all-gather.2.cloned.1.call-done), kind=kOutput, calls=%fused_computation.2 | convolution fusion | flops 3356098560 | bytes 15728640 | tf_op jit(solution)/shard_map/dot_general | solution.py:159
  120.5 12.8 %shard_map.103 = (bf16[256,1280]{1,0:T(8,128)(2,1)}, bf16[4,2,256,1280]{3,2,1,0:T(8,128)(2,1)}) custom-call(bf16[256,2560]{1,0:T(8,128)(2,1)} %q_ref.4, bf16[256,2560]{1,0:T(8,128)(2,1)} %k0.5, bf16[256,2560]{1,0:T(8,128)(2,1)} %copy-done.5, bf16[256,2560]{1,0:T(8,128)(2,1)} %collective-permute-done.1.k2, bf16[256,2560]{1,0:T(8,128)(2,1)} %collective-permute-done.2.k3, ...), custom_call_target="tpu_custom_call" | custom-call | flops 14000000000 | bytes 7864320 | tf_op jit(solution)/shard_map/pallas_call | solution.py:102
  133.2 1.9 slice.67
  135.2 0.3 collective-permute-start.6
  135.5 4.6 %collective-permute-done.6 = bf16[2,2,256,1280]{3,2,1,0:T(8,128)(2,1)S(1)} collective-permute-done((bf16[2,2,256,1280]{3,2,1,0:T(8,128)(2,1)S(1)}, bf16[2,2,256,1280]{3,2,1,0:T(8,128)(2,1)S(1)}, u32[]{:S(2)}, u32[]{:S(2)}) %collective-permute-start.6) | collective-permute-done | bytes 2621472 | tf_op jit(solution)/shard_map/ppermute | solution.py:124
  140.2 0.0 copy-start.2
  140.2 2.6 %fusion.2 = bf16[2,256,1280]{2,1,0:T(8,128)(2,1)S(1)} fusion(bf16[2,2,256,1280]{3,2,1,0:T(8,128)(2,1)S(1)} %collective-permute-done.6, bf16[4,2,256,1280]{3,2,1,0:T(8,128)(2,1)} %get-tuple-element.20), kind=kLoop, calls=%fused_computation.9 | loop fusion | flops 2621440 | bytes 3932160 | tf_op jit(solution)/shard_map/convert_element_type | solution.py:166
  142.8 0.0 copy-done.2
  142.8 1.6 collective-permute-start.7
  144.4 0.0 copy-start.4
  144.4 12.6 %shard_map.104 = (bf16[256,1280]{1,0:T(8,128)(2,1)}, bf16[4,2,256,1280]{3,2,1,0:T(8,128)(2,1)}) custom-call(bf16[256,2560]{1,0:T(8,128)(2,1)} %q_ref.4, bf16[256,2560]{1,0:T(8,128)(2,1)} %k0.5, bf16[256,2560]{1,0:T(8,128)(2,1)} %copy-done.5, bf16[256,2560]{1,0:T(8,128)(2,1)} %collective-permute-done.1.k2, bf16[256,2560]{1,0:T(8,128)(2,1)} %collective-permute-done.2.k3, ...), custom_call_target="tpu_custom_call" | custom-call | flops 14000000000 | bytes 7864320 | tf_op jit(solution)/shard_map/pallas_call | solution.py:102
  157.0 16.1 %collective-permute-done.7 = bf16[2,256,1280]{2,1,0:T(8,128)(2,1)S(1)} collective-permute-done((bf16[2,256,1280]{2,1,0:T(8,128)(2,1)S(1)}, bf16[2,256,1280]{2,1,0:T(8,128)(2,1)S(1)}, u32[]{:S(2)}, u32[]{:S(2)}) %collective-permute-start.7) | collective-permute-done | bytes 1310752 | tf_op jit(solution)/shard_map/ppermute | solution.py:124
  173.2 0.0 copy-start.3
  173.2 0.0 slice-start
  173.2 2.1 slice.70
  175.2 1.2 collective-permute-start.8
  176.4 0.0 copy-done.4
  176.4 0.0 slice-start.1
  176.4 2.3 %pad_maximum_fusion = bf16[256,2560]{1,0:T(8,128)(2,1)} fusion(bf16[256,1280]{1,0:T(8,128)(2,1)} %get-tuple-element.29, bf16[256,1280]{1,0:T(8,128)(2,1)S(1)} %copy-done.4), kind=kLoop, calls=%fused_computation.11 | loop fusion | flops 2621440 | bytes 2621440 | tf_op jit(solution)/shard_map/concatenate | solution.py:188
  178.8 0.0 copy-done.3
  178.8 1.8 fusion.1
  180.6 0.4 collective-permute-done.8
  181.0 0.0 slice-done
  181.0 0.0 slice-done.1
  181.0 0.3 fusion.3
  181.3 0.0 copy-start.6
  181.3 1.4 collective-permute-start.9
  182.7 0.1 slice_bitcast_fusion.1
  182.8 0.0 copy-done.6
  182.8 9.4 %convolution_convert_fusion = bf16[256,2560]{1,0:T(8,128)(2,1)} fusion(bf16[256,2560]{1,0:T(8,128)(2,1)S(1)} %copy-done.6, bf16[2560,2560]{1,0:T(8,128)(2,1)} %all-gather.2.cloned.1.call-done), kind=kOutput, calls=%fused_computation.1 | convolution fusion | flops 3356098560 | bytes 15728640 | tf_op jit(solution)/shard_map/dot_general | solution.py:193
  192.2 19.2 %collective-permute-done.9 = bf16[2,256,1280]{2,1,0:T(8,128)(2,1)S(1)} collective-permute-done((bf16[2,256,1280]{2,1,0:T(8,128)(2,1)S(1)}, bf16[2,256,1280]{2,1,0:T(8,128)(2,1)S(1)}, u32[]{:S(2)}, u32[]{:S(2)}) %collective-permute-start.9) | collective-permute-done | bytes 1310752 | tf_op jit(solution)/shard_map/ppermute | solution.py:124
  211.3 0.5 fusion
  211.9 0.1 slice_bitcast_fusion
  212.0 0.0 copy-start.1
  212.0 1.7 pad_maximum_fusion.1
  213.7 0.0 copy-done.1
  (5 shorter events, 0.0 us)
Async XLA Ops:
  7.2 103.9 %copy-start = (bf16[256,2560]{1,0:T(8,128)(2,1)S(1)}, bf16[256,2560]{1,0:T(8,128)(2,1)}, u32[]{:S(2)}) copy-start(bf16[256,2560]{1,0:T(8,128)(2,1)} %param.11) | copy-start | bytes 3932164
  7.2 103.9 %all-gather.2.cloned.1.call-start = ((), (), s32[]{:S(2)}) async-start(), calls=%async_computation | async-start | bytes 13312000 | tf_op jit(solution)/shard_map/all_gather | solution.py:137
  7.9 32.7 %collective-permute-start = (bf16[256,2560]{1,0:T(8,128)(2,1)}, bf16[256,2560]{1,0:T(8,128)(2,1)S(1)}, u32[]{:S(2)}, u32[]{:S(2)}) collective-permute-start(bf16[256,2560]{1,0:T(8,128)(2,1)} %k0.5), channel_id=1, source_target_pairs={{0,2},{2,0},{4,6},{6,4},{1,3},{3,1},{5,7},{7,5},{8,10},{10,8},{12,... | collective-permute-start | bytes 3932168 | tf_op jit(solution)/shard_map/ppermute | solution.py:124
  10.1 62.9 %collective-permute-start.3 = (bf16[256,2560]{1,0:T(8,128)(2,1)}, bf16[256,2560]{1,0:T(8,128)(2,1)}, u32[]{:S(2)}, u32[]{:S(2)}) collective-permute-start(bf16[256,2560]{1,0:T(8,128)(2,1)} %v0.5), channel_id=1, source_target_pairs={{0,2},{2,0},{4,6},{6,4},{1,3},{3,1},{5,7},{7,5},{8,10},{10,8},{12,... | collective-permute-start | bytes 3932168 | tf_op jit(solution)/shard_map/ppermute | solution.py:124
  10.2 72.2 %collective-permute-start.1 = (bf16[256,2560]{1,0:T(8,128)(2,1)}, bf16[256,2560]{1,0:T(8,128)(2,1)}, u32[]{:S(2)}, u32[]{:S(2)}) collective-permute-start(bf16[256,2560]{1,0:T(8,128)(2,1)} %k0.5), channel_id=1, source_target_pairs={{0,1},{1,0},{2,3},{3,2},{4,5},{5,4},{6,7},{7,6},{8,9},{9,8},{10,11... | collective-permute-start | bytes 3932168 | tf_op jit(solution)/shard_map/ppermute | solution.py:124
  13.2 69.2 %collective-permute-start.4 = (bf16[256,2560]{1,0:T(8,128)(2,1)}, bf16[256,2560]{1,0:T(8,128)(2,1)}, u32[]{:S(2)}, u32[]{:S(2)}) collective-permute-start(bf16[256,2560]{1,0:T(8,128)(2,1)} %v0.5), channel_id=1, source_target_pairs={{0,1},{1,0},{2,3},{3,2},{4,5},{5,4},{6,7},{7,6},{8,9},{9,8},{10,11... | collective-permute-start | bytes 3932168 | tf_op jit(solution)/shard_map/ppermute | solution.py:124
  40.7 41.8 %copy-start.5 = (bf16[256,2560]{1,0:T(8,128)(2,1)}, bf16[256,2560]{1,0:T(8,128)(2,1)S(1)}, u32[]{:S(2)}) copy-start(bf16[256,2560]{1,0:T(8,128)(2,1)S(1)} %collective-permute-done.k1) | copy-start | bytes 3932164
  40.7 41.8 %collective-permute-start.2 = (bf16[256,2560]{1,0:T(8,128)(2,1)S(1)}, bf16[256,2560]{1,0:T(8,128)(2,1)}, u32[]{:S(2)}, u32[]{:S(2)}) collective-permute-start(bf16[256,2560]{1,0:T(8,128)(2,1)S(1)} %collective-permute-done.k1), channel_id=1, source_target_pairs={{0,1},{1,0},{2,3},{3,2},{4,5},{5,4},{6,7},{7,6},{8,9},{9,8},{10,11... | collective-permute-start | bytes 3932168 | tf_op jit(solution)/shard_map/ppermute | solution.py:124
  73.0 9.5 %collective-permute-start.5 = (bf16[256,2560]{1,0:T(8,128)(2,1)}, bf16[256,2560]{1,0:T(8,128)(2,1)}, u32[]{:S(2)}, u32[]{:S(2)}) collective-permute-start(bf16[256,2560]{1,0:T(8,128)(2,1)} %collective-permute-done.3.v1), channel_id=1, source_target_pairs={{0,1},{1,0},{2,3},{3,2},{4,5},{5,4},{6,7},{7,6},{8,9},{9,8},{10,11... | collective-permute-start | bytes 3932168 | tf_op jit(solution)/shard_map/ppermute | solution.py:124
  135.2 5.0 %collective-permute-start.6 = (bf16[2,2,256,1280]{3,2,1,0:T(8,128)(2,1)S(1)}, bf16[2,2,256,1280]{3,2,1,0:T(8,128)(2,1)S(1)}, u32[]{:S(2)}, u32[]{:S(2)}) collective-permute-start(bf16[2,2,256,1280]{3,2,1,0:T(8,128)(2,1)S(1)} %slice.67), channel_id=1, source_target_pairs={{0,1},{1,0},{2,3},{3,2},{4,5},{5,4},{6,7},{7,6},{8,9},{9,8},{10,11... | collective-permute-start | bytes 7864328 | tf_op jit(solution)/shard_map/ppermute | solution.py:124
  140.2 2.6 %copy-start.2 = (bf16[2,2,256,1280]{3,2,1,0:T(8,128)(2,1)}, bf16[2,2,256,1280]{3,2,1,0:T(8,128)(2,1)S(1)}, u32[]{:S(2)}) copy-start(bf16[2,2,256,1280]{3,2,1,0:T(8,128)(2,1)S(1)} %collective-permute-done.6) | copy-start | bytes 7864324
  142.8 30.4 %collective-permute-start.7 = (bf16[2,256,1280]{2,1,0:T(8,128)(2,1)S(1)}, bf16[2,256,1280]{2,1,0:T(8,128)(2,1)S(1)}, u32[]{:S(2)}, u32[]{:S(2)}) collective-permute-start(bf16[2,256,1280]{2,1,0:T(8,128)(2,1)S(1)} %fusion.2), channel_id=1, source_target_pairs={{0,2},{2,0},{4,6},{6,4},{1,3},{3,1},{5,7},{7,5},{8,10},{10,8},{12,... | collective-permute-start | bytes 3932168 | tf_op jit(solution)/shard_map/ppermute | solution.py:124
  144.4 32.0 %copy-start.4 = (bf16[256,1280]{1,0:T(8,128)(2,1)S(1)}, bf16[256,1280]{1,0:T(8,128)(2,1)}, u32[]{:S(2)}) copy-start(bf16[256,1280]{1,0:T(8,128)(2,1)} %get-tuple-element.28) | copy-start | bytes 1966084
  173.2 5.6 %copy-start.3 = (bf16[2,2,256,1280]{3,2,1,0:T(8,128)(2,1)S(1)}, bf16[2,2,256,1280]{3,2,1,0:T(8,128)(2,1)}, u32[]{:S(2)}) copy-start(bf16[2,2,256,1280]{3,2,1,0:T(8,128)(2,1)} %copy-done.2) | copy-start | bytes 7864324
  173.2 7.8 %slice-start = ((s8[5242880]{0:T(1024)(128)(4,1)}), s8[4194304]{0:T(1024)(128)(4,1)S(1)}, s32[]{:S(2)}) async-start(s8[5242880]{0:T(1024)(128)(4,1)} %bitcast.28), calls=%async_computation.1 | async-start | bytes 8388608
  175.2 5.7 %collective-permute-start.8 = (bf16[2,2,256,1280]{3,2,1,0:T(8,128)(2,1)S(1)}, bf16[2,2,256,1280]{3,2,1,0:T(8,128)(2,1)S(1)}, u32[]{:S(2)}, u32[]{:S(2)}) collective-permute-start(bf16[2,2,256,1280]{3,2,1,0:T(8,128)(2,1)S(1)} %slice.70), channel_id=1, source_target_pairs={{0,1},{1,0},{2,3},{3,2},{4,5},{5,4},{6,7},{7,6},{8,9},{9,8},{10,11... | collective-permute-start | bytes 7864328 | tf_op jit(solution)/shard_map/ppermute | solution.py:124
  176.4 4.5 %slice-start.1 = ((s8[5242880]{0:T(1024)(128)(4,1)}), s8[1048576]{0:T(1024)(128)(4,1)S(1)}, s32[]{:S(2)}) async-start(s8[5242880]{0:T(1024)(128)(4,1)} %bitcast.28), calls=%async_computation.2 | async-start | bytes 2097152
  181.3 1.5 copy-start.6
  181.3 30.1 %collective-permute-start.9 = (bf16[2,256,1280]{2,1,0:T(8,128)(2,1)S(1)}, bf16[2,256,1280]{2,1,0:T(8,128)(2,1)S(1)}, u32[]{:S(2)}, u32[]{:S(2)}) collective-permute-start(bf16[2,256,1280]{2,1,0:T(8,128)(2,1)S(1)} %fusion.3), channel_id=1, source_target_pairs={{0,2},{2,0},{4,6},{6,4},{1,3},{3,1},{5,7},{7,5},{8,10},{10,8},{12,... | collective-permute-start | bytes 3932168 | tf_op jit(solution)/shard_map/ppermute | solution.py:124
  212.0 1.7 copy-start.1
Sparse Core Ops, SparseCore 0:
  10.7 100.3 all-gather.1

commit v6 on v4

--- a/solution.py
+++ b/solution.py
@@ -106,7 +106,8 @@
             flops=count * 14 * 10**8, transcendentals=count * rows * 1024,
             bytes_accessed=12 * rows * width,
         ),
-        in_specs=[col] * 11
+        in_specs=[col] * 9
+        + [out_col, col]
         + [
             pl.BlockSpec((per_step, rows, 1), lambda h: (h + lead, 0, 0)),
             pl.BlockSpec(mask.shape, lambda h: (0, 0)),
@@ -157,9 +158,6 @@
     vs = (value_rows, v_x, v_p, v_d)
     ctx, lse = attention_fwd(query_rows, ks, vs, mask, 4)
 
-    grad_context = lax.dot_general(
-        cotangent, full_weight, (((1,), (1,)), ((), ())), preferred_element_type=jnp.float32
-    ).astype(jnp.bfloat16)
 
     def presum(parts):
         back = swap(parts[2:4], "core")
@@ -174,10 +172,14 @@
     heads = query_rows.shape[1] // HSIZE
     half = heads // 2
     pieces = []
-    later = (query_rows, grad_context, ctx)
+    later = (query_rows, ctx)
     for first, count in ((0, half), (half, heads - half)):
-        q_in, do_in, ctx_in = later
-        dq, dk, dv = attention_bwd(q_in, ks, vs, do_in, ctx_in, lse, mask, first, count, 2)
+        q_in, ctx_in = later
+        w_rows = lax.slice_in_dim(full_weight, first * HSIZE, (first + count) * HSIZE, axis=0)
+        do_part = lax.dot_general(
+            cotangent, w_rows, (((1,), (1,)), ((), ())), preferred_element_type=jnp.float32
+        ).astype(jnp.bfloat16)
+        dq, dk, dv = attention_bwd(q_in, ks, vs, do_part, ctx_in, lse, mask, first, count, 2)
         k_own, k_cross = presum(dk)
         v_own, v_cross = presum(dv)
         later, k_cross, v_cross = lax.optimization_barrier((later, k_cross, v_cross))
@@ -186,7 +188,7 @@
     grad_keys = jnp.concatenate([p[1] for p in pieces], axis=1)
     grad_values = jnp.concatenate([p[2] for p in pieces], axis=1)
 
-    ctx_out = later[2]
+    ctx_out = later[1]
     sublayer_out = jnp.dot(ctx_out, full_weight, preferred_element_type=jnp.float32).astype(
         jnp.bfloat16
     )

time: 215 us -> 215 us (level)
    dot_general x1 -> x2, matrix products: 9.36 us -> 11.2 us  [per_device(): lax.dot_general(cotangent, w_rows, (((1,), (1,)), ((), ())), preferred_el...]
  transfers between devices with their start and end apart: 15 -> 15, of which waited for: 7 -> 6; matrix products, arithmetic and copies ran while one was open for 10% -> 13% of each run, Pallas kernels for 14% -> 14%
where the time goes in v6:
time: 215 us; the launch traced here: 214 us
  waiting for transfers between devices  94.8 us (44%)
  Pallas kernels  43.1 us (20%)
  starting transfers between devices  21.6 us (10%)
  matrix products  20.6 us (10%)
  between operations  14.2 us (7%)
  other arithmetic  12.3 us (6%)
  local copies, waits for them, and re-layouts  6.97 us (3%)
    ppermute x14, waiting for transfers between devices, swap(): return lax.ppermute(x, axis, [(i, i ^ 1) for i in range(count)])  83.1 us
    pallas_call x2, Pallas kernels, attention_bwd(): pl.pallas_call(bwd_kernel, grid=(count // per_step,), cost_estimate=pl.Co...  25.5 us
    ppermute x14, starting transfers between devices, swap(): return lax.ppermute(x, axis, [(i, i ^ 1) for i in range(count)])  21.6 us
    pallas_call x1, Pallas kernels, attention_fwd(): pl.pallas_call(fwd_kernel, grid=(heads // per_step,), cost_estimate=pl.Co...  17.6 us
    dot_general x2, matrix products, per_device(): lax.dot_general(cotangent, w_rows, (((1,), (1,)), ((), ())), preferred_el...  11.2 us
    all_gather x1, waiting for transfers between devices, per_device(): lax.all_gather(weight_out, ('z', 'y', 'core'), axis=0, tiled=True)  11 us
    dot_general x1, matrix products, per_device(): jnp.dot(ctx_out, full_weight, preferred_element_type=jnp.float32)  9.37 us
  transfers between devices with their start and end apart: 15, of which 6 were waited for; matrix products, arithmetic and copies ran while one was open for 13% of the time, Pallas kernels for 14%

profile of v6, /device:TPU:1, one launch (start us, length us, event | category | flops | bytes accessed | tf_op | source)
XLA Modules:
  0.0 213.6 jit_solution(11501888140846698404)
XLA Ops:
  7.2 0.0 copy-start
  7.2 0.0 all-gather.2.cloned.1.call-start
  7.2 0.7 all-gather.2.cloned.1.call-update
  7.9 2.2 %collective-permute-start = (bf16[256,2560]{1,0:T(8,128)(2,1)}, bf16[256,2560]{1,0:T(8,128)(2,1)S(1)}, u32[]{:S(2)}, u32[]{:S(2)}) collective-permute-start(bf16[256,2560]{1,0:T(8,128)(2,1)} %k0.5), channel_id=1, source_target_pairs={{0,2},{2,0},{4,6},{6,4},{1,3},{3,1},{5,7},{7,5},{8,10},{10,8},{12,... | collective-permute-start | bytes 3932168 | tf_op jit(solution)/shard_map/ppermute | solution.py:126
  10.1 0.1 collective-permute-start.3
  10.2 3.0 %collective-permute-start.1 = (bf16[256,2560]{1,0:T(8,128)(2,1)}, bf16[256,2560]{1,0:T(8,128)(2,1)}, u32[]{:S(2)}, u32[]{:S(2)}) collective-permute-start(bf16[256,2560]{1,0:T(8,128)(2,1)} %k0.5), channel_id=1, source_target_pairs={{0,1},{1,0},{2,3},{3,2},{4,5},{5,4},{6,7},{7,6},{8,9},{9,8},{10,11... | collective-permute-start | bytes 3932168 | tf_op jit(solution)/shard_map/ppermute | solution.py:126
  13.2 0.0 collective-permute-start.4
  13.2 27.4 %collective-permute-done.k1 = bf16[256,2560]{1,0:T(8,128)(2,1)S(1)} collective-permute-done((bf16[256,2560]{1,0:T(8,128)(2,1)}, bf16[256,2560]{1,0:T(8,128)(2,1)S(1)}, u32[]{:S(2)}, u32[]{:S(2)}) %collective-permute-start) | collective-permute-done | bytes 1310752 | tf_op jit(solution)/shard_map/ppermute | solution.py:126
  40.7 5.7 %collective-permute-start.2 = (bf16[256,2560]{1,0:T(8,128)(2,1)S(1)}, bf16[256,2560]{1,0:T(8,128)(2,1)}, u32[]{:S(2)}, u32[]{:S(2)}) collective-permute-start(bf16[256,2560]{1,0:T(8,128)(2,1)S(1)} %collective-permute-done.k1), channel_id=1, source_target_pairs={{0,1},{1,0},{2,3},{3,2},{4,5},{5,4},{6,7},{7,6},{8,9},{9,8},{10,11... | collective-permute-start | bytes 3932168 | tf_op jit(solution)/shard_map/ppermute | solution.py:126
  46.4 26.6 %collective-permute-done.3.v1 = bf16[256,2560]{1,0:T(8,128)(2,1)} collective-permute-done((bf16[256,2560]{1,0:T(8,128)(2,1)}, bf16[256,2560]{1,0:T(8,128)(2,1)}, u32[]{:S(2)}, u32[]{:S(2)}) %collective-permute-start.3) | collective-permute-done | bytes 1310752 | tf_op jit(solution)/shard_map/ppermute | solution.py:126
  73.0 5.5 %collective-permute-start.5 = (bf16[256,2560]{1,0:T(8,128)(2,1)}, bf16[256,2560]{1,0:T(8,128)(2,1)}, u32[]{:S(2)}, u32[]{:S(2)}) collective-permute-start(bf16[256,2560]{1,0:T(8,128)(2,1)} %collective-permute-done.3.v1), channel_id=1, source_target_pairs={{0,1},{1,0},{2,3},{3,2},{4,5},{5,4},{6,7},{7,6},{8,9},{9,8},{10,11... | collective-permute-start | bytes 3932168 | tf_op jit(solution)/shard_map/ppermute | solution.py:126
  78.5 0.8 constant_dynamic-slice_fusion
  79.3 0.1 copy.12
  79.4 0.7 gather_fusion
  80.2 0.5 slice_reduce_fusion.5
  80.7 1.8 or_convert_fusion.mask_ref
  82.4 0.0 collective-permute-done.1.k2
  82.4 0.0 collective-permute-done.4.v2
  82.4 0.0 collective-permute-done.2.k3
  82.4 0.0 collective-permute-done.5.v3
  82.5 17.6 %shard_map.102 = (bf16[256,2560]{1,0:T(8,128)(2,1)}, f32[20,256,1]{2,1,0:T(8,128)}) custom-call(bf16[256,2560]{1,0:T(8,128)(2,1)} %q_ref.4, bf16[256,2560]{1,0:T(8,128)(2,1)} %k0.5, bf16[256,2560]{1,0:T(8,128)(2,1)} %copy-done.9, bf16[256,2560]{1,0:T(8,128)(2,1)} %collective-permute-done.1.k2, bf16[256,2560]{1,0:T(8,128)(2,1)} %collective-permute-done.2.k3, ...), custom_call_target="tpu_custom_call" | custom-call | flops 40000000000 | bytes 15728640 | tf_op jit(solution)/shard_map/pallas_call | solution.py:79
  100.1 11.0 %all-gather.2.cloned.1.call-done = bf16[2560,2560]{1,0:T(8,128)(2,1)} async-done(((bf16[40,2560]{1,0:T(8,128)(2,1)}), bf16[2560,2560]{1,0:T(8,128)(2,1)}) %all-gather.2.cloned.1.call-update) | async-done | bytes 13107216 | tf_op jit(solution)/shard_map/all_gather | solution.py:139
  111.1 5.6 %fusion.4.do_ref = bf16[256,1280]{1,0:T(8,128)(2,1)} fusion(bf16[256,2560]{1,0:T(8,128)(2,1)S(1)} %copy-done, bf16[2560,2560]{1,0:T(8,128)(2,1)} %all-gather.2.cloned.1.call-done), kind=kOutput, calls=%fused_computation.6 | convolution fusion | flops 1678049280 | bytes 8519680 | tf_op jit(solution)/shard_map/dot_general | solution.py:179
  116.7 12.8 %shard_map.103 = (bf16[256,1280]{1,0:T(8,128)(2,1)}, bf16[4,256,1280]{2,1,0:T(8,128)(2,1)}, bf16[4,256,1280]{2,1,0:T(8,128)(2,1)}) custom-call(bf16[256,2560]{1,0:T(8,128)(2,1)} %q_ref.4, bf16[256,2560]{1,0:T(8,128)(2,1)} %k0.5, bf16[256,2560]{1,0:T(8,128)(2,1)} %copy-done.9, bf16[256,2560]{1,0:T(8,128)(2,1)} %collective-permute-done.1.k2, ...), custom_call_target="tpu_custom_call" | custom-call | flops 14000000000 | bytes 7864320 | tf_op jit(solution)/shard_map/pallas_call | solution.py:102
  129.5 1.6 slice.95
  131.1 0.3 collective-permute-start.7
  131.4 0.2 copy-done.2
  131.7 0.1 slice.92
  131.7 0.5 collective-permute-start.6
  132.3 5.6 %fusion.7.do_ref = bf16[256,1280]{1,0:T(8,128)(2,1)} fusion(bf16[256,2560]{1,0:T(8,128)(2,1)S(1)} %copy-done, bf16[2560,2560]{1,0:T(8,128)(2,1)} %all-gather.2.cloned.1.call-done), kind=kOutput, calls=%fused_computation.7 | convolution fusion | flops 1678049280 | bytes 8519680 | tf_op jit(solution)/shard_map/dot_general | solution.py:179
  137.9 0.0 collective-permute-done.7
  137.9 2.6 %fusion.15 = bf16[256,1280]{1,0:T(8,128)(2,1)} fusion(bf16[2,256,1280]{2,1,0:T(8,128)(2,1)S(1)} %collective-permute-done.7, bf16[4,256,1280]{2,1,0:T(8,128)(2,1)} %get-tuple-element.22), kind=kLoop, calls=%fused_computation.25 | loop fusion | flops 1310720 | bytes 1966080 | tf_op jit(solution)/shard_map/convert_element_type | solution.py:165
  140.4 0.0 collective-permute-done.6
  140.4 1.0 fusion.14
  141.5 1.3 collective-permute-start.12
  142.8 12.7 %shard_map.104 = (bf16[256,1280]{1,0:T(8,128)(2,1)}, bf16[4,256,1280]{2,1,0:T(8,128)(2,1)}, bf16[4,256,1280]{2,1,0:T(8,128)(2,1)}) custom-call(bf16[256,2560]{1,0:T(8,128)(2,1)} %q_ref.4, bf16[256,2560]{1,0:T(8,128)(2,1)} %k0.5, bf16[256,2560]{1,0:T(8,128)(2,1)} %copy-done.9, bf16[256,2560]{1,0:T(8,128)(2,1)} %collective-permute-done.1.k2, ...), custom_call_target="tpu_custom_call" | custom-call | flops 14000000000 | bytes 7864320 | tf_op jit(solution)/shard_map/pallas_call | solution.py:102
  155.5 1.6 slice.102
  157.0 0.6 collective-permute-start.9
  157.6 0.1 slice.99
  157.7 0.6 collective-permute-start.8
  158.3 0.4 copy-done.8
  158.7 0.1 collective-permute-start.10
  158.9 0.1 copy-done.6
  158.9 0.2 copy-done.7
  159.1 1.1 pad_maximum_fusion
  160.3 0.0 collective-permute-done.12
  160.3 0.6 copy-done.5
  160.9 1.3 fusion.11
  162.3 12.3 %collective-permute-done.10 = bf16[256,1280]{1,0:T(8,128)(2,1)S(1)} collective-permute-done((bf16[256,1280]{1,0:T(8,128)(2,1)S(1)}, bf16[256,1280]{1,0:T(8,128)(2,1)S(1)}, u32[]{:S(2)}, u32[]{:S(2)}) %collective-permute-start.10) | collective-permute-done | bytes 655392 | tf_op jit(solution)/shard_map/ppermute | solution.py:126
  174.5 1.4 fusion.13
  175.9 0.0 collective-permute-done.9
  175.9 0.2 fusion.17
  176.1 0.0 copy-start.10
  176.1 0.0 collective-permute-done.8
  176.1 0.2 fusion.16
  176.3 0.2 collective-permute-start.13
  176.5 1.3 collective-permute-start.11
  177.8 9.4 %convolution_convert_fusion = bf16[256,2560]{1,0:T(8,128)(2,1)} fusion(bf16[256,2560]{1,0:T(8,128)(2,1)S(1)} %copy-done.10, bf16[2560,2560]{1,0:T(8,128)(2,1)} %all-gather.2.cloned.1.call-done), kind=kOutput, calls=%fused_computation.5 | convolution fusion | flops 3356098560 | bytes 15728640 | tf_op jit(solution)/shard_map/dot_general | solution.py:192
  187.2 4.1 %collective-permute-done.13 = bf16[256,1280]{1,0:T(8,128)(2,1)S(1)} collective-permute-done((bf16[256,1280]{1,0:T(8,128)(2,1)S(1)}, bf16[256,1280]{1,0:T(8,128)(2,1)S(1)}, u32[]{:S(2)}, u32[]{:S(2)}) %collective-permute-start.13) | collective-permute-done | bytes 655392 | tf_op jit(solution)/shard_map/ppermute | solution.py:126
  191.3 0.2 fusion.10
  191.5 1.1 pad_maximum_fusion.2
  192.7 12.7 %collective-permute-done.11 = bf16[256,1280]{1,0:T(8,128)(2,1)S(1)} collective-permute-done((bf16[256,1280]{1,0:T(8,128)(2,1)S(1)}, bf16[256,1280]{1,0:T(8,128)(2,1)S(1)}, u32[]{:S(2)}, u32[]{:S(2)}) %collective-permute-start.11) | collective-permute-done | bytes 655392 | tf_op jit(solution)/shard_map/ppermute | solution.py:126
  205.3 0.2 fusion.12
  205.6 1.1 pad_maximum_fusion.1
  (19 shorter events, 0.1 us)
Async XLA Ops:
  7.2 103.9 %copy-start = (bf16[256,2560]{1,0:T(8,128)(2,1)S(1)}, bf16[256,2560]{1,0:T(8,128)(2,1)}, u32[]{:S(2)}) copy-start(bf16[256,2560]{1,0:T(8,128)(2,1)} %param.11) | copy-start | bytes 3932164
  7.2 103.9 %all-gather.2.cloned.1.call-start = ((), (), s32[]{:S(2)}) async-start(), calls=%async_computation | async-start | bytes 13312000 | tf_op jit(solution)/shard_map/all_gather | solution.py:139
  7.9 32.7 %collective-permute-start = (bf16[256,2560]{1,0:T(8,128)(2,1)}, bf16[256,2560]{1,0:T(8,128)(2,1)S(1)}, u32[]{:S(2)}, u32[]{:S(2)}) collective-permute-start(bf16[256,2560]{1,0:T(8,128)(2,1)} %k0.5), channel_id=1, source_target_pairs={{0,2},{2,0},{4,6},{6,4},{1,3},{3,1},{5,7},{7,5},{8,10},{10,8},{12,... | collective-permute-start | bytes 3932168 | tf_op jit(solution)/shard_map/ppermute | solution.py:126
  10.1 62.9 %collective-permute-start.3 = (bf16[256,2560]{1,0:T(8,128)(2,1)}, bf16[256,2560]{1,0:T(8,128)(2,1)}, u32[]{:S(2)}, u32[]{:S(2)}) collective-permute-start(bf16[256,2560]{1,0:T(8,128)(2,1)} %v0.5), channel_id=1, source_target_pairs={{0,2},{2,0},{4,6},{6,4},{1,3},{3,1},{5,7},{7,5},{8,10},{10,8},{12,... | collective-permute-start | bytes 3932168 | tf_op jit(solution)/shard_map/ppermute | solution.py:126
  10.2 72.2 %collective-permute-start.1 = (bf16[256,2560]{1,0:T(8,128)(2,1)}, bf16[256,2560]{1,0:T(8,128)(2,1)}, u32[]{:S(2)}, u32[]{:S(2)}) collective-permute-start(bf16[256,2560]{1,0:T(8,128)(2,1)} %k0.5), channel_id=1, source_target_pairs={{0,1},{1,0},{2,3},{3,2},{4,5},{5,4},{6,7},{7,6},{8,9},{9,8},{10,11... | collective-permute-start | bytes 3932168 | tf_op jit(solution)/shard_map/ppermute | solution.py:126
  13.2 69.2 %collective-permute-start.4 = (bf16[256,2560]{1,0:T(8,128)(2,1)}, bf16[256,2560]{1,0:T(8,128)(2,1)}, u32[]{:S(2)}, u32[]{:S(2)}) collective-permute-start(bf16[256,2560]{1,0:T(8,128)(2,1)} %v0.5), channel_id=1, source_target_pairs={{0,1},{1,0},{2,3},{3,2},{4,5},{5,4},{6,7},{7,6},{8,9},{9,8},{10,11... | collective-permute-start | bytes 3932168 | tf_op jit(solution)/shard_map/ppermute | solution.py:126
  40.7 41.8 %copy-start.9 = (bf16[256,2560]{1,0:T(8,128)(2,1)}, bf16[256,2560]{1,0:T(8,128)(2,1)S(1)}, u32[]{:S(2)}) copy-start(bf16[256,2560]{1,0:T(8,128)(2,1)S(1)} %collective-permute-done.k1) | copy-start | bytes 3932164
  40.7 41.8 %collective-permute-start.2 = (bf16[256,2560]{1,0:T(8,128)(2,1)S(1)}, bf16[256,2560]{1,0:T(8,128)(2,1)}, u32[]{:S(2)}, u32[]{:S(2)}) collective-permute-start(bf16[256,2560]{1,0:T(8,128)(2,1)S(1)} %collective-permute-done.k1), channel_id=1, source_target_pairs={{0,1},{1,0},{2,3},{3,2},{4,5},{5,4},{6,7},{7,6},{8,9},{9,8},{10,11... | collective-permute-start | bytes 3932168 | tf_op jit(solution)/shard_map/ppermute | solution.py:126
  73.0 9.5 %collective-permute-start.5 = (bf16[256,2560]{1,0:T(8,128)(2,1)}, bf16[256,2560]{1,0:T(8,128)(2,1)}, u32[]{:S(2)}, u32[]{:S(2)}) collective-permute-start(bf16[256,2560]{1,0:T(8,128)(2,1)} %collective-permute-done.3.v1), channel_id=1, source_target_pairs={{0,1},{1,0},{2,3},{3,2},{4,5},{5,4},{6,7},{7,6},{8,9},{9,8},{10,11... | collective-permute-start | bytes 3932168 | tf_op jit(solution)/shard_map/ppermute | solution.py:126
  129.5 2.1 copy-start.2
  131.1 6.8 %collective-permute-start.7 = (bf16[2,256,1280]{2,1,0:T(8,128)(2,1)S(1)}, bf16[2,256,1280]{2,1,0:T(8,128)(2,1)S(1)}, u32[]{:S(2)}, u32[]{:S(2)}) collective-permute-start(bf16[2,256,1280]{2,1,0:T(8,128)(2,1)S(1)} %slice.95), channel_id=1, source_target_pairs={{0,1},{1,0},{2,3},{3,2},{4,5},{5,4},{6,7},{7,6},{8,9},{9,8},{10,11... | collective-permute-start | bytes 3932168 | tf_op jit(solution)/shard_map/ppermute | solution.py:126
  131.7 8.7 %collective-permute-start.6 = (bf16[2,256,1280]{2,1,0:T(8,128)(2,1)S(1)}, bf16[2,256,1280]{2,1,0:T(8,128)(2,1)S(1)}, u32[]{:S(2)}, u32[]{:S(2)}) collective-permute-start(bf16[2,256,1280]{2,1,0:T(8,128)(2,1)S(1)} %slice.92), channel_id=1, source_target_pairs={{0,1},{1,0},{2,3},{3,2},{4,5},{5,4},{6,7},{7,6},{8,9},{9,8},{10,11... | collective-permute-start | bytes 3932168 | tf_op jit(solution)/shard_map/ppermute | solution.py:126
  137.9 3.6 %copy-start.4 = (bf16[2,256,1280]{2,1,0:T(8,128)(2,1)}, bf16[2,256,1280]{2,1,0:T(8,128)(2,1)S(1)}, u32[]{:S(2)}) copy-start(bf16[2,256,1280]{2,1,0:T(8,128)(2,1)S(1)} %collective-permute-done.7) | copy-start | bytes 3932164
  141.5 18.8 %collective-permute-start.12 = (bf16[256,1280]{1,0:T(8,128)(2,1)}, bf16[256,1280]{1,0:T(8,128)(2,1)S(1)}, u32[]{:S(2)}, u32[]{:S(2)}) collective-permute-start(bf16[256,1280]{1,0:T(8,128)(2,1)} %fusion.15), channel_id=1, source_target_pairs={{0,2},{2,0},{4,6},{6,4},{1,3},{3,1},{5,7},{7,5},{8,10},{10,8},{12,... | collective-permute-start | bytes 1966088 | tf_op jit(solution)/shard_map/ppermute | solution.py:126
  155.5 2.2 %copy-start.1 = (bf16[4,256,1280]{2,1,0:T(8,128)(2,1)S(1)}, bf16[4,256,1280]{2,1,0:T(8,128)(2,1)}, u32[]{:S(2)}) copy-start(bf16[4,256,1280]{2,1,0:T(8,128)(2,1)} %get-tuple-element.25) | copy-start | bytes 7864324
  157.0 18.9 %collective-permute-start.9 = (bf16[2,256,1280]{2,1,0:T(8,128)(2,1)S(1)}, bf16[2,256,1280]{2,1,0:T(8,128)(2,1)S(1)}, u32[]{:S(2)}, u32[]{:S(2)}) collective-permute-start(bf16[2,256,1280]{2,1,0:T(8,128)(2,1)S(1)} %slice.102), channel_id=1, source_target_pairs={{0,1},{1,0},{2,3},{3,2},{4,5},{5,4},{6,7},{7,6},{8,9},{9,8},{10,11... | collective-permute-start | bytes 3932168 | tf_op jit(solution)/shard_map/ppermute | solution.py:126
  157.6 1.1 copy-start.8
  157.6 1.3 copy-start.6
  157.6 1.5 copy-start.7
  157.7 18.4 %collective-permute-start.8 = (bf16[2,256,1280]{2,1,0:T(8,128)(2,1)S(1)}, bf16[2,256,1280]{2,1,0:T(8,128)(2,1)S(1)}, u32[]{:S(2)}, u32[]{:S(2)}) collective-permute-start(bf16[2,256,1280]{2,1,0:T(8,128)(2,1)S(1)} %slice.99), channel_id=1, source_target_pairs={{0,1},{1,0},{2,3},{3,2},{4,5},{5,4},{6,7},{7,6},{8,9},{9,8},{10,11... | collective-permute-start | bytes 3932168 | tf_op jit(solution)/shard_map/ppermute | solution.py:126
  158.7 15.8 %collective-permute-start.10 = (bf16[256,1280]{1,0:T(8,128)(2,1)S(1)}, bf16[256,1280]{1,0:T(8,128)(2,1)S(1)}, u32[]{:S(2)}, u32[]{:S(2)}) collective-permute-start(bf16[256,1280]{1,0:T(8,128)(2,1)S(1)} %copy-done.8), channel_id=1, source_target_pairs={{0,2},{2,0},{4,6},{6,4},{1,3},{3,1},{5,7},{7,5},{8,10},{10,8},{12,... | collective-permute-start | bytes 1966088 | tf_op jit(solution)/shard_map/ppermute | solution.py:126
  159.1 1.8 copy-start.5
  162.2 13.7 %copy-start.3 = (bf16[4,256,1280]{2,1,0:T(8,128)(2,1)S(1)}, bf16[4,256,1280]{2,1,0:T(8,128)(2,1)}, u32[]{:S(2)}) copy-start(bf16[4,256,1280]{2,1,0:T(8,128)(2,1)} %get-tuple-element.26) | copy-start | bytes 7864324
  176.1 1.7 copy-start.10
  176.3 15.0 %collective-permute-start.13 = (bf16[256,1280]{1,0:T(8,128)(2,1)S(1)}, bf16[256,1280]{1,0:T(8,128)(2,1)S(1)}, u32[]{:S(2)}, u32[]{:S(2)}) collective-permute-start(bf16[256,1280]{1,0:T(8,128)(2,1)S(1)} %fusion.17), channel_id=1, source_target_pairs={{0,2},{2,0},{4,6},{6,4},{1,3},{3,1},{5,7},{7,5},{8,10},{10,8},{12,... | collective-permute-start | bytes 1966088 | tf_op jit(solution)/shard_map/ppermute | solution.py:126
  176.5 28.9 %collective-permute-start.11 = (bf16[256,1280]{1,0:T(8,128)(2,1)S(1)}, bf16[256,1280]{1,0:T(8,128)(2,1)S(1)}, u32[]{:S(2)}, u32[]{:S(2)}) collective-permute-start(bf16[256,1280]{1,0:T(8,128)(2,1)S(1)} %fusion.16), channel_id=1, source_target_pairs={{0,2},{2,0},{4,6},{6,4},{1,3},{3,1},{5,7},{7,5},{8,10},{10,8},{12,... | collective-permute-start | bytes 1966088 | tf_op jit(solution)/shard_map/ppermute | solution.py:126
Sparse Core Ops, SparseCore 0:
  10.7 100.3 all-gather.1

commit v7 on v6

--- a/solution.py
+++ b/solution.py
@@ -45,7 +45,7 @@
 
 
 def bwd_kernel(q_ref, k0, k1, k2, k3, v0, v1, v2, v3, do_ref, ctx_ref, lse_ref, mask_ref,
-               dq_ref, dk_ref, dv_ref):
+               dq_ref, dk_keep, dk_send, dv_keep, dv_send):
     scaling = 1.0 / math.sqrt(HSIZE)
     nt = (((1,), (1,)), ((), ()))
     tn = (((0,), (0,)), ((), ()))
@@ -68,8 +68,12 @@
         dq_ref[:, cols] = dq.astype(jnp.bfloat16)
         dk = lax.dot_general(ds, q, tn, preferred_element_type=jnp.float32) * scaling
         dv = lax.dot_general(p_low, do, tn, preferred_element_type=jnp.float32)
-        dk_ref[:, :, cols] = dk.astype(jnp.bfloat16).reshape(4, -1, HSIZE)
-        dv_ref[:, :, cols] = dv.astype(jnp.bfloat16).reshape(4, -1, HSIZE)
+        dk = dk.astype(jnp.bfloat16).reshape(4, -1, HSIZE)
+        dv = dv.astype(jnp.bfloat16).reshape(4, -1, HSIZE)
+        dk_keep[:, :, cols] = dk[0:2]
+        dk_send[:, :, cols] = dk[2:4]
+        dv_keep[:, :, cols] = dv[0:2]
+        dv_send[:, :, cols] = dv[2:4]
 
 
 def attention_fwd(q, ks, vs, mask, per_step):
@@ -98,7 +102,7 @@
     span = per_step * HSIZE
     col = pl.BlockSpec((rows, span), lambda h: (0, h + lead))
     out_col = pl.BlockSpec((rows, span), lambda h: (0, h))
-    slot_col = pl.BlockSpec((4, rows, span), lambda h: (0, 0, h))
+    slot_col = pl.BlockSpec((2, rows, span), lambda h: (0, 0, h))
     return pl.pallas_call(
         bwd_kernel,
         grid=(count // per_step,),
@@ -112,12 +116,9 @@
             pl.BlockSpec((per_step, rows, 1), lambda h: (h + lead, 0, 0)),
             pl.BlockSpec(mask.shape, lambda h: (0, 0)),
         ],
-        out_specs=[out_col, slot_col, slot_col],
-        out_shape=[
-            jax.ShapeDtypeStruct((rows, count * HSIZE), jnp.bfloat16),
-            jax.ShapeDtypeStruct((4, rows, count * HSIZE), jnp.bfloat16),
-            jax.ShapeDtypeStruct((4, rows, count * HSIZE), jnp.bfloat16),
-        ],
+        out_specs=[out_col] + [slot_col] * 4,
+        out_shape=[jax.ShapeDtypeStruct((rows, count * HSIZE), jnp.bfloat16)]
+        + [jax.ShapeDtypeStruct((2, rows, count * HSIZE), jnp.bfloat16)] * 4,
     )(q, *ks, *vs, do, ctx, lse, mask)
 
 
@@ -159,10 +160,10 @@
     ctx, lse = attention_fwd(query_rows, ks, vs, mask, 4)
 
 
-    def presum(parts):
-        back = swap(parts[2:4], "core")
-        own = parts[0].astype(jnp.float32) + back[0].astype(jnp.float32)
-        cross = (parts[1].astype(jnp.float32) + back[1].astype(jnp.float32)).astype(jnp.bfloat16)
+    def presum(keep, send):
+        back = swap(send, "core")
+        own = keep[0].astype(jnp.float32) + back[0].astype(jnp.float32)
+        cross = (keep[1].astype(jnp.float32) + back[1].astype(jnp.float32)).astype(jnp.bfloat16)
         return own, cross
 
     def finish(own, cross):
@@ -179,9 +180,11 @@
         do_part = lax.dot_general(
             cotangent, w_rows, (((1,), (1,)), ((), ())), preferred_element_type=jnp.float32
         ).astype(jnp.bfloat16)
-        dq, dk, dv = attention_bwd(q_in, ks, vs, do_part, ctx_in, lse, mask, first, count, 2)
-        k_own, k_cross = presum(dk)
-        v_own, v_cross = presum(dv)
+        dq, dk_keep, dk_send, dv_keep, dv_send = attention_bwd(
+            q_in, ks, vs, do_part, ctx_in, lse, mask, first, count, 2
+        )
+        k_own, k_cross = presum(dk_keep, dk_send)
+        v_own, v_cross = presum(dv_keep, dv_send)
         later, k_cross, v_cross = lax.optimization_barrier((later, k_cross, v_cross))
         pieces.append((dq, finish(k_own, k_cross), finish(v_own, v_cross)))
     grad_queries = jnp.concatenate([p[0] for p in pieces], axis=1)

time: 215 us -> 210 us (0.977)
  local copies, waits for them, and re-layouts: 6.97 us -> 4.34 us
    slice x4 -> x0, local copies, waits for them, and re-layouts: 3.28 us -> none  [presum(): back = swap(parts[2:4], 'core')]
  transfers between devices with their start and end apart: 15 -> 15, of which waited for: 6 -> 6; matrix products, arithmetic and copies ran while one was open for 13% -> 12% of each run, Pallas kernels for 14% -> 14%
where the time goes in v7:
time: 210 us; the launch traced here: 209 us
  waiting for transfers between devices  94.7 us (45%)
  Pallas kernels  42.7 us (20%)
  starting transfers between devices  20.9 us (10%)
  matrix products  20.7 us (10%)
  between operations  14.2 us (7%)
  other arithmetic  11 us (5%)
  local copies, waits for them, and re-layouts  4.34 us (2%)
    ppermute x14, waiting for transfers between devices, swap(): return lax.ppermute(x, axis, [(i, i ^ 1) for i in range(count)])  83 us
    pallas_call x2, Pallas kernels, attention_bwd(): pl.pallas_call(bwd_kernel, grid=(count // per_step,), cost_estimate=pl.Co...  25.1 us
    ppermute x14, starting transfers between devices, swap(): return lax.ppermute(x, axis, [(i, i ^ 1) for i in range(count)])  20.9 us
    pallas_call x1, Pallas kernels, attention_fwd(): pl.pallas_call(fwd_kernel, grid=(heads // per_step,), cost_estimate=pl.Co...  17.6 us
    dot_general x2, matrix products, per_device(): lax.dot_general(cotangent, w_rows, (((1,), (1,)), ((), ())), preferred_el...  11.4 us
    all_gather x1, waiting for transfers between devices, per_device(): lax.all_gather(weight_out, ('z', 'y', 'core'), axis=0, tiled=True)  11 us
    dot_general x1, matrix products, per_device(): jnp.dot(ctx_out, full_weight, preferred_element_type=jnp.float32)  9.37 us
  transfers between devices with their start and end apart: 15, of which 6 were waited for; matrix products, arithmetic and copies ran while one was open for 12% of the time, Pallas kernels for 14%

profile of v7, /device:TPU:1, one launch (start us, length us, event | category | flops | bytes accessed | tf_op | source)
XLA Modules:
  0.0 208.6 jit_solution(1541317343521761156)
XLA Ops:
  7.2 0.0 copy-start
  7.2 0.0 all-gather.2.cloned.1.call-start
  7.2 0.7 all-gather.2.cloned.1.call-update
  7.9 2.2 %collective-permute-start = (bf16[256,2560]{1,0:T(8,128)(2,1)}, bf16[256,2560]{1,0:T(8,128)(2,1)S(1)}, u32[]{:S(2)}, u32[]{:S(2)}) collective-permute-start(bf16[256,2560]{1,0:T(8,128)(2,1)} %k0.5), channel_id=1, source_target_pairs={{0,2},{2,0},{4,6},{6,4},{1,3},{3,1},{5,7},{7,5},{8,10},{10,8},{12,... | collective-permute-start | bytes 3932168 | tf_op jit(solution)/shard_map/ppermute | solution.py:127
  10.1 0.1 collective-permute-start.3
  10.2 3.0 %collective-permute-start.1 = (bf16[256,2560]{1,0:T(8,128)(2,1)}, bf16[256,2560]{1,0:T(8,128)(2,1)}, u32[]{:S(2)}, u32[]{:S(2)}) collective-permute-start(bf16[256,2560]{1,0:T(8,128)(2,1)} %k0.5), channel_id=1, source_target_pairs={{0,1},{1,0},{2,3},{3,2},{4,5},{5,4},{6,7},{7,6},{8,9},{9,8},{10,11... | collective-permute-start | bytes 3932168 | tf_op jit(solution)/shard_map/ppermute | solution.py:127
  13.2 0.0 collective-permute-start.4
  13.2 27.4 %collective-permute-done.k1 = bf16[256,2560]{1,0:T(8,128)(2,1)S(1)} collective-permute-done((bf16[256,2560]{1,0:T(8,128)(2,1)}, bf16[256,2560]{1,0:T(8,128)(2,1)S(1)}, u32[]{:S(2)}, u32[]{:S(2)}) %collective-permute-start) | collective-permute-done | bytes 1310752 | tf_op jit(solution)/shard_map/ppermute | solution.py:127
  40.7 5.7 %collective-permute-start.2 = (bf16[256,2560]{1,0:T(8,128)(2,1)S(1)}, bf16[256,2560]{1,0:T(8,128)(2,1)}, u32[]{:S(2)}, u32[]{:S(2)}) collective-permute-start(bf16[256,2560]{1,0:T(8,128)(2,1)S(1)} %collective-permute-done.k1), channel_id=1, source_target_pairs={{0,1},{1,0},{2,3},{3,2},{4,5},{5,4},{6,7},{7,6},{8,9},{9,8},{10,11... | collective-permute-start | bytes 3932168 | tf_op jit(solution)/shard_map/ppermute | solution.py:127
  46.4 26.6 %collective-permute-done.3.v1 = bf16[256,2560]{1,0:T(8,128)(2,1)} collective-permute-done((bf16[256,2560]{1,0:T(8,128)(2,1)}, bf16[256,2560]{1,0:T(8,128)(2,1)}, u32[]{:S(2)}, u32[]{:S(2)}) %collective-permute-start.3) | collective-permute-done | bytes 1310752 | tf_op jit(solution)/shard_map/ppermute | solution.py:127
  73.0 5.5 %collective-permute-start.5 = (bf16[256,2560]{1,0:T(8,128)(2,1)}, bf16[256,2560]{1,0:T(8,128)(2,1)}, u32[]{:S(2)}, u32[]{:S(2)}) collective-permute-start(bf16[256,2560]{1,0:T(8,128)(2,1)} %collective-permute-done.3.v1), channel_id=1, source_target_pairs={{0,1},{1,0},{2,3},{3,2},{4,5},{5,4},{6,7},{7,6},{8,9},{9,8},{10,11... | collective-permute-start | bytes 3932168 | tf_op jit(solution)/shard_map/ppermute | solution.py:127
  78.5 0.8 constant_dynamic-slice_fusion
  79.3 0.1 copy.12
  79.4 0.7 gather_fusion
  80.2 0.5 slice_reduce_fusion.5
  80.7 1.8 or_convert_fusion.mask_ref
  82.4 0.0 copy-done.11
  82.4 0.0 collective-permute-done.1.k2
  82.4 0.0 collective-permute-done.4.v2
  82.4 0.0 collective-permute-done.2.k3
  82.4 0.0 collective-permute-done.5.v3
  82.5 17.6 %shard_map.102 = (bf16[256,2560]{1,0:T(8,128)(2,1)}, f32[20,256,1]{2,1,0:T(8,128)}) custom-call(bf16[256,2560]{1,0:T(8,128)(2,1)} %q_ref.4, bf16[256,2560]{1,0:T(8,128)(2,1)} %k0.5, bf16[256,2560]{1,0:T(8,128)(2,1)} %copy-done.11, bf16[256,2560]{1,0:T(8,128)(2,1)} %collective-permute-done.1.k2, bf16[256,2560]{1,0:T(8,128)(2,1)} %collective-permute-done.2.k3, ...), custom_call_target="tpu_custom_call" | custom-call | flops 40000000000 | bytes 15728640 | tf_op jit(solution)/shard_map/pallas_call | solution.py:83
  100.1 11.0 %all-gather.2.cloned.1.call-done = bf16[2560,2560]{1,0:T(8,128)(2,1)} async-done(((bf16[40,2560]{1,0:T(8,128)(2,1)}), bf16[2560,2560]{1,0:T(8,128)(2,1)}) %all-gather.2.cloned.1.call-update) | async-done | bytes 13107216 | tf_op jit(solution)/shard_map/all_gather | solution.py:140
  111.1 0.0 copy-done
  111.1 5.6 %fusion.4.do_ref = bf16[256,1280]{1,0:T(8,128)(2,1)} fusion(bf16[256,2560]{1,0:T(8,128)(2,1)S(1)} %copy-done, bf16[2560,2560]{1,0:T(8,128)(2,1)} %all-gather.2.cloned.1.call-done), kind=kOutput, calls=%fused_computation.6 | convolution fusion | flops 1678049280 | bytes 8519680 | tf_op jit(solution)/shard_map/dot_general | solution.py:180
  116.8 12.7 %shard_map.103 = (bf16[256,1280]{1,0:T(8,128)(2,1)}, bf16[2,256,1280]{2,1,0:T(8,128)(2,1)}, bf16[2,256,1280]{2,1,0:T(8,128)(2,1)}, bf16[2,256,1280]{2,1,0:T(8,128)(2,1)}, bf16[2,256,1280]{2,1,0:T(8,128)(2,1)}) custom-call(bf16[256,2560]{1,0:T(8,128)(2,1)} %q_ref.4, bf16[256,2560]{1,0:T(8,128)(2,1)} %k0.5, bf16[256,2560]{1,0:T(8,128)(2,1)} %copy-done.11, ...), custom_call_target="tpu_custom_call" | custom-call | flops 14000000000 | bytes 7864320 | tf_op jit(solution)/shard_map/pallas_call | solution.py:106
  129.4 0.4 collective-permute-start.7
  129.8 0.3 collective-permute-start.6
  130.1 5.7 %fusion.7.do_ref = bf16[256,1280]{1,0:T(8,128)(2,1)} fusion(bf16[256,2560]{1,0:T(8,128)(2,1)S(1)} %copy-done, bf16[2560,2560]{1,0:T(8,128)(2,1)} %all-gather.2.cloned.1.call-done), kind=kOutput, calls=%fused_computation.7 | convolution fusion | flops 1678049280 | bytes 8519680 | tf_op jit(solution)/shard_map/dot_general | solution.py:180
  135.8 0.0 collective-permute-done.7
  135.8 1.0 fusion.15
  136.8 0.0 collective-permute-done.6
  136.8 1.1 copy-done.6
  137.9 0.0 copy-done.3
  137.9 1.0 fusion.14
  138.9 1.3 collective-permute-start.12
  140.2 12.5 %shard_map.104 = (bf16[256,1280]{1,0:T(8,128)(2,1)}, bf16[2,256,1280]{2,1,0:T(8,128)(2,1)}, bf16[2,256,1280]{2,1,0:T(8,128)(2,1)}, bf16[2,256,1280]{2,1,0:T(8,128)(2,1)}, bf16[2,256,1280]{2,1,0:T(8,128)(2,1)}) custom-call(bf16[256,2560]{1,0:T(8,128)(2,1)} %q_ref.4, bf16[256,2560]{1,0:T(8,128)(2,1)} %k0.5, bf16[256,2560]{1,0:T(8,128)(2,1)} %copy-done.11, ...), custom_call_target="tpu_custom_call" | custom-call | flops 14000000000 | bytes 7864320 | tf_op jit(solution)/shard_map/pallas_call | solution.py:106
  152.7 0.6 collective-permute-start.9
  153.3 0.1 collective-permute-start.8
  153.4 0.1 collective-permute-start.10
  153.5 0.0 copy-done.10
  153.6 2.4 %pad_maximum_fusion = bf16[256,2560]{1,0:T(8,128)(2,1)} fusion(bf16[256,1280]{1,0:T(8,128)(2,1)} %get-tuple-element.37, bf16[256,1280]{1,0:T(8,128)(2,1)S(1)} %copy-done.10), kind=kLoop, calls=%fused_computation.8 | loop fusion | flops 2621440 | bytes 2621440 | tf_op jit(solution)/shard_map/concatenate | solution.py:190
  155.9 0.0 collective-permute-done.12
  156.0 1.5 fusion.11
  157.4 12.1 %collective-permute-done.10 = bf16[256,1280]{1,0:T(8,128)(2,1)S(1)} collective-permute-done((bf16[256,1280]{1,0:T(8,128)(2,1)}, bf16[256,1280]{1,0:T(8,128)(2,1)S(1)}, u32[]{:S(2)}, u32[]{:S(2)}) %collective-permute-start.10) | collective-permute-done | bytes 655392 | tf_op jit(solution)/shard_map/ppermute | solution.py:127
  169.5 0.3 fusion.13
  169.8 0.0 copy-start.1
  169.8 0.0 collective-permute-done.9
  169.8 0.0 copy-done.2
  169.8 0.2 fusion.17
  170.0 0.0 copy-start.12
  170.0 0.0 collective-permute-done.8
  170.0 1.1 copy-done.1
  171.1 0.2 fusion.16
  171.3 1.1 collective-permute-start.13
  172.4 0.4 collective-permute-start.11
  172.8 0.0 copy-done.12
  172.8 9.4 %convolution_convert_fusion = bf16[256,2560]{1,0:T(8,128)(2,1)} fusion(bf16[256,2560]{1,0:T(8,128)(2,1)S(1)} %copy-done.12, bf16[2560,2560]{1,0:T(8,128)(2,1)} %all-gather.2.cloned.1.call-done), kind=kOutput, calls=%fused_computation.5 | convolution fusion | flops 3356098560 | bytes 15728640 | tf_op jit(solution)/shard_map/dot_general | solution.py:195
  182.2 4.2 %collective-permute-done.13 = bf16[256,1280]{1,0:T(8,128)(2,1)S(1)} collective-permute-done((bf16[256,1280]{1,0:T(8,128)(2,1)S(1)}, bf16[256,1280]{1,0:T(8,128)(2,1)S(1)}, u32[]{:S(2)}, u32[]{:S(2)}) %collective-permute-start.13) | collective-permute-done | bytes 655392 | tf_op jit(solution)/shard_map/ppermute | solution.py:127
  186.4 0.2 fusion.10
  186.6 1.1 pad_maximum_fusion.2
  187.8 12.7 %collective-permute-done.11 = bf16[256,1280]{1,0:T(8,128)(2,1)S(1)} collective-permute-done((bf16[256,1280]{1,0:T(8,128)(2,1)S(1)}, bf16[256,1280]{1,0:T(8,128)(2,1)S(1)}, u32[]{:S(2)}, u32[]{:S(2)}) %collective-permute-start.11) | collective-permute-done | bytes 655392 | tf_op jit(solution)/shard_map/ppermute | solution.py:127
  200.4 0.2 fusion.12
  200.7 1.1 pad_maximum_fusion.1
  (19 shorter events, 0.1 us)
Async XLA Ops:
  7.2 103.9 %copy-start = (bf16[256,2560]{1,0:T(8,128)(2,1)S(1)}, bf16[256,2560]{1,0:T(8,128)(2,1)}, u32[]{:S(2)}) copy-start(bf16[256,2560]{1,0:T(8,128)(2,1)} %param.11) | copy-start | bytes 3932164
  7.2 103.9 %all-gather.2.cloned.1.call-start = ((), (), s32[]{:S(2)}) async-start(), calls=%async_computation | async-start | bytes 13312000 | tf_op jit(solution)/shard_map/all_gather | solution.py:140
  7.9 32.7 %collective-permute-start = (bf16[256,2560]{1,0:T(8,128)(2,1)}, bf16[256,2560]{1,0:T(8,128)(2,1)S(1)}, u32[]{:S(2)}, u32[]{:S(2)}) collective-permute-start(bf16[256,2560]{1,0:T(8,128)(2,1)} %k0.5), channel_id=1, source_target_pairs={{0,2},{2,0},{4,6},{6,4},{1,3},{3,1},{5,7},{7,5},{8,10},{10,8},{12,... | collective-permute-start | bytes 3932168 | tf_op jit(solution)/shard_map/ppermute | solution.py:127
  10.1 62.9 %collective-permute-start.3 = (bf16[256,2560]{1,0:T(8,128)(2,1)}, bf16[256,2560]{1,0:T(8,128)(2,1)}, u32[]{:S(2)}, u32[]{:S(2)}) collective-permute-start(bf16[256,2560]{1,0:T(8,128)(2,1)} %v0.5), channel_id=1, source_target_pairs={{0,2},{2,0},{4,6},{6,4},{1,3},{3,1},{5,7},{7,5},{8,10},{10,8},{12,... | collective-permute-start | bytes 3932168 | tf_op jit(solution)/shard_map/ppermute | solution.py:127
  10.2 72.2 %collective-permute-start.1 = (bf16[256,2560]{1,0:T(8,128)(2,1)}, bf16[256,2560]{1,0:T(8,128)(2,1)}, u32[]{:S(2)}, u32[]{:S(2)}) collective-permute-start(bf16[256,2560]{1,0:T(8,128)(2,1)} %k0.5), channel_id=1, source_target_pairs={{0,1},{1,0},{2,3},{3,2},{4,5},{5,4},{6,7},{7,6},{8,9},{9,8},{10,11... | collective-permute-start | bytes 3932168 | tf_op jit(solution)/shard_map/ppermute | solution.py:127
  13.2 69.2 %collective-permute-start.4 = (bf16[256,2560]{1,0:T(8,128)(2,1)}, bf16[256,2560]{1,0:T(8,128)(2,1)}, u32[]{:S(2)}, u32[]{:S(2)}) collective-permute-start(bf16[256,2560]{1,0:T(8,128)(2,1)} %v0.5), channel_id=1, source_target_pairs={{0,1},{1,0},{2,3},{3,2},{4,5},{5,4},{6,7},{7,6},{8,9},{9,8},{10,11... | collective-permute-start | bytes 3932168 | tf_op jit(solution)/shard_map/ppermute | solution.py:127
  40.7 41.8 %copy-start.11 = (bf16[256,2560]{1,0:T(8,128)(2,1)}, bf16[256,2560]{1,0:T(8,128)(2,1)S(1)}, u32[]{:S(2)}) copy-start(bf16[256,2560]{1,0:T(8,128)(2,1)S(1)} %collective-permute-done.k1) | copy-start | bytes 3932164
  40.7 41.8 %collective-permute-start.2 = (bf16[256,2560]{1,0:T(8,128)(2,1)S(1)}, bf16[256,2560]{1,0:T(8,128)(2,1)}, u32[]{:S(2)}, u32[]{:S(2)}) collective-permute-start(bf16[256,2560]{1,0:T(8,128)(2,1)S(1)} %collective-permute-done.k1), channel_id=1, source_target_pairs={{0,1},{1,0},{2,3},{3,2},{4,5},{5,4},{6,7},{7,6},{8,9},{9,8},{10,11... | collective-permute-start | bytes 3932168 | tf_op jit(solution)/shard_map/ppermute | solution.py:127
  73.0 9.5 %collective-permute-start.5 = (bf16[256,2560]{1,0:T(8,128)(2,1)}, bf16[256,2560]{1,0:T(8,128)(2,1)}, u32[]{:S(2)}, u32[]{:S(2)}) collective-permute-start(bf16[256,2560]{1,0:T(8,128)(2,1)} %collective-permute-done.3.v1), channel_id=1, source_target_pairs={{0,1},{1,0},{2,3},{3,2},{4,5},{5,4},{6,7},{7,6},{8,9},{9,8},{10,11... | collective-permute-start | bytes 3932168 | tf_op jit(solution)/shard_map/ppermute | solution.py:127
  129.4 6.4 %collective-permute-start.7 = (bf16[2,256,1280]{2,1,0:T(8,128)(2,1)}, bf16[2,256,1280]{2,1,0:T(8,128)(2,1)S(1)}, u32[]{:S(2)}, u32[]{:S(2)}) collective-permute-start(bf16[2,256,1280]{2,1,0:T(8,128)(2,1)} %get-tuple-element.28), channel_id=1, source_target_pairs={{0,1},{1,0},{2,3},{3,2},{4,5},{5,4},{6,7},{7,6},{8,9},{9,8},{10,11... | collective-permute-start | bytes 3932168 | tf_op jit(solution)/shard_map/ppermute | solution.py:127
  129.8 6.0 %copy-start.4 = (bf16[2,256,1280]{2,1,0:T(8,128)(2,1)S(1)}, bf16[2,256,1280]{2,1,0:T(8,128)(2,1)}, u32[]{:S(2)}) copy-start(bf16[2,256,1280]{2,1,0:T(8,128)(2,1)} %get-tuple-element.27) | copy-start | bytes 3932164
  129.8 7.0 %collective-permute-start.6 = (bf16[2,256,1280]{2,1,0:T(8,128)(2,1)}, bf16[2,256,1280]{2,1,0:T(8,128)(2,1)S(1)}, u32[]{:S(2)}, u32[]{:S(2)}) collective-permute-start(bf16[2,256,1280]{2,1,0:T(8,128)(2,1)} %get-tuple-element.26), channel_id=1, source_target_pairs={{0,1},{1,0},{2,3},{3,2},{4,5},{5,4},{6,7},{7,6},{8,9},{9,8},{10,11... | collective-permute-start | bytes 3932168 | tf_op jit(solution)/shard_map/ppermute | solution.py:127
  135.8 2.1 %copy-start.3 = (bf16[2,256,1280]{2,1,0:T(8,128)(2,1)S(1)}, bf16[2,256,1280]{2,1,0:T(8,128)(2,1)}, u32[]{:S(2)}) copy-start(bf16[2,256,1280]{2,1,0:T(8,128)(2,1)} %get-tuple-element.25) | copy-start | bytes 3932164
  135.8 3.1 %copy-start.8 = (bf16[2,256,1280]{2,1,0:T(8,128)(2,1)}, bf16[2,256,1280]{2,1,0:T(8,128)(2,1)S(1)}, u32[]{:S(2)}) copy-start(bf16[2,256,1280]{2,1,0:T(8,128)(2,1)S(1)} %collective-permute-done.7) | copy-start | bytes 3932164
  136.8 1.1 copy-start.6
  138.9 14.6 %copy-start.10 = (bf16[256,1280]{1,0:T(8,128)(2,1)S(1)}, bf16[256,1280]{1,0:T(8,128)(2,1)}, u32[]{:S(2)}) copy-start(bf16[256,1280]{1,0:T(8,128)(2,1)} %get-tuple-element.36) | copy-start | bytes 1966084
  138.9 17.0 %collective-permute-start.12 = (bf16[256,1280]{1,0:T(8,128)(2,1)}, bf16[256,1280]{1,0:T(8,128)(2,1)}, u32[]{:S(2)}, u32[]{:S(2)}) collective-permute-start(bf16[256,1280]{1,0:T(8,128)(2,1)} %fusion.15), channel_id=1, source_target_pairs={{0,2},{2,0},{4,6},{6,4},{1,3},{3,1},{5,7},{7,5},{8,10},{10,8},{12,... | collective-permute-start | bytes 1966088 | tf_op jit(solution)/shard_map/ppermute | solution.py:127
  152.7 17.1 %collective-permute-start.9 = (bf16[2,256,1280]{2,1,0:T(8,128)(2,1)}, bf16[2,256,1280]{2,1,0:T(8,128)(2,1)S(1)}, u32[]{:S(2)}, u32[]{:S(2)}) collective-permute-start(bf16[2,256,1280]{2,1,0:T(8,128)(2,1)} %get-tuple-element.34), channel_id=1, source_target_pairs={{0,1},{1,0},{2,3},{3,2},{4,5},{5,4},{6,7},{7,6},{8,9},{9,8},{10,11... | collective-permute-start | bytes 3932168 | tf_op jit(solution)/shard_map/ppermute | solution.py:127
  153.3 16.7 %collective-permute-start.8 = (bf16[2,256,1280]{2,1,0:T(8,128)(2,1)}, bf16[2,256,1280]{2,1,0:T(8,128)(2,1)S(1)}, u32[]{:S(2)}, u32[]{:S(2)}) collective-permute-start(bf16[2,256,1280]{2,1,0:T(8,128)(2,1)} %get-tuple-element.32), channel_id=1, source_target_pairs={{0,1},{1,0},{2,3},{3,2},{4,5},{5,4},{6,7},{7,6},{8,9},{9,8},{10,11... | collective-permute-start | bytes 3932168 | tf_op jit(solution)/shard_map/ppermute | solution.py:127
  153.4 16.1 %collective-permute-start.10 = (bf16[256,1280]{1,0:T(8,128)(2,1)}, bf16[256,1280]{1,0:T(8,128)(2,1)S(1)}, u32[]{:S(2)}, u32[]{:S(2)}) collective-permute-start(bf16[256,1280]{1,0:T(8,128)(2,1)} %fusion.14), channel_id=1, source_target_pairs={{0,2},{2,0},{4,6},{6,4},{1,3},{3,1},{5,7},{7,5},{8,10},{10,8},{12,... | collective-permute-start | bytes 1966088 | tf_op jit(solution)/shard_map/ppermute | solution.py:127
  153.5 2.4 %copy-start.5 = (bf16[2,256,1280]{2,1,0:T(8,128)(2,1)S(1)}, bf16[2,256,1280]{2,1,0:T(8,128)(2,1)}, u32[]{:S(2)}) copy-start(bf16[2,256,1280]{2,1,0:T(8,128)(2,1)} %get-tuple-element.27) | copy-start | bytes 3932164
  153.5 2.4 %copy-start.9 = (bf16[2,256,1280]{2,1,0:T(8,128)(2,1)S(1)}, bf16[2,256,1280]{2,1,0:T(8,128)(2,1)}, u32[]{:S(2)}) copy-start(bf16[2,256,1280]{2,1,0:T(8,128)(2,1)} %copy-done.8) | copy-start | bytes 3932164
  155.9 13.6 %copy-start.7 = (bf16[2,256,1280]{2,1,0:T(8,128)(2,1)S(1)}, bf16[2,256,1280]{2,1,0:T(8,128)(2,1)}, u32[]{:S(2)}) copy-start(bf16[2,256,1280]{2,1,0:T(8,128)(2,1)} %copy-done.6) | copy-start | bytes 3932164
  157.4 12.4 %copy-start.2 = (bf16[2,256,1280]{2,1,0:T(8,128)(2,1)S(1)}, bf16[2,256,1280]{2,1,0:T(8,128)(2,1)}, u32[]{:S(2)}) copy-start(bf16[2,256,1280]{2,1,0:T(8,128)(2,1)} %get-tuple-element.33) | copy-start | bytes 3932164
  169.8 1.3 copy-start.1
  170.0 2.8 %copy-start.12 = (bf16[256,2560]{1,0:T(8,128)(2,1)S(1)}, bf16[256,2560]{1,0:T(8,128)(2,1)}, u32[]{:S(2)}) copy-start(bf16[256,2560]{1,0:T(8,128)(2,1)} %get-tuple-element.35.ctx_ref) | copy-start | bytes 3932164
  171.3 15.1 %collective-permute-start.13 = (bf16[256,1280]{1,0:T(8,128)(2,1)S(1)}, bf16[256,1280]{1,0:T(8,128)(2,1)S(1)}, u32[]{:S(2)}, u32[]{:S(2)}) collective-permute-start(bf16[256,1280]{1,0:T(8,128)(2,1)S(1)} %fusion.17), channel_id=1, source_target_pairs={{0,2},{2,0},{4,6},{6,4},{1,3},{3,1},{5,7},{7,5},{8,10},{10,8},{12,... | collective-permute-start | bytes 1966088 | tf_op jit(solution)/shard_map/ppermute | solution.py:127
  172.4 28.0 %collective-permute-start.11 = (bf16[256,1280]{1,0:T(8,128)(2,1)S(1)}, bf16[256,1280]{1,0:T(8,128)(2,1)S(1)}, u32[]{:S(2)}, u32[]{:S(2)}) collective-permute-start(bf16[256,1280]{1,0:T(8,128)(2,1)S(1)} %fusion.16), channel_id=1, source_target_pairs={{0,2},{2,0},{4,6},{6,4},{1,3},{3,1},{5,7},{7,5},{8,10},{10,8},{12,... | collective-permute-start | bytes 1966088 | tf_op jit(solution)/shard_map/ppermute | solution.py:127
Sparse Core Ops, SparseCore 0:
  10.7 100.3 all-gather.1

commit v8 on v7

--- a/solution.py
+++ b/solution.py
@@ -181,7 +181,7 @@
             cotangent, w_rows, (((1,), (1,)), ((), ())), preferred_element_type=jnp.float32
         ).astype(jnp.bfloat16)
         dq, dk_keep, dk_send, dv_keep, dv_send = attention_bwd(
-            q_in, ks, vs, do_part, ctx_in, lse, mask, first, count, 2
+            q_in, ks, vs, do_part, ctx_in, lse, mask, first, count, 5
         )
         k_own, k_cross = presum(dk_keep, dk_send)
         v_own, v_cross = presum(dv_keep, dv_send)

time: 210 us -> 211 us (level)
  transfers between devices with their start and end apart: 15 -> 15, of which waited for: 6 -> 6; matrix products, arithmetic and copies ran while one was open for 12% -> 12% of each run, Pallas kernels for 14% -> 15%
where the time goes in v8:
time: 211 us; the launch traced here: 210 us
  waiting for transfers between devices  94.7 us (45%)
  Pallas kernels  44 us (21%)
  starting transfers between devices  21 us (10%)
  matrix products  20.7 us (10%)
  between operations  14.2 us (7%)
  other arithmetic  11 us (5%)
  local copies, waits for them, and re-layouts  4.34 us (2%)
    ppermute x14, waiting for transfers between devices, swap(): return lax.ppermute(x, axis, [(i, i ^ 1) for i in range(count)])  83 us
    pallas_call x2, Pallas kernels, attention_bwd(): pl.pallas_call(bwd_kernel, grid=(count // per_step,), cost_estimate=pl.Co...  26.3 us
    ppermute x14, starting transfers between devices, swap(): return lax.ppermute(x, axis, [(i, i ^ 1) for i in range(count)])  20.9 us
    pallas_call x1, Pallas kernels, attention_fwd(): pl.pallas_call(fwd_kernel, grid=(heads // per_step,), cost_estimate=pl.Co...  17.6 us
    dot_general x2, matrix products, per_device(): lax.dot_general(cotangent, w_rows, (((1,), (1,)), ((), ())), preferred_el...  11.3 us
    all_gather x1, waiting for transfers between devices, per_device(): lax.all_gather(weight_out, ('z', 'y', 'core'), axis=0, tiled=True)  11 us
    dot_general x1, matrix products, per_device(): jnp.dot(ctx_out, full_weight, preferred_element_type=jnp.float32)  9.37 us
  transfers between devices with their start and end apart: 15, of which 6 were waited for; matrix products, arithmetic and copies ran while one was open for 12% of the time, Pallas kernels for 15%

profile of v8, /device:TPU:1, one launch (start us, length us, event | category | flops | bytes accessed | tf_op | source)
XLA Modules:
  0.0 209.8 jit_solution(9616564132496417575)
XLA Ops:
  7.2 0.0 copy-start
  7.2 0.0 all-gather.2.cloned.1.call-start
  7.2 0.7 all-gather.2.cloned.1.call-update
  7.9 2.2 %collective-permute-start = (bf16[256,2560]{1,0:T(8,128)(2,1)}, bf16[256,2560]{1,0:T(8,128)(2,1)S(1)}, u32[]{:S(2)}, u32[]{:S(2)}) collective-permute-start(bf16[256,2560]{1,0:T(8,128)(2,1)} %k0.5), channel_id=1, source_target_pairs={{0,2},{2,0},{4,6},{6,4},{1,3},{3,1},{5,7},{7,5},{8,10},{10,8},{12,... | collective-permute-start | bytes 3932168 | tf_op jit(solution)/shard_map/ppermute | solution.py:127
  10.1 0.1 collective-permute-start.3
  10.2 3.0 %collective-permute-start.1 = (bf16[256,2560]{1,0:T(8,128)(2,1)}, bf16[256,2560]{1,0:T(8,128)(2,1)}, u32[]{:S(2)}, u32[]{:S(2)}) collective-permute-start(bf16[256,2560]{1,0:T(8,128)(2,1)} %k0.5), channel_id=1, source_target_pairs={{0,1},{1,0},{2,3},{3,2},{4,5},{5,4},{6,7},{7,6},{8,9},{9,8},{10,11... | collective-permute-start | bytes 3932168 | tf_op jit(solution)/shard_map/ppermute | solution.py:127
  13.2 0.0 collective-permute-start.4
  13.2 27.4 %collective-permute-done.k1 = bf16[256,2560]{1,0:T(8,128)(2,1)S(1)} collective-permute-done((bf16[256,2560]{1,0:T(8,128)(2,1)}, bf16[256,2560]{1,0:T(8,128)(2,1)S(1)}, u32[]{:S(2)}, u32[]{:S(2)}) %collective-permute-start) | collective-permute-done | bytes 1310752 | tf_op jit(solution)/shard_map/ppermute | solution.py:127
  40.7 5.7 %collective-permute-start.2 = (bf16[256,2560]{1,0:T(8,128)(2,1)S(1)}, bf16[256,2560]{1,0:T(8,128)(2,1)}, u32[]{:S(2)}, u32[]{:S(2)}) collective-permute-start(bf16[256,2560]{1,0:T(8,128)(2,1)S(1)} %collective-permute-done.k1), channel_id=1, source_target_pairs={{0,1},{1,0},{2,3},{3,2},{4,5},{5,4},{6,7},{7,6},{8,9},{9,8},{10,11... | collective-permute-start | bytes 3932168 | tf_op jit(solution)/shard_map/ppermute | solution.py:127
  46.4 26.6 %collective-permute-done.3.v1 = bf16[256,2560]{1,0:T(8,128)(2,1)} collective-permute-done((bf16[256,2560]{1,0:T(8,128)(2,1)}, bf16[256,2560]{1,0:T(8,128)(2,1)}, u32[]{:S(2)}, u32[]{:S(2)}) %collective-permute-start.3) | collective-permute-done | bytes 1310752 | tf_op jit(solution)/shard_map/ppermute | solution.py:127
  73.0 5.5 %collective-permute-start.5 = (bf16[256,2560]{1,0:T(8,128)(2,1)}, bf16[256,2560]{1,0:T(8,128)(2,1)}, u32[]{:S(2)}, u32[]{:S(2)}) collective-permute-start(bf16[256,2560]{1,0:T(8,128)(2,1)} %collective-permute-done.3.v1), channel_id=1, source_target_pairs={{0,1},{1,0},{2,3},{3,2},{4,5},{5,4},{6,7},{7,6},{8,9},{9,8},{10,11... | collective-permute-start | bytes 3932168 | tf_op jit(solution)/shard_map/ppermute | solution.py:127
  78.5 0.8 constant_dynamic-slice_fusion
  79.3 0.1 copy.12
  79.4 0.7 gather_fusion
  80.2 0.5 slice_reduce_fusion.5
  80.7 1.8 or_convert_fusion.mask_ref
  82.4 0.0 copy-done.11
  82.4 0.0 collective-permute-done.1.k2
  82.4 0.0 collective-permute-done.4.v2
  82.4 0.0 collective-permute-done.2.k3
  82.4 0.0 collective-permute-done.5.v3
  82.5 17.6 %shard_map.102 = (bf16[256,2560]{1,0:T(8,128)(2,1)}, f32[20,256,1]{2,1,0:T(8,128)}) custom-call(bf16[256,2560]{1,0:T(8,128)(2,1)} %q_ref.4, bf16[256,2560]{1,0:T(8,128)(2,1)} %k0.5, bf16[256,2560]{1,0:T(8,128)(2,1)} %copy-done.11, bf16[256,2560]{1,0:T(8,128)(2,1)} %collective-permute-done.1.k2, bf16[256,2560]{1,0:T(8,128)(2,1)} %collective-permute-done.2.k3, ...), custom_call_target="tpu_custom_call" | custom-call | flops 40000000000 | bytes 15728640 | tf_op jit(solution)/shard_map/pallas_call | solution.py:83
  100.1 11.0 %all-gather.2.cloned.1.call-done = bf16[2560,2560]{1,0:T(8,128)(2,1)} async-done(((bf16[40,2560]{1,0:T(8,128)(2,1)}), bf16[2560,2560]{1,0:T(8,128)(2,1)}) %all-gather.2.cloned.1.call-update) | async-done | bytes 13107216 | tf_op jit(solution)/shard_map/all_gather | solution.py:140
  111.1 0.0 copy-done
  111.1 5.6 %fusion.4.do_ref = bf16[256,1280]{1,0:T(8,128)(2,1)} fusion(bf16[256,2560]{1,0:T(8,128)(2,1)S(1)} %copy-done, bf16[2560,2560]{1,0:T(8,128)(2,1)} %all-gather.2.cloned.1.call-done), kind=kOutput, calls=%fused_computation.6 | convolution fusion | flops 1678049280 | bytes 8519680 | tf_op jit(solution)/shard_map/dot_general | solution.py:180
  116.8 13.4 %shard_map.103 = (bf16[256,1280]{1,0:T(8,128)(2,1)}, bf16[2,256,1280]{2,1,0:T(8,128)(2,1)}, bf16[2,256,1280]{2,1,0:T(8,128)(2,1)}, bf16[2,256,1280]{2,1,0:T(8,128)(2,1)}, bf16[2,256,1280]{2,1,0:T(8,128)(2,1)}) custom-call(bf16[256,2560]{1,0:T(8,128)(2,1)} %q_ref.4, bf16[256,2560]{1,0:T(8,128)(2,1)} %k0.5, bf16[256,2560]{1,0:T(8,128)(2,1)} %copy-done.11, ...), custom_call_target="tpu_custom_call" | custom-call | flops 14000000000 | bytes 7864320 | tf_op jit(solution)/shard_map/pallas_call | solution.py:106
  130.1 0.3 collective-permute-start.7
  130.5 0.3 collective-permute-start.6
  130.8 5.7 %fusion.7.do_ref = bf16[256,1280]{1,0:T(8,128)(2,1)} fusion(bf16[256,2560]{1,0:T(8,128)(2,1)S(1)} %copy-done, bf16[2560,2560]{1,0:T(8,128)(2,1)} %all-gather.2.cloned.1.call-done), kind=kOutput, calls=%fused_computation.7 | convolution fusion | flops 1678049280 | bytes 8519680 | tf_op jit(solution)/shard_map/dot_general | solution.py:180
  136.5 0.0 collective-permute-done.7
  136.5 0.0 copy-done.4
  136.5 1.0 fusion.15
  137.5 0.0 collective-permute-done.6
  137.5 1.1 copy-done.6
  138.6 0.0 copy-done.3
  138.6 1.0 fusion.14
  139.6 1.3 collective-permute-start.12
  140.9 12.9 %shard_map.104 = (bf16[256,1280]{1,0:T(8,128)(2,1)}, bf16[2,256,1280]{2,1,0:T(8,128)(2,1)}, bf16[2,256,1280]{2,1,0:T(8,128)(2,1)}, bf16[2,256,1280]{2,1,0:T(8,128)(2,1)}, bf16[2,256,1280]{2,1,0:T(8,128)(2,1)}) custom-call(bf16[256,2560]{1,0:T(8,128)(2,1)} %q_ref.4, bf16[256,2560]{1,0:T(8,128)(2,1)} %k0.5, bf16[256,2560]{1,0:T(8,128)(2,1)} %copy-done.11, ...), custom_call_target="tpu_custom_call" | custom-call | flops 14000000000 | bytes 7864320 | tf_op jit(solution)/shard_map/pallas_call | solution.py:106
  153.9 0.6 collective-permute-start.9
  154.5 0.1 collective-permute-start.8
  154.6 0.2 collective-permute-start.10
  154.8 0.0 copy-done.10
  154.8 2.4 %pad_maximum_fusion = bf16[256,2560]{1,0:T(8,128)(2,1)} fusion(bf16[256,1280]{1,0:T(8,128)(2,1)} %get-tuple-element.37, bf16[256,1280]{1,0:T(8,128)(2,1)S(1)} %copy-done.10), kind=kLoop, calls=%fused_computation.8 | loop fusion | flops 2621440 | bytes 2621440 | tf_op jit(solution)/shard_map/concatenate | solution.py:190
  157.1 0.0 collective-permute-done.12
  157.2 1.5 fusion.11
  158.6 12.0 %collective-permute-done.10 = bf16[256,1280]{1,0:T(8,128)(2,1)S(1)} collective-permute-done((bf16[256,1280]{1,0:T(8,128)(2,1)}, bf16[256,1280]{1,0:T(8,128)(2,1)S(1)}, u32[]{:S(2)}, u32[]{:S(2)}) %collective-permute-start.10) | collective-permute-done | bytes 655392 | tf_op jit(solution)/shard_map/ppermute | solution.py:127
  170.7 0.3 fusion.13
  171.0 0.0 copy-start.1
  171.0 0.0 collective-permute-done.9
  171.0 0.0 copy-done.2
  171.0 0.2 fusion.17
  171.2 0.0 copy-start.12
  171.2 0.0 collective-permute-done.8
  171.2 1.1 copy-done.1
  172.3 0.2 fusion.16
  172.4 0.7 collective-permute-start.13
  173.2 0.8 collective-permute-start.11
  174.0 9.4 %convolution_convert_fusion = bf16[256,2560]{1,0:T(8,128)(2,1)} fusion(bf16[256,2560]{1,0:T(8,128)(2,1)S(1)} %copy-done.12, bf16[2560,2560]{1,0:T(8,128)(2,1)} %all-gather.2.cloned.1.call-done), kind=kOutput, calls=%fused_computation.5 | convolution fusion | flops 3356098560 | bytes 15728640 | tf_op jit(solution)/shard_map/dot_general | solution.py:195
  183.4 4.2 %collective-permute-done.13 = bf16[256,1280]{1,0:T(8,128)(2,1)S(1)} collective-permute-done((bf16[256,1280]{1,0:T(8,128)(2,1)S(1)}, bf16[256,1280]{1,0:T(8,128)(2,1)S(1)}, u32[]{:S(2)}, u32[]{:S(2)}) %collective-permute-start.13) | collective-permute-done | bytes 655392 | tf_op jit(solution)/shard_map/ppermute | solution.py:127
  187.6 0.2 fusion.10
  187.8 1.1 pad_maximum_fusion.2
  188.9 12.7 %collective-permute-done.11 = bf16[256,1280]{1,0:T(8,128)(2,1)S(1)} collective-permute-done((bf16[256,1280]{1,0:T(8,128)(2,1)S(1)}, bf16[256,1280]{1,0:T(8,128)(2,1)S(1)}, u32[]{:S(2)}, u32[]{:S(2)}) %collective-permute-start.11) | collective-permute-done | bytes 655392 | tf_op jit(solution)/shard_map/ppermute | solution.py:127
  201.6 0.2 fusion.12
  201.8 1.1 pad_maximum_fusion.1
  (19 shorter events, 0.1 us)
Async XLA Ops:
  7.2 103.9 %copy-start = (bf16[256,2560]{1,0:T(8,128)(2,1)S(1)}, bf16[256,2560]{1,0:T(8,128)(2,1)}, u32[]{:S(2)}) copy-start(bf16[256,2560]{1,0:T(8,128)(2,1)} %param.11) | copy-start | bytes 3932164
  7.2 103.9 %all-gather.2.cloned.1.call-start = ((), (), s32[]{:S(2)}) async-start(), calls=%async_computation | async-start | bytes 13312000 | tf_op jit(solution)/shard_map/all_gather | solution.py:140
  7.9 32.7 %collective-permute-start = (bf16[256,2560]{1,0:T(8,128)(2,1)}, bf16[256,2560]{1,0:T(8,128)(2,1)S(1)}, u32[]{:S(2)}, u32[]{:S(2)}) collective-permute-start(bf16[256,2560]{1,0:T(8,128)(2,1)} %k0.5), channel_id=1, source_target_pairs={{0,2},{2,0},{4,6},{6,4},{1,3},{3,1},{5,7},{7,5},{8,10},{10,8},{12,... | collective-permute-start | bytes 3932168 | tf_op jit(solution)/shard_map/ppermute | solution.py:127
  10.1 62.9 %collective-permute-start.3 = (bf16[256,2560]{1,0:T(8,128)(2,1)}, bf16[256,2560]{1,0:T(8,128)(2,1)}, u32[]{:S(2)}, u32[]{:S(2)}) collective-permute-start(bf16[256,2560]{1,0:T(8,128)(2,1)} %v0.5), channel_id=1, source_target_pairs={{0,2},{2,0},{4,6},{6,4},{1,3},{3,1},{5,7},{7,5},{8,10},{10,8},{12,... | collective-permute-start | bytes 3932168 | tf_op jit(solution)/shard_map/ppermute | solution.py:127
  10.2 72.2 %collective-permute-start.1 = (bf16[256,2560]{1,0:T(8,128)(2,1)}, bf16[256,2560]{1,0:T(8,128)(2,1)}, u32[]{:S(2)}, u32[]{:S(2)}) collective-permute-start(bf16[256,2560]{1,0:T(8,128)(2,1)} %k0.5), channel_id=1, source_target_pairs={{0,1},{1,0},{2,3},{3,2},{4,5},{5,4},{6,7},{7,6},{8,9},{9,8},{10,11... | collective-permute-start | bytes 3932168 | tf_op jit(solution)/shard_map/ppermute | solution.py:127
  13.2 69.2 %collective-permute-start.4 = (bf16[256,2560]{1,0:T(8,128)(2,1)}, bf16[256,2560]{1,0:T(8,128)(2,1)}, u32[]{:S(2)}, u32[]{:S(2)}) collective-permute-start(bf16[256,2560]{1,0:T(8,128)(2,1)} %v0.5), channel_id=1, source_target_pairs={{0,1},{1,0},{2,3},{3,2},{4,5},{5,4},{6,7},{7,6},{8,9},{9,8},{10,11... | collective-permute-start | bytes 3932168 | tf_op jit(solution)/shard_map/ppermute | solution.py:127
  40.7 41.8 %copy-start.11 = (bf16[256,2560]{1,0:T(8,128)(2,1)}, bf16[256,2560]{1,0:T(8,128)(2,1)S(1)}, u32[]{:S(2)}) copy-start(bf16[256,2560]{1,0:T(8,128)(2,1)S(1)} %collective-permute-done.k1) | copy-start | bytes 3932164
  40.7 41.8 %collective-permute-start.2 = (bf16[256,2560]{1,0:T(8,128)(2,1)S(1)}, bf16[256,2560]{1,0:T(8,128)(2,1)}, u32[]{:S(2)}, u32[]{:S(2)}) collective-permute-start(bf16[256,2560]{1,0:T(8,128)(2,1)S(1)} %collective-permute-done.k1), channel_id=1, source_target_pairs={{0,1},{1,0},{2,3},{3,2},{4,5},{5,4},{6,7},{7,6},{8,9},{9,8},{10,11... | collective-permute-start | bytes 3932168 | tf_op jit(solution)/shard_map/ppermute | solution.py:127
  73.0 9.5 %collective-permute-start.5 = (bf16[256,2560]{1,0:T(8,128)(2,1)}, bf16[256,2560]{1,0:T(8,128)(2,1)}, u32[]{:S(2)}, u32[]{:S(2)}) collective-permute-start(bf16[256,2560]{1,0:T(8,128)(2,1)} %collective-permute-done.3.v1), channel_id=1, source_target_pairs={{0,1},{1,0},{2,3},{3,2},{4,5},{5,4},{6,7},{7,6},{8,9},{9,8},{10,11... | collective-permute-start | bytes 3932168 | tf_op jit(solution)/shard_map/ppermute | solution.py:127
  130.1 6.3 %collective-permute-start.7 = (bf16[2,256,1280]{2,1,0:T(8,128)(2,1)}, bf16[2,256,1280]{2,1,0:T(8,128)(2,1)S(1)}, u32[]{:S(2)}, u32[]{:S(2)}) collective-permute-start(bf16[2,256,1280]{2,1,0:T(8,128)(2,1)} %get-tuple-element.28), channel_id=1, source_target_pairs={{0,1},{1,0},{2,3},{3,2},{4,5},{5,4},{6,7},{7,6},{8,9},{9,8},{10,11... | collective-permute-start | bytes 3932168 | tf_op jit(solution)/shard_map/ppermute | solution.py:127
  130.5 6.0 %copy-start.4 = (bf16[2,256,1280]{2,1,0:T(8,128)(2,1)S(1)}, bf16[2,256,1280]{2,1,0:T(8,128)(2,1)}, u32[]{:S(2)}) copy-start(bf16[2,256,1280]{2,1,0:T(8,128)(2,1)} %get-tuple-element.27) | copy-start | bytes 3932164
  130.5 7.0 %collective-permute-start.6 = (bf16[2,256,1280]{2,1,0:T(8,128)(2,1)}, bf16[2,256,1280]{2,1,0:T(8,128)(2,1)S(1)}, u32[]{:S(2)}, u32[]{:S(2)}) collective-permute-start(bf16[2,256,1280]{2,1,0:T(8,128)(2,1)} %get-tuple-element.26), channel_id=1, source_target_pairs={{0,1},{1,0},{2,3},{3,2},{4,5},{5,4},{6,7},{7,6},{8,9},{9,8},{10,11... | collective-permute-start | bytes 3932168 | tf_op jit(solution)/shard_map/ppermute | solution.py:127
  136.5 2.1 %copy-start.3 = (bf16[2,256,1280]{2,1,0:T(8,128)(2,1)S(1)}, bf16[2,256,1280]{2,1,0:T(8,128)(2,1)}, u32[]{:S(2)}) copy-start(bf16[2,256,1280]{2,1,0:T(8,128)(2,1)} %get-tuple-element.25) | copy-start | bytes 3932164
  136.5 3.1 %copy-start.8 = (bf16[2,256,1280]{2,1,0:T(8,128)(2,1)}, bf16[2,256,1280]{2,1,0:T(8,128)(2,1)S(1)}, u32[]{:S(2)}) copy-start(bf16[2,256,1280]{2,1,0:T(8,128)(2,1)S(1)} %collective-permute-done.7) | copy-start | bytes 3932164
  137.5 1.1 copy-start.6
  139.6 15.1 %copy-start.10 = (bf16[256,1280]{1,0:T(8,128)(2,1)S(1)}, bf16[256,1280]{1,0:T(8,128)(2,1)}, u32[]{:S(2)}) copy-start(bf16[256,1280]{1,0:T(8,128)(2,1)} %get-tuple-element.36) | copy-start | bytes 1966084
  139.6 17.5 %collective-permute-start.12 = (bf16[256,1280]{1,0:T(8,128)(2,1)}, bf16[256,1280]{1,0:T(8,128)(2,1)}, u32[]{:S(2)}, u32[]{:S(2)}) collective-permute-start(bf16[256,1280]{1,0:T(8,128)(2,1)} %fusion.15), channel_id=1, source_target_pairs={{0,2},{2,0},{4,6},{6,4},{1,3},{3,1},{5,7},{7,5},{8,10},{10,8},{12,... | collective-permute-start | bytes 1966088 | tf_op jit(solution)/shard_map/ppermute | solution.py:127
  153.9 17.1 %collective-permute-start.9 = (bf16[2,256,1280]{2,1,0:T(8,128)(2,1)}, bf16[2,256,1280]{2,1,0:T(8,128)(2,1)S(1)}, u32[]{:S(2)}, u32[]{:S(2)}) collective-permute-start(bf16[2,256,1280]{2,1,0:T(8,128)(2,1)} %get-tuple-element.34), channel_id=1, source_target_pairs={{0,1},{1,0},{2,3},{3,2},{4,5},{5,4},{6,7},{7,6},{8,9},{9,8},{10,11... | collective-permute-start | bytes 3932168 | tf_op jit(solution)/shard_map/ppermute | solution.py:127
  154.5 16.7 %collective-permute-start.8 = (bf16[2,256,1280]{2,1,0:T(8,128)(2,1)}, bf16[2,256,1280]{2,1,0:T(8,128)(2,1)S(1)}, u32[]{:S(2)}, u32[]{:S(2)}) collective-permute-start(bf16[2,256,1280]{2,1,0:T(8,128)(2,1)} %get-tuple-element.32), channel_id=1, source_target_pairs={{0,1},{1,0},{2,3},{3,2},{4,5},{5,4},{6,7},{7,6},{8,9},{9,8},{10,11... | collective-permute-start | bytes 3932168 | tf_op jit(solution)/shard_map/ppermute | solution.py:127
  154.6 16.1 %collective-permute-start.10 = (bf16[256,1280]{1,0:T(8,128)(2,1)}, bf16[256,1280]{1,0:T(8,128)(2,1)S(1)}, u32[]{:S(2)}, u32[]{:S(2)}) collective-permute-start(bf16[256,1280]{1,0:T(8,128)(2,1)} %fusion.14), channel_id=1, source_target_pairs={{0,2},{2,0},{4,6},{6,4},{1,3},{3,1},{5,7},{7,5},{8,10},{10,8},{12,... | collective-permute-start | bytes 1966088 | tf_op jit(solution)/shard_map/ppermute | solution.py:127
  154.8 2.4 %copy-start.5 = (bf16[2,256,1280]{2,1,0:T(8,128)(2,1)S(1)}, bf16[2,256,1280]{2,1,0:T(8,128)(2,1)}, u32[]{:S(2)}) copy-start(bf16[2,256,1280]{2,1,0:T(8,128)(2,1)} %get-tuple-element.27) | copy-start | bytes 3932164
  154.8 2.4 %copy-start.9 = (bf16[2,256,1280]{2,1,0:T(8,128)(2,1)S(1)}, bf16[2,256,1280]{2,1,0:T(8,128)(2,1)}, u32[]{:S(2)}) copy-start(bf16[2,256,1280]{2,1,0:T(8,128)(2,1)} %copy-done.8) | copy-start | bytes 3932164
  157.1 13.5 %copy-start.7 = (bf16[2,256,1280]{2,1,0:T(8,128)(2,1)S(1)}, bf16[2,256,1280]{2,1,0:T(8,128)(2,1)}, u32[]{:S(2)}) copy-start(bf16[2,256,1280]{2,1,0:T(8,128)(2,1)} %copy-done.6) | copy-start | bytes 3932164
  158.6 12.4 %copy-start.2 = (bf16[2,256,1280]{2,1,0:T(8,128)(2,1)S(1)}, bf16[2,256,1280]{2,1,0:T(8,128)(2,1)}, u32[]{:S(2)}) copy-start(bf16[2,256,1280]{2,1,0:T(8,128)(2,1)} %get-tuple-element.33) | copy-start | bytes 3932164
  171.0 1.3 copy-start.1
  171.2 2.8 %copy-start.12 = (bf16[256,2560]{1,0:T(8,128)(2,1)S(1)}, bf16[256,2560]{1,0:T(8,128)(2,1)}, u32[]{:S(2)}) copy-start(bf16[256,2560]{1,0:T(8,128)(2,1)} %get-tuple-element.35.ctx_ref) | copy-start | bytes 3932164
  172.4 15.1 %collective-permute-start.13 = (bf16[256,1280]{1,0:T(8,128)(2,1)S(1)}, bf16[256,1280]{1,0:T(8,128)(2,1)S(1)}, u32[]{:S(2)}, u32[]{:S(2)}) collective-permute-start(bf16[256,1280]{1,0:T(8,128)(2,1)S(1)} %fusion.17), channel_id=1, source_target_pairs={{0,2},{2,0},{4,6},{6,4},{1,3},{3,1},{5,7},{7,5},{8,10},{10,8},{12,... | collective-permute-start | bytes 1966088 | tf_op jit(solution)/shard_map/ppermute | solution.py:127
  173.2 28.4 %collective-permute-start.11 = (bf16[256,1280]{1,0:T(8,128)(2,1)S(1)}, bf16[256,1280]{1,0:T(8,128)(2,1)S(1)}, u32[]{:S(2)}, u32[]{:S(2)}) collective-permute-start(bf16[256,1280]{1,0:T(8,128)(2,1)S(1)} %fusion.16), channel_id=1, source_target_pairs={{0,2},{2,0},{4,6},{6,4},{1,3},{3,1},{5,7},{7,5},{8,10},{10,8},{12,... | collective-permute-start | bytes 1966088 | tf_op jit(solution)/shard_map/ppermute | solution.py:127
Sparse Core Ops, SparseCore 0:
  10.7 100.3 all-gather.1
